TPU v7x, 256 devices: a whole 4x4x8 slice. The times are simulated.
256 devices in a mesh: tile: 16 (over y, x), query: 2 (over core), dp: 8 (over z).
Axes of the slice: x: 4, y: 4, z: 8, core: 2. Of those that a mesh axis runs over, the one named last changes fastest.
Arguments:
- features: bfloat16 [8, 131072, 256], P('dp', ('tile', 'query')), may hold values from -6 to 6
- queries: bfloat16 [8, 256, 256], P('dp', ('tile', 'query')), may hold values from -6 to 6
- out_grad: bfloat16 [8, 256, 256], P('dp', ('tile', 'query')), may hold values from -48 to 48
- value_weight: bfloat16 [256, 256], replicated, may hold values from -0.375 to 0.375
- attn_weight: bfloat16 [256, 128], replicated, may hold values from -0.375 to 0.375
- out_weight: bfloat16 [256, 256], replicated, may hold values from -0.375 to 0.375
- slot_point: int32 [8, 65536], P('dp', ('tile', 'query')), may hold values from 0 to 32767, as said below
- slot_rows: int32 [8, 4, 65536], P('dp', None, ('tile', 'query')), may hold values from 0 to 4095, as said below
- slot_bilinear: float32 [8, 4, 65536], P('dp', None, ('tile', 'query')), may hold values from 0 to 1, as said below
- slot_count: int32 [8, 32], P('dp', ('tile', 'query')), may hold values from 1 to 2048, as said below
Outputs:
- feature_grad: bfloat16 [8, 131072, 256], P('dp', ('tile', 'query'))
- query_grad: bfloat16 [8, 256, 256], P('dp', ('tile', 'query'))
- value_weight_grad: float32 [256, 256], replicated
- attn_weight_grad: float32 [256, 128], replicated
- out_weight_grad: float32 [256, 256], replicated
Inputs may be any that keep to these rules, and one draw needn't show every extreme that they name: `slot_count`: per page one owner has exactly 2048 live slots; the counts of a page sum to 32768. `slot_point`: the live slots of a page name every sample point exactly once, point m = q * 128 + head * 4 * 4 + level * 4 + point; slots that are not live hold arbitrary point numbers. `slot_rows`: the corners of a slot are rows r, r + 1, r + 64, r + 65 of the owner's tokens laid out in lines of 64. `slot_bilinear`: the four weights of a slot sum to one.
All inputs are finite; a program needn't handle non-finite values.
Results may differ from a plain program's by a relative error of at most 0.0064.
Values may be sent and summed in bfloat16 or wider, within the bound.
No kernel may reach another device: no remote copies, remote signals or barrier semaphores. Data moves between devices by JAX's collectives and lax.ppermute only.
A program may use at most 128 MiB of HBM per device.

v0:
```python
import jax
import jax.numpy as jnp
from jax import lax
from jax.sharding import PartitionSpec as P

HEADS = 8
TILE_W = 64


def over_rows(left, right):
    return lax.dot_general(
        left, right, (((0,), (0,)), ((), ())), preferred_element_type=jnp.float32
    )


def over_rows_exact(left, right):
    return lax.dot_general(
        left,
        right,
        (((0,), (0,)), ((), ())),
        precision=lax.Precision.HIGHEST,
        preferred_element_type=jnp.float32,
    )


def times_transpose(left, right):
    return lax.dot_general(
        left, right, (((1,), (1,)), ((), ())), preferred_element_type=jnp.float32
    )


def shift_down(block, offset):
    return jnp.concatenate(
        [jnp.zeros((offset, block.shape[1]), block.dtype), block[: block.shape[0] - offset]], axis=0
    )


def local(
    features,
    queries,
    out_grad,
    value_weight,
    attn_weight,
    out_weight,
    slot_point,
    slot_rows,
    slot_bilinear,
    slot_count,
):
    owners = lax.axis_size(("tile", "query"))
    page_count = lax.axis_size("dp")
    local_queries = queries.shape[1]
    all_queries = local_queries * owners
    grad_scale = float(page_count * all_queries) ** (-0.5)
    width = features.shape[2]
    att_width = attn_weight.shape[1]
    per_head = att_width // HEADS
    head_width = width // HEADS
    exponent = jnp.exp(
        jnp.dot(queries[0], attn_weight, preferred_element_type=jnp.float32)
    ).reshape(local_queries, HEADS, per_head)
    attention = (exponent / jnp.sum(exponent, axis=2, keepdims=True)).reshape(
        local_queries, att_width
    )
    attn_rounded = attention.astype(jnp.bfloat16)
    sample_grad = times_transpose(out_grad[0], out_weight).astype(jnp.bfloat16)
    every_grad, every_attn = (
        lax.all_gather(sample_grad, ("tile", "query"), axis=0, tiled=True),
        lax.all_gather(attn_rounded, ("tile", "query"), axis=0, tiled=True),
    )
    projected = jnp.dot(features[0], value_weight, preferred_element_type=jnp.float32).astype(
        jnp.bfloat16
    )
    token_count = projected.shape[0]
    capacity = slot_point.shape[1]
    points = slot_point[0]
    alive_slot = jnp.arange(capacity, dtype=jnp.int32) < slot_count[0, 0]
    query_index = points // att_width
    attn_column = points % att_width
    head_index = attn_column // per_head
    query_match = query_index[:, None] == jnp.arange(all_queries, dtype=jnp.int32)[None, :]
    query_onehot = query_match.astype(jnp.bfloat16)
    column_match = attn_column[:, None] == jnp.arange(att_width, dtype=jnp.int32)[None, :]
    attn_rows = jnp.dot(query_onehot, every_attn, preferred_element_type=jnp.float32)
    picked_attn = jnp.sum(jnp.where(column_match, attn_rows, jnp.zeros((), jnp.float32)), axis=1)
    weight = jnp.where(alive_slot, picked_attn, jnp.zeros((), jnp.float32))
    head_mask = jnp.arange(width, dtype=jnp.int32)[None, :] // head_width == head_index[:, None]
    grad_rows = jnp.dot(query_onehot, every_grad, preferred_element_type=jnp.float32)
    slot_grad = jnp.where(head_mask, grad_rows, jnp.zeros((), jnp.float32))
    offsets = (0, 1, TILE_W, TILE_W + 1)
    padded = jnp.concatenate([projected, jnp.zeros((TILE_W + 1, width), jnp.bfloat16)], axis=0)
    corner_table = jnp.concatenate(
        [padded[offset : offset + token_count] for offset in offsets], axis=1
    )
    base_row = slot_rows[0, 0]
    picked_all = corner_table[base_row].astype(jnp.float32)
    mixed_rows = jnp.zeros((capacity, width), jnp.float32)
    corner_dots = jnp.zeros((capacity,), jnp.float32)
    contributions = []
    for corner in range(4):
        bilinear = slot_bilinear[0, corner]
        picked = picked_all[:, corner * width : (corner + 1) * width]
        mixed_rows = mixed_rows + bilinear[:, None] * picked
        corner_dots = corner_dots + bilinear * jnp.sum(picked * slot_grad, axis=1)
        contributions.append((weight * bilinear)[:, None] * slot_grad)
    corner_sums = (
        jnp.zeros((token_count, 4 * width), jnp.float32)
        .at[base_row]
        .add(jnp.concatenate(contributions, axis=1))
    )
    value_grad = corner_sums[:, 0:width]
    for corner in range(1, 4):
        value_grad = value_grad + shift_down(
            corner_sums[:, corner * width : (corner + 1) * width], offsets[corner]
        )
    query_float = query_match.astype(jnp.float32)
    sampled_part = over_rows_exact(
        query_float, jnp.where(head_mask, weight[:, None] * mixed_rows, jnp.zeros((), jnp.float32))
    )
    dots_table = jnp.where(
        jnp.logical_and(column_match, alive_slot[:, None]),
        corner_dots[:, None],
        jnp.zeros((), jnp.float32),
    )
    attn_part = over_rows_exact(query_float, dots_table)
    sampled_share, attn_grad = (
        lax.psum_scatter(sampled_part, ("tile", "query"), scatter_dimension=0, tiled=True),
        lax.psum_scatter(attn_part, ("tile", "query"), scatter_dimension=0, tiled=True),
    )
    out_term = over_rows_exact(sampled_share, out_grad[0].astype(jnp.float32))
    attn_three = attention.reshape(local_queries, HEADS, per_head)
    grad_three = attn_grad.reshape(local_queries, HEADS, per_head)
    logit_grad = (
        (attn_three * (grad_three - jnp.sum(attn_three * grad_three, axis=2, keepdims=True)))
        .reshape(local_queries, att_width)
        .astype(jnp.bfloat16)
    )
    query_grad = times_transpose(logit_grad, attn_weight).astype(jnp.bfloat16)
    value_rounded = value_grad.astype(jnp.bfloat16)
    feature_grad = times_transpose(value_rounded, value_weight).astype(jnp.bfloat16)
    value_term = over_rows(features[0], value_rounded)
    attn_term = over_rows(queries[0], logit_grad)
    summed = lax.psum((value_term, attn_term, out_term), ("tile", "query", "dp"))
    return (
        feature_grad[None],
        query_grad[None],
        summed[0] * grad_scale,
        summed[1] * grad_scale,
        summed[2] * grad_scale,
    )


def solution(mesh):
    in_specs = (
        P("dp", ("tile", "query"), None),
        P("dp", ("tile", "query"), None),
        P("dp", ("tile", "query"), None),
        P(),
        P(),
        P(),
        P("dp", ("tile", "query")),
        P("dp", None, ("tile", "query")),
        P("dp", None, ("tile", "query")),
        P("dp", ("tile", "query")),
    )
    out_specs = (P("dp", ("tile", "query"), None), P("dp", ("tile", "query"), None), P(), P(), P())
    return jax.shard_map(local, mesh=mesh, in_specs=in_specs, out_specs=out_specs, check_vma=False)
```

profile of v0, /device:TPU:1, one launch (start us, length us, event | category | flops | bytes accessed | tf_op | source)
XLA Modules:
  0.0 575.8 jit_solution(11358282747532985319)
XLA Ops:
  7.2 0.0 copy-start
  7.2 0.0 all-reduce.9.cloned.1.call-start
  8.0 0.8 compare_select_fusion.2
  8.8 0.7 add_select_fusion.2
  9.5 1.0 convolution_exponential_fusion
  10.5 0.1 reshape.239
  10.6 0.1 reduce_sum.63
  10.7 0.1 div.48
  10.8 0.1 div.49
  10.9 0.9 fusion.64
  11.8 25.9 %all_gather.6 = bf16[256,128]{1,0:T(8,128)(2,1)S(1)} all-gather(bf16[8,128]{1,0:T(8,128)(2,1)S(1)} %divide_convert_fusion), channel_id=1, replica_groups=mesh['tile'=16,'query'=2,'dp'=8] {'tile','query'}, dimensions={0}, use_global_device_ids=true | all-gather | bytes 67584 | tf_op jit(solution)/shard_map/all_gather | solution.py:69
  37.7 1.1 convolution_convert_fusion.3
  38.8 24.1 %all_gather.7 = bf16[256,256]{1,0:T(8,128)(2,1)S(1)} all-gather(bf16[8,256]{1,0:T(8,128)(2,1)S(1)} %convolution_convert_fusion.3), channel_id=1, replica_groups=mesh['tile'=16,'query'=2,'dp'=8] {'tile','query'}, dimensions={0}, use_global_device_ids=true | all-gather | bytes 135168 | tf_op jit(solution)/shard_map/all_gather | solution.py:68
  62.8 0.0 copy-done
  62.8 1.6 convolution_convert_fusion
  64.4 1.3 pad_slice_fusion.2
  65.8 3.9 pad_maximum_fusion.1
  69.7 15.5 %gather_fusion = bf16[2048,1024]{1,0:T(8,128)(2,1)} fusion(bf16[4096,1024]{1,0:T(8,128)(2,1)} %pad_maximum_fusion.1, s32[2048]{0:T(1024)S(1)} %broadcast_clamp_fusion), kind=kCustom, calls=%fused_computation | custom fusion | bytes 8396800 | tf_op jit(solution)/shard_map/gather | solution.py:96
  85.2 6.5 %copy.27 = bf16[2048,1024]{0,1:T(8,128)(2,1)} copy(bf16[2048,1024]{1,0:T(8,128)(2,1)} %gather_fusion) | data formatting | bytes 8388608 | tf_op jit(solution)/shard_map/gather | solution.py:96
  91.7 3.3 convert_element_type.32
  94.9 0.0 copy-start.1
  94.9 0.7 fusion.27
  95.6 4.6 multiply_reduce_fusion.3
  100.3 0.5 copy-done.1
  100.7 2.4 fusion.25
  103.1 0.0 all-reduce.9.cloned.1.call-update
  103.2 0.0 reduce-scatter.2.cloned.1.call-start
  103.2 5.5 fusion.7
  108.7 0.0 reduce-scatter.2.cloned.1.call-update
  108.7 0.2 all-reduce.11.cloned.1.call-start
  109.0 6.0 %pad_maximum_fusion = f32[2048,1024]{0,1:T(8,128)} fusion(f32[2048,256]{0,1:T(8,128)} %get-tuple-element.29, f32[2048,256]{0,1:T(8,128)} %get-tuple-element.30, f32[2048,256]{0,1:T(8,128)} %get-tuple-element.31, f32[2048,256]{0,1:T(8,128)} %get-tuple-element.32), kind=kLoop, calls=%fused_computation.3 | loop fusion | flops 6291456 | bytes 16777216 | tf_op jit(solution)/shard_map/concatenate | solution.py:109
  115.0 9.3 %copy.26 = f32[2048,1024]{1,0:T(8,128)} copy(f32[2048,1024]{0,1:T(8,128)} %pad_maximum_fusion) | data formatting | bytes 16777216 | tf_op jit(solution)/shard_map/concatenate | solution.py:109
  124.2 25.7 %scatter_custom_fusion = f32[4096,1024]{1,0:T(8,128)} fusion(s32[2048]{0:T(1024)S(1)} %bitcast.62, f32[2048,1024]{1,0:T(8,128)} %copy.26, f32[]{:T(128)} %constant.54.clone.1), kind=kCustom, calls=%fused_computation.5 | custom fusion | flops 2097152 | bytes 16777728 | tf_op jit(solution)/shard_map/scatter-add | solution.py:109
  149.9 2.4 slice.75
  152.4 2.4 slice.74
  154.8 2.5 slice.73
  157.3 4.7 fusion.6
  162.0 0.0 copy-start.6
  162.0 0.0 copy-start.5
  162.0 3.1 fusion.28
  165.1 0.0 copy-done.6
  165.1 0.6 dynamic-slice
  166.3 47.7 %all-reduce.9.cloned.1.call-done = f32[256,128]{1,0:T(8,128)} async-done(((f32[256,128]{1,0:T(8,128)}), f32[256,128]{1,0:T(8,128)}) %all-reduce.9.cloned.1.call-update) | async-done | bytes 131088
  214.0 0.7 constant_dynamic-slice_fusion
  214.7 0.1 reshape.240
  214.8 1.2 fusion
  216.0 0.1 sub.31
  216.1 0.0 copy-done.5
  216.1 1.6 convolution_bitcast_fusion
  217.7 83.4 %reduce-scatter.2.cloned.1.call-done = f32[8,256]{1,0:T(8,128)} async-done(((f32[256,256]{1,0:T(8,128)}), f32[8,256]{1,0:T(8,128)}) %reduce-scatter.2.cloned.1.call-update) | async-done | bytes 8208 | tf_op jit(solution)/shard_map/reduce_scatter | solution.py:127
  301.0 0.0 copy-done.4
  301.0 1.7 fusion.56
  302.8 0.0 all-reduce.11.cloned.1.call-update
  302.8 0.0 copy-done.2
  302.8 0.0 copy-start.3
  302.8 3.7 fusion.3
  306.5 0.0 copy-done.3
  306.5 1.4 fusion.31
  307.9 256.9 %all-reduce.11.cloned.1.call-done = (f32[256,256]{0,1:T(8,128)}, f32[256,128]{0,1:T(8,128)}, f32[256,256]{0,1:T(8,128)}) async-done(((f32[256,256]{0,1:T(8,128)}, f32[256,128]{0,1:T(8,128)}, f32[256,256]{0,1:T(8,128)}), (f32[256,256]{0,1:T(8,128)}, f32[256,128]{0,1:T(8,128)}, f32[256,256]{0,1:T(8,128)})) %all-reduce.11.cloned.1.call-update) | async-done | bytes 655376 | tf_op jit(solution)/shard_map/psum | solution.py:143
  564.8 1.1 broadcast_multiply_fusion.4
  565.9 0.8 copy.31
  566.7 0.9 broadcast_multiply_fusion.6
  567.6 0.8 copy.30
  568.4 0.8 copy.29
  (9 shorter events, 0.0 us)
Async XLA Ops:
  7.2 55.7 %copy-start = (bf16[1,4096,256]{2,1,0:T(8,128)(2,1)S(1)}, bf16[1,4096,256]{2,1,0:T(8,128)(2,1)}, u32[]{:S(2)}) copy-start(bf16[1,4096,256]{2,1,0:T(8,128)(2,1)} %param.10) | copy-start | bytes 6291460
  7.2 206.8 %all-reduce.9.cloned.1.call-start = ((), (), s32[]{:S(2)}) async-start(), calls=%async_computation.2 | async-start | bytes 262144
  94.9 5.8 %copy-start.1 = (f32[2048,1024]{0,1:T(8,128)}, f32[2048,1024]{0,1:T(8,128)S(1)}, u32[]{:S(2)}) copy-start(f32[2048,1024]{0,1:T(8,128)S(1)} %convert_element_type.32) | copy-start | bytes 25165828
  103.2 197.9 %reduce-scatter.2.cloned.1.call-start = ((), (), s32[]{:S(2)}) async-start(), calls=%async_computation.1 | async-start | bytes 270336 | tf_op jit(solution)/shard_map/reduce_scatter | solution.py:127
  108.7 456.1 %all-reduce.11.cloned.1.call-start = ((), (), s32[]{:S(2)}) async-start(), calls=%async_computation.3 | async-start | bytes 1310720 | tf_op jit(solution)/shard_map/psum | solution.py:143
  162.0 3.1 copy-start.6
  162.0 54.1 %copy-start.5 = (bf16[1,8,256]{2,1,0:T(8,128)(2,1)S(1)}, bf16[1,8,256]{2,1,0:T(8,128)(2,1)}, u32[]{:S(2)}) copy-start(bf16[1,8,256]{2,1,0:T(8,128)(2,1)} %param.11) | copy-start | bytes 12292
  162.0 139.1 %copy-start.4 = (bf16[1,8,256]{2,1,0:T(8,128)(2,1)S(1)}, bf16[1,8,256]{2,1,0:T(8,128)(2,1)}, u32[]{:S(2)}) copy-start(bf16[1,8,256]{2,1,0:T(8,128)(2,1)} %param.12) | copy-start | bytes 12292
  162.0 140.8 %copy-start.2 = (bf16[256,256]{1,0:T(8,128)(2,1)S(1)}, bf16[256,256]{1,0:T(8,128)(2,1)}, u32[]{:S(2)}) copy-start(bf16[256,256]{1,0:T(8,128)(2,1)} %param.13) | copy-start | bytes 393220
  302.8 3.7 copy-start.3
Sparse Core Ops, SparseCore 0:
  103.3 110.7 all-reduce.8
  218.3 82.6 reduce-scatter.1
  307.6 257.1 all-reduce.10
where the time goes:
time: 577 us; the launch traced here: 576 us
  waiting for transfers between devices  388 us (67%)
  blocking collectives  49.9 us (9%)
  other arithmetic  48.4 us (8%)
  local copies, waits for them, and re-layouts  45.4 us (8%)
  matrix products  28.4 us (5%)
  between operations  15.3 us (3%)
    psum x1, waiting for transfers between devices, local(): lax.psum((value_term, attn_term, out_term), ('tile', 'query', 'dp'))  257 us
    reduce_scatter x1, waiting for transfers between devices, local(): lax.psum_scatter(sampled_part, ('tile', 'query'), scatter_dimension=0, ti...  83.4 us
    unnamed x4, waiting for transfers between devices  47.8 us
    all_gather x1, blocking collectives, local(): lax.all_gather(attn_rounded, ('tile', 'query'), axis=0, tiled=True)  25.9 us
    scatter-add x1, other arithmetic, local(): corner_sums = jnp.zeros((token_count, 4 * width), jnp.float32).at[base_ro...  25.7 us
    all_gather x1, blocking collectives, local(): lax.all_gather(sample_grad, ('tile', 'query'), axis=0, tiled=True)  24.1 us
    gather x2, local copies, waits for them, and re-layouts, local(): picked_all = corner_table[base_row].astype(jnp.float32)  22 us
  transfers between devices with their start and end apart: 3, of which 3 were waited for; matrix products, arithmetic and copies ran while one was open for 12% of the time, Pallas kernels for 0%

commit v1 on v0

--- a/solution.py
+++ b/solution.py
@@ -27,6 +27,27 @@
     return lax.dot_general(
         left, right, (((1,), (1,)), ((), ())), preferred_element_type=jnp.float32
     )
+
+
+def gather_rows(block, axes):
+    count = lax.axis_size(axes)
+    copies = jnp.broadcast_to(block[None], (count,) + block.shape)
+    gathered = lax.all_to_all(copies, axes, 0, 0, tiled=True)
+    return gathered.reshape((count * block.shape[0],) + block.shape[1:])
+
+
+def scatter_sum_rows(block, axes):
+    count = lax.axis_size(axes)
+    pieces = block.reshape((count, block.shape[0] // count) + block.shape[1:])
+    return jnp.sum(lax.all_to_all(pieces, axes, 0, 0, tiled=True), axis=0)
+
+
+def sum_everywhere(block, stages):
+    for axis in stages:
+        block = scatter_sum_rows(block, axis)
+    for axis in reversed(stages):
+        block = gather_rows(block, axis)
+    return block
 
 
 def shift_down(block, offset):
@@ -64,10 +85,11 @@
     )
     attn_rounded = attention.astype(jnp.bfloat16)
     sample_grad = times_transpose(out_grad[0], out_weight).astype(jnp.bfloat16)
-    every_grad, every_attn = (
-        lax.all_gather(sample_grad, ("tile", "query"), axis=0, tiled=True),
-        lax.all_gather(attn_rounded, ("tile", "query"), axis=0, tiled=True),
+    every_both = gather_rows(
+        jnp.concatenate([sample_grad, attn_rounded], axis=1), ("tile", "query")
     )
+    every_grad = every_both[:, :width]
+    every_attn = every_both[:, width:]
     projected = jnp.dot(features[0], value_weight, preferred_element_type=jnp.float32).astype(
         jnp.bfloat16
     )
@@ -123,10 +145,11 @@
         jnp.zeros((), jnp.float32),
     )
     attn_part = over_rows_exact(query_float, dots_table)
-    sampled_share, attn_grad = (
-        lax.psum_scatter(sampled_part, ("tile", "query"), scatter_dimension=0, tiled=True),
-        lax.psum_scatter(attn_part, ("tile", "query"), scatter_dimension=0, tiled=True),
+    shares = scatter_sum_rows(
+        jnp.concatenate([sampled_part, attn_part], axis=1), ("tile", "query")
     )
+    sampled_share = shares[:, :width]
+    attn_grad = shares[:, width:]
     out_term = over_rows_exact(sampled_share, out_grad[0].astype(jnp.float32))
     attn_three = attention.reshape(local_queries, HEADS, per_head)
     grad_three = attn_grad.reshape(local_queries, HEADS, per_head)
@@ -140,13 +163,15 @@
     feature_grad = times_transpose(value_rounded, value_weight).astype(jnp.bfloat16)
     value_term = over_rows(features[0], value_rounded)
     attn_term = over_rows(queries[0], logit_grad)
-    summed = lax.psum((value_term, attn_term, out_term), ("tile", "query", "dp"))
+    summed = sum_everywhere(
+        jnp.concatenate([value_term, attn_term, out_term], axis=1), ("query", "tile", "dp")
+    )
     return (
         feature_grad[None],
         query_grad[None],
-        summed[0] * grad_scale,
-        summed[1] * grad_scale,
-        summed[2] * grad_scale,
+        summed[:, :width] * grad_scale,
+        summed[:, width : width + att_width] * grad_scale,
+        summed[:, width + att_width :] * grad_scale,
     )
 
 

time: 577 us -> 200 us (0.35)
  waiting for transfers between devices: 388 us -> 4.48 us
  starting transfers between devices: 0.3 us -> 19.5 us
  between operations: 15.3 us -> 1.57 us
  matrix products: 28.4 us -> 20.3 us
    psum x1 -> x0, waiting for transfers between devices: 257 us -> none  [local(): lax.psum((value_term, attn_term, out_term), ('tile', 'query', 'dp'))]
    reduce_scatter x1 -> x0, waiting for transfers between devices: 83.4 us -> none  [local(): lax.psum_scatter(sampled_part, ('tile', 'query'), scatter_dimension=0, ti...]
    all_to_all x0 -> x5, blocking collectives: none -> 51.3 us  [the longest x3 33.1 us: scatter_sum_rows(): return jnp.sum(lax.all_to_all(pieces, axes, 0, 0, tiled=True), axis=0)]
    all_gather x2 -> x0, blocking collectives: 49.9 us -> none  [the longest x1 25.9 us: local(): lax.all_gather(attn_rounded, ('tile', 'query'), axis=0, tiled=True)]
    unnamed x4 -> x0, waiting for transfers between devices: 47.8 us -> none
    all_to_all x0 -> x3, starting transfers between devices: none -> 19.5 us  [the longest x2 12.1 us: gather_rows(): gathered = lax.all_to_all(copies, axes, 0, 0, tiled=True)]
    slice x3, local copies, waits for them, and re-layouts: 7.34 us -> 13.2 us  [shift_down(): block[:block.shape[0] - offset]]
  transfers between devices with their start and end apart: 3 -> 3, of which waited for: 3 -> 2; matrix products, arithmetic and copies ran while one was open for 12% -> 25% of each run, Pallas kernels for 0% -> 0%
where the time goes in v1:
time: 200 us; the launch traced here: 199 us
  blocking collectives  51.3 us (26%)
  local copies, waits for them, and re-layouts  51.1 us (26%)
  other arithmetic  50.8 us (25%)
  matrix products  20.3 us (10%)
  starting transfers between devices  19.5 us (10%)
  waiting for transfers between devices  4.48 us (2%)
    all_to_all x3, blocking collectives, scatter_sum_rows(): return jnp.sum(lax.all_to_all(pieces, axes, 0, 0, tiled=True), axis=0)  33.1 us
    scatter-add x1, other arithmetic, local(): corner_sums = jnp.zeros((token_count, 4 * width), jnp.float32).at[base_ro...  25.7 us
    gather x2, local copies, waits for them, and re-layouts, local(): picked_all = corner_table[base_row].astype(jnp.float32)  22 us
    all_to_all x2, blocking collectives, gather_rows(): gathered = lax.all_to_all(copies, axes, 0, 0, tiled=True)  18.1 us
    slice x3, local copies, waits for them, and re-layouts, shift_down(): block[:block.shape[0] - offset]  13.2 us
    all_to_all x2, starting transfers between devices, gather_rows(): gathered = lax.all_to_all(copies, axes, 0, 0, tiled=True)  12.1 us
    concatenate x1, local copies, waits for them, and re-layouts, local(): jnp.concatenate(contributions, axis=1)  9.27 us
    all_to_all x1, starting transfers between devices, scatter_sum_rows(): return jnp.sum(lax.all_to_all(pieces, axes, 0, 0, tiled=True), axis=0)  7.38 us
  transfers between devices with their start and end apart: 3, of which 2 were waited for; matrix products, arithmetic and copies ran while one was open for 25% of the time, Pallas kernels for 0%

profile of v1, /device:TPU:1, one launch (start us, length us, event | category | flops | bytes accessed | tf_op | source)
XLA Modules:
  0.0 199.0 jit_solution(13134733005614984939)
XLA Ops:
  0.6 0.0 copy-start
  0.6 1.1 convolution_exponential_fusion
  1.8 0.1 reshape.265
  1.9 0.1 reduce_sum.99
  1.9 0.1 div.48
  2.0 0.1 div.49
  2.1 1.1 convolution_convert_fusion.3
  3.2 0.7 broadcast_in_dim.42
  3.9 8.6 %all-to-all-start = ((bf16[32,8,384]{2,1,0:T(8,128)(2,1)}), bf16[32,8,384]{2,1,0:T(8,128)(2,1)S(1)}, u32[]{:S(2)}, u32[]{:S(2)}) async-start(bf16[32,8,384]{2,1,0:T(8,128)(2,1)} %broadcast_in_dim.42), calls=%async_computation | async-start | bytes 393216 | tf_op jit(solution)/shard_map/all_to_all | solution.py:35
  12.5 0.9 fusion.65
  14.1 0.0 copy-done
  14.1 1.6 convolution_convert_fusion
  15.8 1.3 pad_slice_fusion.2
  17.1 0.8 compare_select_fusion.2
  17.9 3.9 %pad_maximum_fusion.1 = bf16[4096,1024]{1,0:T(8,128)(2,1)} fusion(bf16[4096,256]{1,0:T(8,128)(2,1)S(1)} %get-tuple-element.19, bf16[4096,256]{1,0:T(8,128)(2,1)S(1)} %get-tuple-element.18, bf16[4096,256]{1,0:T(8,128)(2,1)S(1)} %get-tuple-element.17, bf16[4096,256]{1,0:T(8,128)(2,1)S(1)} %convolution_convert_fusion), kind=kLoop, calls=%fused_computation.4 | loop fusion | flops 33554432 | bytes 16777216 | tf_op jit(solution)/shard_map/concatenate | solution.py:114
  21.8 15.5 %gather_fusion = bf16[2048,1024]{1,0:T(8,128)(2,1)} fusion(bf16[4096,1024]{1,0:T(8,128)(2,1)} %pad_maximum_fusion.1, s32[2048]{0:T(1024)S(1)} %broadcast_clamp_fusion), kind=kCustom, calls=%fused_computation | custom fusion | bytes 8396800 | tf_op jit(solution)/shard_map/gather | solution.py:118
  37.3 6.5 %copy.25 = bf16[2048,1024]{0,1:T(8,128)(2,1)} copy(bf16[2048,1024]{1,0:T(8,128)(2,1)} %gather_fusion) | data formatting | bytes 8388608 | tf_op jit(solution)/shard_map/gather | solution.py:118
  43.8 0.0 copy-start.6
  43.8 6.5 %convert_element_type.32 = f32[2048,1024]{0,1:T(8,128)} convert(bf16[2048,1024]{0,1:T(8,128)(2,1)} %copy.25) | non-fusion elementwise | flops 2097152 | bytes 12582912 | tf_op jit(solution)/shard_map/convert_element_type | solution.py:118
  50.3 0.0 copy-done.6
  50.3 0.0 all-to-all-done
  50.3 0.7 fusion.24
  51.0 4.6 %fusion.7 = f32[256,256]{0,1:T(8,128)S(1)} fusion(f32[2048,1024]{0,1:T(8,128)} %convert_element_type.32, f32[2048]{0:T(1024)S(1)} %bitcast.69, f32[2048]{0:T(1024)S(1)} %bitcast.72, f32[2048]{0:T(1024)S(1)} %bitcast.66, f32[2048]{0:T(1024)S(1)} %bitcast.75, f32[2048]{0:T(1024)S(1)} %get-tuple-element.10, s32[2048]{0:T(1024)S(1)} %get-tuple-element.30, ...), kind=kOutput, calls=%fused_computation.17 | convolution fusion | flops 1616379904 | bytes 8709120 | tf_op jit(solution)/shard_map/dot_general | solution.py:17
  55.6 4.4 %multiply_reduce_fusion.3 = (f32[2048]{0:T(1024)S(1)}, f32[2048]{0:T(1024)S(1)}, f32[2048]{0:T(1024)S(1)}, f32[2048]{0:T(1024)S(1)}, f32[2048,256]{0,1:T(8,128)S...) fusion(f32[2048,1024]{0,1:T(8,128)} %convert_element_type.32, ...), kind=kOutput, calls=%fused_computation.24 | convolution fusion | flops 276291584 | bytes 16991232 | tf_op jit(solution)/shard_map/dot_general | solution.py:110
  60.0 3.8 %pad_maximum_fusion = f32[2048,1024]{0,1:T(8,128)} fusion(f32[2048,256]{0,1:T(8,128)S(1)} %get-tuple-element.13, f32[2048,256]{0,1:T(8,128)S(1)} %get-tuple-element.14, f32[2048,256]{0,1:T(8,128)S(1)} %get-tuple-element.15, f32[2048,256]{0,1:T(8,128)S(1)} %get-tuple-element.16), kind=kLoop, calls=%fused_computation.3 | loop fusion | flops 6291456 | bytes 16777216 | tf_op jit(solution)/shard_map/concatenate | solution.py:131
  63.8 9.3 %copy.24 = f32[2048,1024]{1,0:T(8,128)} copy(f32[2048,1024]{0,1:T(8,128)} %pad_maximum_fusion) | data formatting | bytes 16777216 | tf_op jit(solution)/shard_map/concatenate | solution.py:131
  73.1 25.7 %scatter_custom_fusion = f32[4096,1024]{1,0:T(8,128)} fusion(s32[2048]{0:T(1024)S(1)} %bitcast.78, f32[2048,1024]{1,0:T(8,128)} %copy.24, f32[]{:T(128)} %constant.54.clone.1), kind=kCustom, calls=%fused_computation.5 | custom fusion | flops 2097152 | bytes 16777728 | tf_op jit(solution)/shard_map/scatter-add | solution.py:131
  98.8 4.4 %slice.103 = f32[4095,256]{1,0:T(8,128)} slice(f32[4096,1024]{1,0:T(8,128)} %scatter_custom_fusion), slice={[0:4095], [256:512]} | slice | bytes 8386560 | tf_op jit(solution)/shard_map/slice | solution.py:55
  103.2 4.4 %slice.104 = f32[4032,256]{1,0:T(8,128)} slice(f32[4096,1024]{1,0:T(8,128)} %scatter_custom_fusion), slice={[0:4032], [512:768]} | slice | bytes 8257536 | tf_op jit(solution)/shard_map/slice | solution.py:55
  107.6 4.4 %slice.105 = f32[4031,256]{1,0:T(8,128)} slice(f32[4096,1024]{1,0:T(8,128)} %scatter_custom_fusion), slice={[0:4031], [768:1024]} | slice | bytes 8255488 | tf_op jit(solution)/shard_map/slice | solution.py:55
  112.0 1.2 fusion.19
  113.2 0.9 copy.26
  114.1 7.4 %all-to-all-start.1 = ((f32[32,8,384]{2,1,0:T(8,128)}), f32[32,8,384]{2,1,0:T(8,128)S(1)}, u32[]{:S(2)}, u32[]{:S(2)}) async-start(f32[32,8,384]{2,1,0:T(8,128)} %bitcast.13), calls=%async_computation.1 | async-start | bytes 786432 | tf_op jit(solution)/shard_map/all_to_all | solution.py:42
  121.5 7.0 %fusion.6 = bf16[4096,256]{1,0:T(8,128)(2,1)S(1)} fusion(f32[4096,1024]{1,0:T(8,128)} %scatter_custom_fusion, f32[4031,256]{1,0:T(8,128)} %slice.105, f32[4032,256]{1,0:T(8,128)} %slice.104, f32[4095,256]{1,0:T(8,128)} %slice.103), kind=kLoop, calls=%fused_computation.13 | loop fusion | flops 4194304 | bytes 18741248 | tf_op jit(solution)/shard_map/convert_element_type | solution.py:162
  128.5 0.0 copy-start.1
  128.5 1.3 copy-done.1
  129.8 0.0 copy-start.4
  129.8 0.0 copy-start.5
  129.8 0.7 fusion.25
  130.6 1.1 all-to-all-done.1
  131.7 0.0 copy-done.4
  131.7 0.3 fusion.52
  132.0 0.1 reshape.268
  132.1 1.2 fusion
  133.3 0.1 sub.31
  133.4 0.0 copy-done.5
  133.4 0.2 convolution_bitcast_fusion
  133.7 4.2 %all_to_all.40 = f32[2,128,640]{1,2,0:T(8,128)S(1)} all-to-all(f32[2,128,640]{1,2,0:T(8,128)S(1)} %copy_bitcast_fusion), channel_id=1, replica_groups=mesh['tile'=16,'query'=2,'dp'=8] {'query'}, dimensions={0} | all-to-all | bytes 1310720 | tf_op jit(solution)/shard_map/all_to_all | solution.py:42
  137.9 0.0 copy-start.2
  137.9 0.2 copy.29
  138.1 14.3 %all_to_all.41 = f32[16,8,640]{2,1,0:T(8,128)S(1)} all-to-all(f32[16,8,640]{2,1,0:T(8,128)S(1)} %bitcast.60), channel_id=1, replica_groups=mesh['tile'=16,'query'=2,'dp'=8] {'tile'}, dimensions={0} | all-to-all | bytes 655360 | tf_op jit(solution)/shard_map/all_to_all | solution.py:42
  152.5 14.6 %all_to_all.42 = f32[8,1,640]{2,1,0:T(1,128)S(1)} all-to-all(f32[8,1,640]{2,1,0:T(1,128)S(1)} %reshape.271), channel_id=1, replica_groups=mesh['tile'=16,'query'=2,'dp'=8] {'dp'}, dimensions={0} | all-to-all | bytes 40960 | tf_op jit(solution)/shard_map/all_to_all | solution.py:42
  167.1 9.0 %all_to_all.43 = f32[8,1,640]{2,1,0:T(1,128)S(1)} all-to-all(f32[8,1,640]{2,1,0:T(1,128)S(1)} %broadcast_in_dim.49), channel_id=1, replica_groups=mesh['tile'=16,'query'=2,'dp'=8] {'dp'}, dimensions={0} | all-to-all | bytes 40960 | tf_op jit(solution)/shard_map/all_to_all | solution.py:35
  176.1 0.8 broadcast_in_dim.51
  176.9 3.5 %all-to-all-start.6 = ((f32[16,8,640]{2,1,0:T(8,128)}), f32[16,8,640]{2,1,0:T(8,128)S(1)}, u32[]{:S(2)}, u32[]{:S(2)}) async-start(f32[16,8,640]{2,1,0:T(8,128)} %broadcast_in_dim.51), calls=%async_computation.6 | async-start | bytes 655360 | tf_op jit(solution)/shard_map/all_to_all | solution.py:35
  180.5 0.0 copy-done.2
  180.5 0.0 copy-start.3
  180.5 3.7 %fusion.3 = bf16[1,4096,256]{2,1,0:T(8,128)(2,1)} fusion(bf16[4096,256]{1,0:T(8,128)(2,1)} %copy-done.1, bf16[256,256]{1,0:T(8,128)(2,1)S(1)} %copy-done.2), kind=kOutput, calls=%fused_computation.9 | convolution fusion | flops 537919488 | bytes 4325376 | tf_op jit(solution)/shard_map/dot_general | solution.py:27
  184.2 0.0 copy-done.3
  184.2 0.7 fusion.28
  184.9 3.4 %all-to-all-done.6 = f32[16,8,640]{2,1,0:T(8,128)S(1)} async-done(((f32[16,8,640]{2,1,0:T(8,128)}), f32[16,8,640]{2,1,0:T(8,128)S(1)}, u32[]{:S(2)}, u32[]{:S(2)}) %all-to-all-start.6) | async-done | bytes 327712 | tf_op jit(solution)/shard_map/all_to_all | solution.py:35
  188.4 9.1 %all_to_all.44 = f32[2,128,640]{2,1,0:T(8,128)S(1)} all-to-all(f32[2,128,640]{2,1,0:T(8,128)S(1)} %broadcast_in_dim.91), channel_id=1, replica_groups=mesh['tile'=16,'query'=2,'dp'=8] {'query'}, dimensions={0} | all-to-all | bytes 1310720 | tf_op jit(solution)/shard_map/all_to_all | solution.py:35
  197.5 0.8 slice_multiply_fusion
  198.4 0.7 slice_multiply_fusion.2
  (21 shorter events, 0.4 us)
Async XLA Ops:
  0.6 13.5 %copy-start = (bf16[1,4096,256]{2,1,0:T(8,128)(2,1)S(1)}, bf16[1,4096,256]{2,1,0:T(8,128)(2,1)}, u32[]{:S(2)}) copy-start(bf16[1,4096,256]{2,1,0:T(8,128)(2,1)} %param.10) | copy-start | bytes 6291460
  3.9 46.4 %all-to-all-start = ((bf16[32,8,384]{2,1,0:T(8,128)(2,1)}), bf16[32,8,384]{2,1,0:T(8,128)(2,1)S(1)}, u32[]{:S(2)}, u32[]{:S(2)}) async-start(bf16[32,8,384]{2,1,0:T(8,128)(2,1)} %broadcast_in_dim.42), calls=%async_computation | async-start | bytes 393216 | tf_op jit(solution)/shard_map/all_to_all | solution.py:35
  43.8 6.5 %copy-start.6 = (s32[1,2048]{1,0:T(1,128)S(1)}, s32[1,2048]{1,0:T(1,128)}, u32[]{:S(2)}) copy-start(s32[1,2048]{1,0:T(1,128)} %param.16) | copy-start | bytes 24580
  114.1 17.5 %all-to-all-start.1 = ((f32[32,8,384]{2,1,0:T(8,128)}), f32[32,8,384]{2,1,0:T(8,128)S(1)}, u32[]{:S(2)}, u32[]{:S(2)}) async-start(f32[32,8,384]{2,1,0:T(8,128)} %bitcast.13), calls=%async_computation.1 | async-start | bytes 786432 | tf_op jit(solution)/shard_map/all_to_all | solution.py:42
  128.5 1.4 copy-start.1
  129.8 1.9 copy-start.4
  129.8 3.6 %copy-start.5 = (bf16[1,8,256]{2,1,0:T(8,128)(2,1)S(1)}, bf16[1,8,256]{2,1,0:T(8,128)(2,1)}, u32[]{:S(2)}) copy-start(bf16[1,8,256]{2,1,0:T(8,128)(2,1)} %param.11) | copy-start | bytes 12292
  137.9 42.6 %copy-start.2 = (bf16[256,256]{1,0:T(8,128)(2,1)S(1)}, bf16[256,256]{1,0:T(8,128)(2,1)}, u32[]{:S(2)}) copy-start(bf16[256,256]{1,0:T(8,128)(2,1)} %param.13) | copy-start | bytes 393220
  176.9 11.4 %all-to-all-start.6 = ((f32[16,8,640]{2,1,0:T(8,128)}), f32[16,8,640]{2,1,0:T(8,128)S(1)}, u32[]{:S(2)}, u32[]{:S(2)}) async-start(f32[16,8,640]{2,1,0:T(8,128)} %broadcast_in_dim.51), calls=%async_computation.6 | async-start | bytes 655360 | tf_op jit(solution)/shard_map/all_to_all | solution.py:35
  180.5 3.7 %copy-start.3 = (bf16[256,128]{1,0:T(8,128)(2,1)S(1)}, bf16[256,128]{1,0:T(8,128)(2,1)}, u32[]{:S(2)}) copy-start(bf16[256,128]{1,0:T(8,128)(2,1)} %param.14) | copy-start | bytes 196612

commit v2 on v1

--- a/solution.py
+++ b/solution.py
@@ -42,13 +42,12 @@
     return jnp.sum(lax.all_to_all(pieces, axes, 0, 0, tiled=True), axis=0)
 
 
-def sum_everywhere(block, stages):
-    for axis in stages:
-        block = scatter_sum_rows(block, axis)
-    for axis in reversed(stages):
-        block = gather_rows(block, axis)
-    return block
-
+def sum_everywhere(block):
+    block = scatter_sum_rows(block, ("tile", "query"))
+    count = lax.axis_size("dp")
+    copies = jnp.broadcast_to(block[None], (count,) + block.shape)
+    block = jnp.sum(lax.all_to_all(copies, "dp", 0, 0, tiled=True), axis=0)
+    return gather_rows(block, ("tile", "query"))
 
 def shift_down(block, offset):
     return jnp.concatenate(
@@ -163,9 +162,7 @@
     feature_grad = times_transpose(value_rounded, value_weight).astype(jnp.bfloat16)
     value_term = over_rows(features[0], value_rounded)
     attn_term = over_rows(queries[0], logit_grad)
-    summed = sum_everywhere(
-        jnp.concatenate([value_term, attn_term, out_term], axis=1), ("query", "tile", "dp")
-    )
+    summed = sum_everywhere(jnp.concatenate([value_term, attn_term, out_term], axis=1))
     return (
         feature_grad[None],
         query_grad[None],

time: 200 us -> 192 us (0.960)
  blocking collectives: 51.3 us -> 35.6 us
  waiting for transfers between devices: 4.48 us -> 9.46 us
  starting transfers between devices: 19.5 us -> 21.9 us
    all_to_all x3 -> x1, blocking collectives: 33.1 us -> 19.1 us  [scatter_sum_rows(): return jnp.sum(lax.all_to_all(pieces, axes, 0, 0, tiled=True), axis=0)]
    all_to_all x2, waiting for transfers between devices: 3.4 us -> 8.38 us  [gather_rows(): gathered = lax.all_to_all(copies, axes, 0, 0, tiled=True)]
    all_to_all x2, starting transfers between devices: 12.1 us -> 14.5 us  [gather_rows(): gathered = lax.all_to_all(copies, axes, 0, 0, tiled=True)]
    all_to_all x2 -> x1, blocking collectives: 18.1 us -> 16.5 us  [sum_everywhere(): block = jnp.sum(lax.all_to_all(copies, 'dp', 0, 0, tiled=True), axis=0)]
  transfers between devices with their start and end apart: 3 -> 3, of which waited for: 2 -> 2; matrix products, arithmetic and copies ran while one was open for 25% -> 26% of each run, Pallas kernels for 0% -> 0%
where the time goes in v2:
time: 192 us; the launch traced here: 191 us
  local copies, waits for them, and re-layouts  51.2 us (27%)
  other arithmetic  50.8 us (26%)
  blocking collectives  35.6 us (19%)
  starting transfers between devices  21.9 us (11%)
  matrix products  20.3 us (11%)
  waiting for transfers between devices  9.46 us (5%)
    scatter-add x1, other arithmetic, local(): corner_sums = jnp.zeros((token_count, 4 * width), jnp.float32).at[base_ro...  25.7 us
    gather x2, local copies, waits for them, and re-layouts, local(): picked_all = corner_table[base_row].astype(jnp.float32)  22 us
    all_to_all x1, blocking collectives, scatter_sum_rows(): return jnp.sum(lax.all_to_all(pieces, axes, 0, 0, tiled=True), axis=0)  19.1 us
    all_to_all x1, blocking collectives, sum_everywhere(): block = jnp.sum(lax.all_to_all(copies, 'dp', 0, 0, tiled=True), axis=0)  16.5 us
    all_to_all x2, starting transfers between devices, gather_rows(): gathered = lax.all_to_all(copies, axes, 0, 0, tiled=True)  14.5 us
    slice x3, local copies, waits for them, and re-layouts, shift_down(): block[:block.shape[0] - offset]  13.2 us
    concatenate x1, local copies, waits for them, and re-layouts, local(): jnp.concatenate(contributions, axis=1)  9.27 us
    all_to_all x2, waiting for transfers between devices, gather_rows(): gathered = lax.all_to_all(copies, axes, 0, 0, tiled=True)  8.38 us
  transfers between devices with their start and end apart: 3, of which 2 were waited for; matrix products, arithmetic and copies ran while one was open for 26% of the time, Pallas kernels for 0%

profile of v2, /device:TPU:1, one launch (start us, length us, event | category | flops | bytes accessed | tf_op | source)
XLA Modules:
  0.0 190.8 jit_solution(14449701954422042154)
XLA Ops:
  0.6 0.0 copy-start
  0.6 1.1 convolution_exponential_fusion
  1.8 0.1 reshape.254
  1.9 0.1 reduce_sum.90
  1.9 0.1 div.48
  2.0 0.1 div.49
  2.1 1.1 convolution_convert_fusion.3
  3.2 0.7 broadcast_in_dim.32
  3.9 8.6 %all-to-all-start = ((bf16[32,8,384]{2,1,0:T(8,128)(2,1)}), bf16[32,8,384]{2,1,0:T(8,128)(2,1)S(1)}, u32[]{:S(2)}, u32[]{:S(2)}) async-start(bf16[32,8,384]{2,1,0:T(8,128)(2,1)} %broadcast_in_dim.32), calls=%async_computation | async-start | bytes 393216 | tf_op jit(solution)/shard_map/all_to_all | solution.py:35
  12.5 0.9 fusion.65
  14.1 0.0 copy-done
  14.1 1.6 convolution_convert_fusion
  15.8 1.3 pad_slice_fusion.2
  17.1 0.8 compare_select_fusion.2
  17.9 3.9 %pad_maximum_fusion.1 = bf16[4096,1024]{1,0:T(8,128)(2,1)} fusion(bf16[4096,256]{1,0:T(8,128)(2,1)S(1)} %get-tuple-element.19, bf16[4096,256]{1,0:T(8,128)(2,1)S(1)} %get-tuple-element.18, bf16[4096,256]{1,0:T(8,128)(2,1)S(1)} %get-tuple-element.17, bf16[4096,256]{1,0:T(8,128)(2,1)S(1)} %convolution_convert_fusion), kind=kLoop, calls=%fused_computation.4 | loop fusion | flops 33554432 | bytes 16777216 | tf_op jit(solution)/shard_map/concatenate | solution.py:113
  21.8 15.5 %gather_fusion = bf16[2048,1024]{1,0:T(8,128)(2,1)} fusion(bf16[4096,1024]{1,0:T(8,128)(2,1)} %pad_maximum_fusion.1, s32[2048]{0:T(1024)S(1)} %broadcast_clamp_fusion), kind=kCustom, calls=%fused_computation | custom fusion | bytes 8396800 | tf_op jit(solution)/shard_map/gather | solution.py:117
  37.3 6.5 %copy.21 = bf16[2048,1024]{0,1:T(8,128)(2,1)} copy(bf16[2048,1024]{1,0:T(8,128)(2,1)} %gather_fusion) | data formatting | bytes 8388608 | tf_op jit(solution)/shard_map/gather | solution.py:117
  43.8 0.0 copy-start.6
  43.8 6.5 %convert_element_type.32 = f32[2048,1024]{0,1:T(8,128)} convert(bf16[2048,1024]{0,1:T(8,128)(2,1)} %copy.21) | non-fusion elementwise | flops 2097152 | bytes 12582912 | tf_op jit(solution)/shard_map/convert_element_type | solution.py:117
  50.3 0.0 copy-done.6
  50.3 0.0 all-to-all-done
  50.3 0.7 fusion.24
  51.0 4.6 %fusion.7 = f32[256,256]{0,1:T(8,128)S(1)} fusion(f32[2048,1024]{0,1:T(8,128)} %convert_element_type.32, f32[2048]{0:T(1024)S(1)} %bitcast.58, f32[2048]{0:T(1024)S(1)} %bitcast.61, f32[2048]{0:T(1024)S(1)} %bitcast.55, f32[2048]{0:T(1024)S(1)} %bitcast.64, f32[2048]{0:T(1024)S(1)} %get-tuple-element.10, s32[2048]{0:T(1024)S(1)} %get-tuple-element.30, ...), kind=kOutput, calls=%fused_computation.17 | convolution fusion | flops 1616379904 | bytes 8709120 | tf_op jit(solution)/shard_map/dot_general | solution.py:17
  55.6 4.4 %multiply_reduce_fusion.3 = (f32[2048]{0:T(1024)S(1)}, f32[2048]{0:T(1024)S(1)}, f32[2048]{0:T(1024)S(1)}, f32[2048]{0:T(1024)S(1)}, f32[2048,256]{0,1:T(8,128)S...) fusion(f32[2048,1024]{0,1:T(8,128)} %convert_element_type.32, ...), kind=kOutput, calls=%fused_computation.24 | convolution fusion | flops 276291584 | bytes 16991232 | tf_op jit(solution)/shard_map/dot_general | solution.py:109
  60.0 3.8 %pad_maximum_fusion = f32[2048,1024]{0,1:T(8,128)} fusion(f32[2048,256]{0,1:T(8,128)S(1)} %get-tuple-element.13, f32[2048,256]{0,1:T(8,128)S(1)} %get-tuple-element.14, f32[2048,256]{0,1:T(8,128)S(1)} %get-tuple-element.15, f32[2048,256]{0,1:T(8,128)S(1)} %get-tuple-element.16), kind=kLoop, calls=%fused_computation.3 | loop fusion | flops 6291456 | bytes 16777216 | tf_op jit(solution)/shard_map/concatenate | solution.py:130
  63.8 9.3 %copy.20 = f32[2048,1024]{1,0:T(8,128)} copy(f32[2048,1024]{0,1:T(8,128)} %pad_maximum_fusion) | data formatting | bytes 16777216 | tf_op jit(solution)/shard_map/concatenate | solution.py:130
  73.1 25.7 %scatter_custom_fusion = f32[4096,1024]{1,0:T(8,128)} fusion(s32[2048]{0:T(1024)S(1)} %bitcast.67, f32[2048,1024]{1,0:T(8,128)} %copy.20, f32[]{:T(128)} %constant.54.clone.1), kind=kCustom, calls=%fused_computation.5 | custom fusion | flops 2097152 | bytes 16777728 | tf_op jit(solution)/shard_map/scatter-add | solution.py:130
  98.8 4.4 %slice.103 = f32[4095,256]{1,0:T(8,128)} slice(f32[4096,1024]{1,0:T(8,128)} %scatter_custom_fusion), slice={[0:4095], [256:512]} | slice | bytes 8386560 | tf_op jit(solution)/shard_map/slice | solution.py:54
  103.2 4.4 %slice.104 = f32[4032,256]{1,0:T(8,128)} slice(f32[4096,1024]{1,0:T(8,128)} %scatter_custom_fusion), slice={[0:4032], [512:768]} | slice | bytes 8257536 | tf_op jit(solution)/shard_map/slice | solution.py:54
  107.6 4.4 %slice.105 = f32[4031,256]{1,0:T(8,128)} slice(f32[4096,1024]{1,0:T(8,128)} %scatter_custom_fusion), slice={[0:4031], [768:1024]} | slice | bytes 8255488 | tf_op jit(solution)/shard_map/slice | solution.py:54
  112.0 1.2 fusion.19
  113.2 0.9 copy.22
  114.1 7.4 %all-to-all-start.1 = ((f32[32,8,384]{2,1,0:T(8,128)}), f32[32,8,384]{2,1,0:T(8,128)S(1)}, u32[]{:S(2)}, u32[]{:S(2)}) async-start(f32[32,8,384]{2,1,0:T(8,128)} %bitcast.13), calls=%async_computation.1 | async-start | bytes 786432 | tf_op jit(solution)/shard_map/all_to_all | solution.py:42
  121.5 7.0 %fusion.6 = bf16[4096,256]{1,0:T(8,128)(2,1)S(1)} fusion(f32[4096,1024]{1,0:T(8,128)} %scatter_custom_fusion, f32[4031,256]{1,0:T(8,128)} %slice.105, f32[4032,256]{1,0:T(8,128)} %slice.104, f32[4095,256]{1,0:T(8,128)} %slice.103), kind=kLoop, calls=%fused_computation.13 | loop fusion | flops 4194304 | bytes 18741248 | tf_op jit(solution)/shard_map/convert_element_type | solution.py:161
  128.5 0.0 copy-start.1
  128.5 1.3 copy-done.1
  129.8 0.0 copy-start.4
  129.8 0.0 copy-start.5
  129.8 0.7 fusion.25
  130.6 1.1 all-to-all-done.1
  131.7 0.0 copy-done.4
  131.7 0.3 fusion.52
  132.0 0.1 reshape.257
  132.1 1.2 fusion
  133.3 0.1 sub.31
  133.4 0.0 copy-done.5
  133.4 0.2 convolution_bitcast_fusion
  133.7 0.2 copy.23
  133.9 0.0 copy-start.2
  134.0 19.1 %all_to_all.25 = f32[32,8,640]{2,1,0:T(8,128)S(1)} all-to-all(f32[32,8,640]{2,1,0:T(8,128)S(1)} %bitcast.51), channel_id=1, replica_groups=mesh['tile'=16,'query'=2,'dp'=8] {'tile','query'}, dimensions={0} | all-to-all | bytes 1310720 | tf_op jit(solution)/shard_map/all_to_all | solution.py:42
  153.0 0.1 reduce_sum.98
  153.1 16.5 %all_to_all.26 = f32[8,8,640]{2,1,0:T(8,128)S(1)} all-to-all(f32[8,8,640]{2,1,0:T(8,128)S(1)} %broadcast_in_dim.43), channel_id=1, replica_groups=mesh['tile'=16,'query'=2,'dp'=8] {'dp'}, dimensions={0} | all-to-all | bytes 327680 | tf_op jit(solution)/shard_map/all_to_all | solution.py:49
  169.6 0.9 broadcast_in_dim.44
  170.5 5.9 %all-to-all-start.4 = ((f32[32,8,640]{2,1,0:T(8,128)}), f32[32,8,640]{2,1,0:T(8,128)S(1)}, u32[]{:S(2)}, u32[]{:S(2)}) async-start(f32[32,8,640]{2,1,0:T(8,128)} %broadcast_in_dim.44), calls=%async_computation.4 | async-start | bytes 1310720 | tf_op jit(solution)/shard_map/all_to_all | solution.py:35
  176.4 0.0 copy-done.2
  176.4 0.0 copy-start.3
  176.4 3.7 %fusion.3 = bf16[1,4096,256]{2,1,0:T(8,128)(2,1)} fusion(bf16[4096,256]{1,0:T(8,128)(2,1)} %copy-done.1, bf16[256,256]{1,0:T(8,128)(2,1)S(1)} %copy-done.2), kind=kOutput, calls=%fused_computation.9 | convolution fusion | flops 537919488 | bytes 4325376 | tf_op jit(solution)/shard_map/dot_general | solution.py:27
  180.1 0.0 copy-done.3
  180.1 0.7 fusion.28
  180.9 8.4 %all-to-all-done.4 = f32[32,8,640]{2,1,0:T(8,128)S(1)} async-done(((f32[32,8,640]{2,1,0:T(8,128)}), f32[32,8,640]{2,1,0:T(8,128)S(1)}, u32[]{:S(2)}, u32[]{:S(2)}) %all-to-all-start.4) | async-done | bytes 655392 | tf_op jit(solution)/shard_map/all_to_all | solution.py:35
  189.3 0.8 slice_multiply_fusion
  190.1 0.7 slice_multiply_fusion.2
  (16 shorter events, 0.3 us)
Async XLA Ops:
  0.6 13.5 %copy-start = (bf16[1,4096,256]{2,1,0:T(8,128)(2,1)S(1)}, bf16[1,4096,256]{2,1,0:T(8,128)(2,1)}, u32[]{:S(2)}) copy-start(bf16[1,4096,256]{2,1,0:T(8,128)(2,1)} %param.10) | copy-start | bytes 6291460
  3.9 46.4 %all-to-all-start = ((bf16[32,8,384]{2,1,0:T(8,128)(2,1)}), bf16[32,8,384]{2,1,0:T(8,128)(2,1)S(1)}, u32[]{:S(2)}, u32[]{:S(2)}) async-start(bf16[32,8,384]{2,1,0:T(8,128)(2,1)} %broadcast_in_dim.32), calls=%async_computation | async-start | bytes 393216 | tf_op jit(solution)/shard_map/all_to_all | solution.py:35
  43.8 6.5 %copy-start.6 = (s32[1,2048]{1,0:T(1,128)S(1)}, s32[1,2048]{1,0:T(1,128)}, u32[]{:S(2)}) copy-start(s32[1,2048]{1,0:T(1,128)} %param.16) | copy-start | bytes 24580
  114.1 17.5 %all-to-all-start.1 = ((f32[32,8,384]{2,1,0:T(8,128)}), f32[32,8,384]{2,1,0:T(8,128)S(1)}, u32[]{:S(2)}, u32[]{:S(2)}) async-start(f32[32,8,384]{2,1,0:T(8,128)} %bitcast.13), calls=%async_computation.1 | async-start | bytes 786432 | tf_op jit(solution)/shard_map/all_to_all | solution.py:42
  128.5 1.4 copy-start.1
  129.8 1.9 copy-start.4
  129.8 3.6 %copy-start.5 = (bf16[1,8,256]{2,1,0:T(8,128)(2,1)S(1)}, bf16[1,8,256]{2,1,0:T(8,128)(2,1)}, u32[]{:S(2)}) copy-start(bf16[1,8,256]{2,1,0:T(8,128)(2,1)} %param.11) | copy-start | bytes 12292
  133.9 42.5 %copy-start.2 = (bf16[256,256]{1,0:T(8,128)(2,1)S(1)}, bf16[256,256]{1,0:T(8,128)(2,1)}, u32[]{:S(2)}) copy-start(bf16[256,256]{1,0:T(8,128)(2,1)} %param.13) | copy-start | bytes 393220
  170.5 18.7 %all-to-all-start.4 = ((f32[32,8,640]{2,1,0:T(8,128)}), f32[32,8,640]{2,1,0:T(8,128)S(1)}, u32[]{:S(2)}, u32[]{:S(2)}) async-start(f32[32,8,640]{2,1,0:T(8,128)} %broadcast_in_dim.44), calls=%async_computation.4 | async-start | bytes 1310720 | tf_op jit(solution)/shard_map/all_to_all | solution.py:35
  176.4 3.7 %copy-start.3 = (bf16[256,128]{1,0:T(8,128)(2,1)S(1)}, bf16[256,128]{1,0:T(8,128)(2,1)}, u32[]{:S(2)}) copy-start(bf16[256,128]{1,0:T(8,128)(2,1)} %param.14) | copy-start | bytes 196612

commit v3 on v2

--- a/solution.py
+++ b/solution.py
@@ -1,6 +1,7 @@
 import jax
 import jax.numpy as jnp
 from jax import lax
+from jax.experimental.layout import Layout, with_layout_constraint
 from jax.sharding import PartitionSpec as P
 
 HEADS = 8
@@ -48,6 +49,10 @@
     copies = jnp.broadcast_to(block[None], (count,) + block.shape)
     block = jnp.sum(lax.all_to_all(copies, "dp", 0, 0, tiled=True), axis=0)
     return gather_rows(block, ("tile", "query"))
+
+def row_major(block):
+    return with_layout_constraint(block, Layout(major_to_minor=(0, 1)))
+
 
 def shift_down(block, offset):
     return jnp.concatenate(
@@ -107,14 +112,14 @@
     weight = jnp.where(alive_slot, picked_attn, jnp.zeros((), jnp.float32))
     head_mask = jnp.arange(width, dtype=jnp.int32)[None, :] // head_width == head_index[:, None]
     grad_rows = jnp.dot(query_onehot, every_grad, preferred_element_type=jnp.float32)
-    slot_grad = jnp.where(head_mask, grad_rows, jnp.zeros((), jnp.float32))
+    slot_grad = row_major(jnp.where(head_mask, grad_rows, jnp.zeros((), jnp.float32)))
     offsets = (0, 1, TILE_W, TILE_W + 1)
     padded = jnp.concatenate([projected, jnp.zeros((TILE_W + 1, width), jnp.bfloat16)], axis=0)
     corner_table = jnp.concatenate(
         [padded[offset : offset + token_count] for offset in offsets], axis=1
     )
     base_row = slot_rows[0, 0]
-    picked_all = corner_table[base_row].astype(jnp.float32)
+    picked_all = row_major(corner_table[base_row]).astype(jnp.float32)
     mixed_rows = jnp.zeros((capacity, width), jnp.float32)
     corner_dots = jnp.zeros((capacity,), jnp.float32)
     contributions = []
@@ -124,15 +129,18 @@
         mixed_rows = mixed_rows + bilinear[:, None] * picked
         corner_dots = corner_dots + bilinear * jnp.sum(picked * slot_grad, axis=1)
         contributions.append((weight * bilinear)[:, None] * slot_grad)
+    margin = TILE_W + 1
     corner_sums = (
-        jnp.zeros((token_count, 4 * width), jnp.float32)
-        .at[base_row]
-        .add(jnp.concatenate(contributions, axis=1))
+        jnp.zeros((token_count + margin, 4 * width), jnp.float32)
+        .at[base_row + margin]
+        .add(row_major(jnp.concatenate(contributions, axis=1)))
     )
-    value_grad = corner_sums[:, 0:width]
+    value_grad = corner_sums[margin : margin + token_count, 0:width]
     for corner in range(1, 4):
-        value_grad = value_grad + shift_down(
-            corner_sums[:, corner * width : (corner + 1) * width], offsets[corner]
+        start = margin - offsets[corner]
+        value_grad = (
+            value_grad
+            + corner_sums[start : start + token_count, corner * width : (corner + 1) * width]
         )
     query_float = query_match.astype(jnp.float32)
     sampled_part = over_rows_exact(

time: 192 us -> 167 us (0.87)
  local copies, waits for them, and re-layouts: 51.2 us -> 22.3 us
  matrix products: 20.3 us -> 28.7 us
  other arithmetic: 50.8 us -> 46.8 us
    slice x3 -> x0, local copies, waits for them, and re-layouts: 13.2 us -> none  [shift_down(): block[:block.shape[0] - offset]]
    concatenate x1 -> x0, local copies, waits for them, and re-layouts: 9.27 us -> none  [local(): jnp.concatenate(contributions, axis=1)]
    gather x2 -> x1, local copies, waits for them, and re-layouts: 22 us -> 15.5 us  [local(): picked_all = row_major(corner_table[base_row]).astype(jnp.float32)]
    dot_general x1, matrix products: 4.37 us -> 8.76 us  [local(): jnp.dot(query_onehot, every_grad, preferred_element_type=jnp.float32)]
    dot_general x3, matrix products: 6.09 us -> 10.1 us  [over_rows_exact(): lax.dot_general(left, right, (((0,), (0,)), ((), ())), precision=lax.Prec...]
    concatenate x1 -> x0, other arithmetic: 3.82 us -> none  [local(): jnp.concatenate(contributions, axis=1)]
  transfers between devices with their start and end apart: 3 -> 3, of which waited for: 2 -> 1; matrix products, arithmetic and copies ran while one was open for 26% -> 41% of each run, Pallas kernels for 0% -> 0%
where the time goes in v3:
time: 167 us; the launch traced here: 166 us
  other arithmetic  46.8 us (28%)
  blocking collectives  36.7 us (22%)
  matrix products  28.7 us (17%)
  local copies, waits for them, and re-layouts  22.3 us (13%)
  starting transfers between devices  21.9 us (13%)
  waiting for transfers between devices  8.39 us (5%)
    scatter-add x1, other arithmetic, local(): corner_sums = jnp.zeros((token_count + margin, 4 * width), jnp.float32).a...  25.5 us
    all_to_all x1, blocking collectives, scatter_sum_rows(): return jnp.sum(lax.all_to_all(pieces, axes, 0, 0, tiled=True), axis=0)  20.1 us
    all_to_all x1, blocking collectives, sum_everywhere(): block = jnp.sum(lax.all_to_all(copies, 'dp', 0, 0, tiled=True), axis=0)  16.5 us
    gather x1, local copies, waits for them, and re-layouts, local(): picked_all = row_major(corner_table[base_row]).astype(jnp.float32)  15.5 us
    all_to_all x2, starting transfers between devices, gather_rows(): gathered = lax.all_to_all(copies, axes, 0, 0, tiled=True)  14.5 us
    dot_general x3, matrix products, over_rows_exact(): lax.dot_general(left, right, (((0,), (0,)), ((), ())), precision=lax.Prec...  10.1 us
    dot_general x1, matrix products, local(): jnp.dot(query_onehot, every_grad, preferred_element_type=jnp.float32)  8.76 us
    all_to_all x2, waiting for transfers between devices, gather_rows(): gathered = lax.all_to_all(copies, axes, 0, 0, tiled=True)  8.39 us
  transfers between devices with their start and end apart: 3, of which 1 were waited for; matrix products, arithmetic and copies ran while one was open for 41% of the time, Pallas kernels for 0%

profile of v3, /device:TPU:1, one launch (start us, length us, event | category | flops | bytes accessed | tf_op | source)
XLA Modules:
  0.0 166.3 jit_solution(3926577044997661026)
XLA Ops:
  0.6 0.0 copy-start
  0.6 1.1 convolution_exponential_fusion
  1.8 0.1 reshape.279
  1.9 0.1 reduce_sum.90
  1.9 0.1 div.48
  2.0 0.1 div.49
  2.1 1.1 convolution_convert_fusion.3
  3.2 0.7 broadcast_in_dim.36
  3.9 8.6 %all-to-all-start = ((bf16[32,8,384]{2,1,0:T(8,128)(2,1)}), bf16[32,8,384]{2,1,0:T(8,128)(2,1)S(1)}, u32[]{:S(2)}, u32[]{:S(2)}) async-start(bf16[32,8,384]{2,1,0:T(8,128)(2,1)} %broadcast_in_dim.36), calls=%async_computation | async-start | bytes 393216 | tf_op jit(solution)/shard_map/all_to_all | solution.py:36
  12.5 0.9 fusion.70
  14.1 0.0 copy-done
  14.1 1.6 convolution_convert_fusion
  15.7 1.3 pad_slice_fusion.2
  17.1 0.8 compare_select_fusion.2
  17.9 3.9 %pad_maximum_fusion = bf16[4096,1024]{1,0:T(8,128)(2,1)} fusion(bf16[4096,256]{1,0:T(8,128)(2,1)S(1)} %get-tuple-element.19, bf16[4096,256]{1,0:T(8,128)(2,1)S(1)} %get-tuple-element.18, bf16[4096,256]{1,0:T(8,128)(2,1)S(1)} %get-tuple-element.17, bf16[4096,256]{1,0:T(8,128)(2,1)S(1)} %convolution_convert_fusion), kind=kLoop, calls=%fused_computation.12 | loop fusion | flops 33554432 | bytes 16777216 | tf_op jit(solution)/shard_map/concatenate | solution.py:118
  21.8 15.5 %gather_fusion = bf16[2048,1024]{1,0:T(8,128)(2,1)} fusion(bf16[4096,1024]{1,0:T(8,128)(2,1)} %pad_maximum_fusion, s32[2048]{0:T(1024)S(1)} %broadcast_clamp_fusion), kind=kCustom, calls=%fused_computation | custom fusion | bytes 8396800 | tf_op jit(solution)/shard_map/gather | solution.py:122
  37.3 0.0 copy-start.6
  37.3 6.5 %convert_element_type.32 = f32[2048,1024]{1,0:T(8,128)} convert(bf16[2048,1024]{1,0:T(8,128)(2,1)} %gather_fusion) | non-fusion elementwise | flops 2097152 | bytes 12582912 | tf_op jit(solution)/shard_map/convert_element_type | solution.py:122
  43.7 0.0 copy-done.6
  43.8 0.0 all-to-all-done
  43.8 0.7 fusion.29
  44.5 8.7 %fusion.12 = f32[256,256]{0,1:T(8,128)S(1)} fusion(f32[2048,1024]{1,0:T(8,128)} %convert_element_type.32, f32[2048]{0:T(1024)S(1)} %bitcast.65, f32[2048]{0:T(1024)S(1)} %bitcast.68, f32[2048]{0:T(1024)S(1)} %bitcast.62, f32[2048]{0:T(1024)S(1)} %bitcast.71, f32[2048]{0:T(1024)S(1)} %get-tuple-element.10, s32[256]{0:T(256)S(1)} %and_select_fusion, ...), kind=kOutput, calls=%fused_computation.23 | convolution fusion | flops 1616379904 | bytes 8709120 | tf_op jit(solution)/shard_map/dot_general | solution.py:18
  53.1 8.8 %multiply_reduce_fusion.3 = (f32[2048]{0:T(1024)S(1)}, f32[2048]{0:T(1024)S(1)}, f32[2048]{0:T(1024)S(1)}, f32[2048]{0:T(1024)S(1)}, f32[2048,256]{1,0:T(8,128)}...) fusion(f32[2048,1024]{1,0:T(8,128)} %convert_element_type.32, f32[2048]{0:T(1024)S(1)} %get-tuple-element.29, ...), kind=kOutput, calls=%fused_computation.30 | convolution fusion | flops 276291584 | bytes 16991232 | tf_op jit(solution)/shard_map/dot_general | solution.py:114
  61.9 1.2 fusion.24
  63.1 0.9 copy.17
  64.1 7.4 %all-to-all-start.1 = ((f32[32,8,384]{2,1,0:T(8,128)}), f32[32,8,384]{2,1,0:T(8,128)S(1)}, u32[]{:S(2)}, u32[]{:S(2)}) async-start(f32[32,8,384]{2,1,0:T(8,128)} %bitcast.14), calls=%async_computation.1 | async-start | bytes 786432 | tf_op jit(solution)/shard_map/all_to_all | solution.py:43
  71.5 25.5 %scatter_custom_fusion = f32[4161,1024]{1,0:T(8,128)} fusion(s32[2048]{0:T(1024)S(1)} %bitcast.74, f32[]{:T(128)} %constant.54.clone.1, f32[2048,256]{1,0:T(8,128)} %get-tuple-element.13, f32[]{:T(128)} %constant.79, f32[2048,256]{1,0:T(8,128)} %get-tuple-element.14, f32[2048,256]{1,0:T(8,128)} %get-tuple-element.15, f32[2048,256]{1,0:T(8,128)} %get-tuple-element.16), kind=kCustom, calls=%fused_computation.3 | custom fusion | flops 8388608 | bytes 25432072 | tf_op jit(solution)/shard_map/scatter-add | solution.py:136
  97.0 7.0 %fusion.11 = bf16[4096,256]{1,0:T(8,128)(2,1)S(1)} fusion(f32[4161,1024]{1,0:T(8,128)} %scatter_custom_fusion), kind=kLoop, calls=%fused_computation.17 | loop fusion | flops 4194304 | bytes 18874368 | tf_op jit(solution)/shard_map/convert_element_type | solution.py:169
  104.0 0.0 copy-start.1
  104.0 1.3 copy-done.1
  105.4 0.0 copy-start.4
  105.4 0.0 copy-start.5
  105.4 0.7 fusion.30
  106.1 0.0 all-to-all-done.1
  106.2 0.0 copy-done.4
  106.2 0.3 fusion.57
  106.5 0.1 reshape.282
  106.6 1.2 fusion
  107.8 0.1 sub.31
  107.9 0.0 copy-done.5
  107.9 0.2 convolution_bitcast_fusion
  108.2 0.2 copy.18
  108.4 0.0 copy-start.2
  108.4 20.1 %all_to_all.25 = f32[32,8,640]{2,1,0:T(8,128)S(1)} all-to-all(f32[32,8,640]{2,1,0:T(8,128)S(1)} %bitcast.58), channel_id=1, replica_groups=mesh['tile'=16,'query'=2,'dp'=8] {'tile','query'}, dimensions={0} | all-to-all | bytes 1310720 | tf_op jit(solution)/shard_map/all_to_all | solution.py:43
  128.6 0.1 reduce_sum.98
  128.7 16.5 %all_to_all.26 = f32[8,8,640]{2,1,0:T(8,128)S(1)} all-to-all(f32[8,8,640]{2,1,0:T(8,128)S(1)} %broadcast_in_dim.43), channel_id=1, replica_groups=mesh['tile'=16,'query'=2,'dp'=8] {'dp'}, dimensions={0} | all-to-all | bytes 327680 | tf_op jit(solution)/shard_map/all_to_all | solution.py:50
  145.2 0.9 broadcast_in_dim.44
  146.1 5.9 %all-to-all-start.4 = ((f32[32,8,640]{2,1,0:T(8,128)}), f32[32,8,640]{2,1,0:T(8,128)S(1)}, u32[]{:S(2)}, u32[]{:S(2)}) async-start(f32[32,8,640]{2,1,0:T(8,128)} %broadcast_in_dim.44), calls=%async_computation.4 | async-start | bytes 1310720 | tf_op jit(solution)/shard_map/all_to_all | solution.py:36
  152.0 0.0 copy-done.2
  152.0 0.0 copy-start.3
  152.0 3.7 %fusion.10 = bf16[1,4096,256]{2,1,0:T(8,128)(2,1)} fusion(bf16[4096,256]{1,0:T(8,128)(2,1)} %copy-done.1, bf16[256,256]{1,0:T(8,128)(2,1)S(1)} %copy-done.2), kind=kOutput, calls=%fused_computation.15 | convolution fusion | flops 537919488 | bytes 4325376 | tf_op jit(solution)/shard_map/dot_general | solution.py:28
  155.7 0.0 copy-done.3
  155.7 0.7 fusion.33
  156.4 8.4 %all-to-all-done.4 = f32[32,8,640]{2,1,0:T(8,128)S(1)} async-done(((f32[32,8,640]{2,1,0:T(8,128)}), f32[32,8,640]{2,1,0:T(8,128)S(1)}, u32[]{:S(2)}, u32[]{:S(2)}) %all-to-all-start.4) | async-done | bytes 655392 | tf_op jit(solution)/shard_map/all_to_all | solution.py:36
  164.8 0.8 slice_multiply_fusion
  165.6 0.7 slice_multiply_fusion.2
  (16 shorter events, 0.3 us)
Async XLA Ops:
  0.6 13.5 %copy-start = (bf16[1,4096,256]{2,1,0:T(8,128)(2,1)S(1)}, bf16[1,4096,256]{2,1,0:T(8,128)(2,1)}, u32[]{:S(2)}) copy-start(bf16[1,4096,256]{2,1,0:T(8,128)(2,1)} %param.10) | copy-start | bytes 6291460
  3.9 39.8 %all-to-all-start = ((bf16[32,8,384]{2,1,0:T(8,128)(2,1)}), bf16[32,8,384]{2,1,0:T(8,128)(2,1)S(1)}, u32[]{:S(2)}, u32[]{:S(2)}) async-start(bf16[32,8,384]{2,1,0:T(8,128)(2,1)} %broadcast_in_dim.36), calls=%async_computation | async-start | bytes 393216 | tf_op jit(solution)/shard_map/all_to_all | solution.py:36
  37.3 6.5 %copy-start.6 = (s32[1,2048]{1,0:T(1,128)S(1)}, s32[1,2048]{1,0:T(1,128)}, u32[]{:S(2)}) copy-start(s32[1,2048]{1,0:T(1,128)} %param.16) | copy-start | bytes 24580
  64.1 42.0 %all-to-all-start.1 = ((f32[32,8,384]{2,1,0:T(8,128)}), f32[32,8,384]{2,1,0:T(8,128)S(1)}, u32[]{:S(2)}, u32[]{:S(2)}) async-start(f32[32,8,384]{2,1,0:T(8,128)} %bitcast.14), calls=%async_computation.1 | async-start | bytes 786432 | tf_op jit(solution)/shard_map/all_to_all | solution.py:43
  104.0 1.4 copy-start.1
  105.4 0.8 copy-start.4
  105.4 2.5 %copy-start.5 = (bf16[1,8,256]{2,1,0:T(8,128)(2,1)S(1)}, bf16[1,8,256]{2,1,0:T(8,128)(2,1)}, u32[]{:S(2)}) copy-start(bf16[1,8,256]{2,1,0:T(8,128)(2,1)} %param.11) | copy-start | bytes 12292
  108.4 43.5 %copy-start.2 = (bf16[256,256]{1,0:T(8,128)(2,1)S(1)}, bf16[256,256]{1,0:T(8,128)(2,1)}, u32[]{:S(2)}) copy-start(bf16[256,256]{1,0:T(8,128)(2,1)} %param.13) | copy-start | bytes 393220
  146.1 18.7 %all-to-all-start.4 = ((f32[32,8,640]{2,1,0:T(8,128)}), f32[32,8,640]{2,1,0:T(8,128)S(1)}, u32[]{:S(2)}, u32[]{:S(2)}) async-start(f32[32,8,640]{2,1,0:T(8,128)} %broadcast_in_dim.44), calls=%async_computation.4 | async-start | bytes 1310720 | tf_op jit(solution)/shard_map/all_to_all | solution.py:36
  152.0 3.7 %copy-start.3 = (bf16[256,128]{1,0:T(8,128)(2,1)S(1)}, bf16[256,128]{1,0:T(8,128)(2,1)}, u32[]{:S(2)}) copy-start(bf16[256,128]{1,0:T(8,128)(2,1)} %param.14) | copy-start | bytes 196612

commit v4 on v3

--- a/solution.py
+++ b/solution.py
@@ -90,10 +90,11 @@
     attn_rounded = attention.astype(jnp.bfloat16)
     sample_grad = times_transpose(out_grad[0], out_weight).astype(jnp.bfloat16)
     every_both = gather_rows(
-        jnp.concatenate([sample_grad, attn_rounded], axis=1), ("tile", "query")
+        jnp.concatenate([sample_grad, attn_rounded, out_grad[0]], axis=1), ("tile", "query")
     )
     every_grad = every_both[:, :width]
-    every_attn = every_both[:, width:]
+    every_attn = every_both[:, width : width + att_width]
+    every_out = every_both[:, width + att_width :]
     projected = jnp.dot(features[0], value_weight, preferred_element_type=jnp.float32).astype(
         jnp.bfloat16
     )
@@ -121,14 +122,13 @@
     base_row = slot_rows[0, 0]
     picked_all = row_major(corner_table[base_row]).astype(jnp.float32)
     mixed_rows = jnp.zeros((capacity, width), jnp.float32)
-    corner_dots = jnp.zeros((capacity,), jnp.float32)
     contributions = []
     for corner in range(4):
         bilinear = slot_bilinear[0, corner]
         picked = picked_all[:, corner * width : (corner + 1) * width]
         mixed_rows = mixed_rows + bilinear[:, None] * picked
-        corner_dots = corner_dots + bilinear * jnp.sum(picked * slot_grad, axis=1)
         contributions.append((weight * bilinear)[:, None] * slot_grad)
+    corner_dots = jnp.sum(mixed_rows * slot_grad, axis=1)
     margin = TILE_W + 1
     corner_sums = (
         jnp.zeros((token_count + margin, 4 * width), jnp.float32)
@@ -152,12 +152,8 @@
         jnp.zeros((), jnp.float32),
     )
     attn_part = over_rows_exact(query_float, dots_table)
-    shares = scatter_sum_rows(
-        jnp.concatenate([sampled_part, attn_part], axis=1), ("tile", "query")
-    )
-    sampled_share = shares[:, :width]
-    attn_grad = shares[:, width:]
-    out_term = over_rows_exact(sampled_share, out_grad[0].astype(jnp.float32))
+    attn_grad = scatter_sum_rows(attn_part, ("tile", "query"))
+    out_term = over_rows_exact(sampled_part, every_out.astype(jnp.float32))
     attn_three = attention.reshape(local_queries, HEADS, per_head)
     grad_three = attn_grad.reshape(local_queries, HEADS, per_head)
     logit_grad = (

time: 167 us -> 163 us (0.976)
  matrix products: 28.7 us -> 25.5 us
  local copies, waits for them, and re-layouts: 22.3 us -> 20.6 us
    dot_general x3, matrix products: 10.1 us -> 5.41 us  [over_rows_exact(): lax.dot_general(left, right, (((0,), (0,)), ((), ())), precision=lax.Prec...]
  transfers between devices with their start and end apart: 3 -> 3, of which waited for: 1 -> 1; matrix products, arithmetic and copies ran while one was open for 41% -> 42% of each run, Pallas kernels for 0% -> 0%
where the time goes in v4:
time: 163 us; the launch traced here: 162 us
  other arithmetic  47.5 us (29%)
  blocking collectives  36.7 us (23%)
  matrix products  25.5 us (16%)
  starting transfers between devices  21.8 us (13%)
  local copies, waits for them, and re-layouts  20.6 us (13%)
  waiting for transfers between devices  8.39 us (5%)
    scatter-add x1, other arithmetic, local(): corner_sums = jnp.zeros((token_count + margin, 4 * width), jnp.float32).a...  25.5 us
    all_to_all x1, blocking collectives, scatter_sum_rows(): return jnp.sum(lax.all_to_all(pieces, axes, 0, 0, tiled=True), axis=0)  20.1 us
    all_to_all x1, blocking collectives, sum_everywhere(): block = jnp.sum(lax.all_to_all(copies, 'dp', 0, 0, tiled=True), axis=0)  16.5 us
    gather x1, local copies, waits for them, and re-layouts, local(): picked_all = row_major(corner_table[base_row]).astype(jnp.float32)  15.5 us
    all_to_all x2, starting transfers between devices, gather_rows(): gathered = lax.all_to_all(copies, axes, 0, 0, tiled=True)  14.5 us
    dot_general x1, matrix products, local(): jnp.dot(query_onehot, every_grad, preferred_element_type=jnp.float32)  10.2 us
    all_to_all x2, waiting for transfers between devices, gather_rows(): gathered = lax.all_to_all(copies, axes, 0, 0, tiled=True)  8.39 us
    all_to_all x1, starting transfers between devices, scatter_sum_rows(): return jnp.sum(lax.all_to_all(pieces, axes, 0, 0, tiled=True), axis=0)  7.38 us
  transfers between devices with their start and end apart: 3, of which 1 were waited for; matrix products, arithmetic and copies ran while one was open for 42% of the time, Pallas kernels for 0%

profile of v4, /device:TPU:1, one launch (start us, length us, event | category | flops | bytes accessed | tf_op | source)
XLA Modules:
  0.0 162.0 jit_solution(12804724260575943941)
XLA Ops:
  0.6 0.0 copy-start
  0.6 1.1 convolution_exponential_fusion
  1.8 0.1 reshape.249
  1.9 0.1 reduce_sum.63
  1.9 0.1 div.48
  2.0 0.1 div.49
  2.1 1.1 convolution_convert_fusion.3
  3.2 0.7 pad_maximum_fusion.2
  3.9 0.8 broadcast_in_dim.36
  4.7 8.6 %all-to-all-start = ((bf16[32,8,640]{2,1,0:T(8,128)(2,1)}), bf16[32,8,640]{2,1,0:T(8,128)(2,1)S(1)}, u32[]{:S(2)}, u32[]{:S(2)}) async-start(bf16[32,8,640]{2,1,0:T(8,128)(2,1)} %broadcast_in_dim.36), calls=%async_computation | async-start | bytes 655360 | tf_op jit(solution)/shard_map/all_to_all | solution.py:36
  13.9 0.8 compare_select_fusion.2
  14.7 0.9 fusion.59
  15.7 0.0 copy-done
  15.7 1.6 convolution_convert_fusion
  17.3 1.3 pad_slice_fusion.2
  18.6 3.9 %pad_maximum_fusion = bf16[4096,1024]{1,0:T(8,128)(2,1)} fusion(bf16[4096,256]{1,0:T(8,128)(2,1)S(1)} %get-tuple-element.17, bf16[4096,256]{1,0:T(8,128)(2,1)S(1)} %get-tuple-element.16, bf16[4096,256]{1,0:T(8,128)(2,1)S(1)} %get-tuple-element.15, bf16[4096,256]{1,0:T(8,128)(2,1)S(1)} %convolution_convert_fusion), kind=kLoop, calls=%fused_computation.12 | loop fusion | flops 33554432 | bytes 16777216 | tf_op jit(solution)/shard_map/concatenate | solution.py:119
  22.5 15.5 %gather_fusion = bf16[2048,1024]{1,0:T(8,128)(2,1)} fusion(bf16[4096,1024]{1,0:T(8,128)(2,1)} %pad_maximum_fusion, s32[2048]{0:T(1024)S(1)} %broadcast_clamp_fusion), kind=kCustom, calls=%fused_computation | custom fusion | bytes 8396800 | tf_op jit(solution)/shard_map/gather | solution.py:123
  38.0 0.0 copy-start.5
  38.0 6.5 %convert_element_type.32 = f32[2048,1024]{1,0:T(8,128)} convert(bf16[2048,1024]{1,0:T(8,128)(2,1)} %gather_fusion) | non-fusion elementwise | flops 2097152 | bytes 12582912 | tf_op jit(solution)/shard_map/convert_element_type | solution.py:123
  44.5 0.0 copy-done.5
  44.5 0.0 all-to-all-done
  44.5 0.7 fusion.21
  45.2 10.2 %multiply_reduce_fusion = (f32[2048]{0:T(1024)S(1)}, f32[2048,256]{1,0:T(8,128)S(1)}, f32[2048,256]{1,0:T(8,128)}, f32[2048,256]{1,0:T(8,128)}, f32[2048,256]{1,0:T(8,128)}, /*index=5*/f32[2048,256]{1,0:T(8,128)}) fusion(f32[2048,1024]{1,0:T(8,128)} %convert_element_type.32, f32[2048]{0:T(1024)S(1)} %bitcast.65, f32[2048]{0:T(1024)S(1)} %bitcast.67, ...), kind=kOutput, calls=%fused_computation.35 | convolution fusion | flops 276822016 | bytes 19096576 | tf_op jit(solution)/shard_map/dot_general | solution.py:115
  55.4 2.7 %fusion.12 = f32[256,256]{1,0:T(8,128)S(1)} fusion(f32[2048,256]{1,0:T(8,128)S(1)} %get-tuple-element.6, f32[2048]{0:T(1024)S(1)} %get-tuple-element.8, s32[256]{0:T(256)S(1)} %and_select_fusion, s32[2048]{0:T(1024)S(1)} %get-tuple-element.31, s32[2048]{0:T(1024)S(1)} %get-tuple-element.30), kind=kOutput, calls=%fused_computation.23 | convolution fusion | flops 1612709888 | bytes 2384896 | tf_op jit(solution)/shard_map/dot_general | solution.py:18
  58.2 2.4 %convolution_bitcast_fusion.1 = f32[32,8,128]{2,1,0:T(8,128)} fusion(s32[2048]{0:T(1024)S(1)} %get-tuple-element.31, f32[2048]{0:T(1024)S(1)} %get-tuple-element.5, s32[2048]{0:T(1024)S(1)} %get-tuple-element.29, pred[2048]{0:T(1024)(128)(4,1)S(1)} %iota_compare_fusion.7), kind=kOutput, calls=%fused_computation.44 | convolution fusion | flops 807141376 | bytes 157696 | tf_op jit(solution)/shard_map/dot_general | solution.py:18
  60.6 7.4 %all-to-all-start.1 = ((f32[32,8,128]{2,1,0:T(8,128)}), f32[32,8,128]{2,1,0:T(8,128)S(1)}, u32[]{:S(2)}, u32[]{:S(2)}) async-start(f32[32,8,128]{2,1,0:T(8,128)} %convolution_bitcast_fusion.1), calls=%async_computation.1 | async-start | bytes 262144 | tf_op jit(solution)/shard_map/all_to_all | solution.py:43
  67.9 25.5 %scatter_custom_fusion = f32[4161,1024]{1,0:T(8,128)} fusion(s32[2048]{0:T(1024)S(1)} %bitcast.72, f32[]{:T(128)} %constant.54.clone.1, f32[2048,256]{1,0:T(8,128)} %get-tuple-element.11, f32[]{:T(128)} %constant.79, f32[2048,256]{1,0:T(8,128)} %get-tuple-element.12, f32[2048,256]{1,0:T(8,128)} %get-tuple-element.13, f32[2048,256]{1,0:T(8,128)} %get-tuple-element.14), kind=kCustom, calls=%fused_computation.3 | custom fusion | flops 8388608 | bytes 25432072 | tf_op jit(solution)/shard_map/scatter-add | solution.py:136
  93.4 7.0 %fusion.11 = bf16[4096,256]{1,0:T(8,128)(2,1)S(1)} fusion(f32[4161,1024]{1,0:T(8,128)} %scatter_custom_fusion), kind=kLoop, calls=%fused_computation.17 | loop fusion | flops 4194304 | bytes 18874368 | tf_op jit(solution)/shard_map/convert_element_type | solution.py:165
  100.5 0.0 copy-start.1
  100.5 0.0 copy-start.4
  100.5 0.7 fusion.22
  101.2 0.6 copy-done.1
  101.8 0.3 fusion.42
  102.2 0.0 all-to-all-done.1
  102.2 0.1 reshape.252
  102.3 1.2 fusion
  103.5 0.1 sub.31
  103.6 0.0 copy-done.4
  103.6 0.2 convolution_bitcast_fusion
  103.9 0.2 copy.16
  104.1 0.0 copy-start.2
  104.1 20.1 %all_to_all.25 = f32[32,8,640]{2,1,0:T(8,128)S(1)} all-to-all(f32[32,8,640]{2,1,0:T(8,128)S(1)} %bitcast.58), channel_id=1, replica_groups=mesh['tile'=16,'query'=2,'dp'=8] {'tile','query'}, dimensions={0} | all-to-all | bytes 1310720 | tf_op jit(solution)/shard_map/all_to_all | solution.py:43
  124.3 0.1 reduce_sum.68
  124.4 16.5 %all_to_all.26 = f32[8,8,640]{2,1,0:T(8,128)S(1)} all-to-all(f32[8,8,640]{2,1,0:T(8,128)S(1)} %broadcast_in_dim.43), channel_id=1, replica_groups=mesh['tile'=16,'query'=2,'dp'=8] {'dp'}, dimensions={0} | all-to-all | bytes 327680 | tf_op jit(solution)/shard_map/all_to_all | solution.py:50
  140.9 0.9 broadcast_in_dim.44
  141.8 5.9 %all-to-all-start.4 = ((f32[32,8,640]{2,1,0:T(8,128)}), f32[32,8,640]{2,1,0:T(8,128)S(1)}, u32[]{:S(2)}, u32[]{:S(2)}) async-start(f32[32,8,640]{2,1,0:T(8,128)} %broadcast_in_dim.44), calls=%async_computation.4 | async-start | bytes 1310720 | tf_op jit(solution)/shard_map/all_to_all | solution.py:36
  147.7 0.0 copy-done.2
  147.7 0.0 copy-start.3
  147.7 3.7 %fusion.10 = bf16[1,4096,256]{2,1,0:T(8,128)(2,1)} fusion(bf16[4096,256]{1,0:T(8,128)(2,1)} %copy-done.1, bf16[256,256]{1,0:T(8,128)(2,1)S(1)} %copy-done.2), kind=kOutput, calls=%fused_computation.15 | convolution fusion | flops 537919488 | bytes 4325376 | tf_op jit(solution)/shard_map/dot_general | solution.py:28
  151.4 0.0 copy-done.3
  151.4 0.7 fusion.25
  152.1 8.4 %all-to-all-done.4 = f32[32,8,640]{2,1,0:T(8,128)S(1)} async-done(((f32[32,8,640]{2,1,0:T(8,128)}), f32[32,8,640]{2,1,0:T(8,128)S(1)}, u32[]{:S(2)}, u32[]{:S(2)}) %all-to-all-start.4) | async-done | bytes 655392 | tf_op jit(solution)/shard_map/all_to_all | solution.py:36
  160.5 0.7 slice_multiply_fusion.6
  161.2 0.8 slice_multiply_fusion.4
  (12 shorter events, 0.2 us)
Async XLA Ops:
  0.6 15.0 %copy-start = (bf16[1,4096,256]{2,1,0:T(8,128)(2,1)S(1)}, bf16[1,4096,256]{2,1,0:T(8,128)(2,1)}, u32[]{:S(2)}) copy-start(bf16[1,4096,256]{2,1,0:T(8,128)(2,1)} %param.10) | copy-start | bytes 6291460
  4.7 39.8 %all-to-all-start = ((bf16[32,8,640]{2,1,0:T(8,128)(2,1)}), bf16[32,8,640]{2,1,0:T(8,128)(2,1)S(1)}, u32[]{:S(2)}, u32[]{:S(2)}) async-start(bf16[32,8,640]{2,1,0:T(8,128)(2,1)} %broadcast_in_dim.36), calls=%async_computation | async-start | bytes 655360 | tf_op jit(solution)/shard_map/all_to_all | solution.py:36
  38.0 6.5 %copy-start.5 = (s32[1,2048]{1,0:T(1,128)S(1)}, s32[1,2048]{1,0:T(1,128)}, u32[]{:S(2)}) copy-start(s32[1,2048]{1,0:T(1,128)} %param.16) | copy-start | bytes 24580
  60.6 41.6 %all-to-all-start.1 = ((f32[32,8,128]{2,1,0:T(8,128)}), f32[32,8,128]{2,1,0:T(8,128)S(1)}, u32[]{:S(2)}, u32[]{:S(2)}) async-start(f32[32,8,128]{2,1,0:T(8,128)} %convolution_bitcast_fusion.1), calls=%async_computation.1 | async-start | bytes 262144 | tf_op jit(solution)/shard_map/all_to_all | solution.py:43
  100.5 1.4 copy-start.1
  100.5 3.1 %copy-start.4 = (bf16[1,8,256]{2,1,0:T(8,128)(2,1)S(1)}, bf16[1,8,256]{2,1,0:T(8,128)(2,1)}, u32[]{:S(2)}) copy-start(bf16[1,8,256]{2,1,0:T(8,128)(2,1)} %param.11) | copy-start | bytes 12292
  104.1 43.6 %copy-start.2 = (bf16[256,256]{1,0:T(8,128)(2,1)S(1)}, bf16[256,256]{1,0:T(8,128)(2,1)}, u32[]{:S(2)}) copy-start(bf16[256,256]{1,0:T(8,128)(2,1)} %param.13) | copy-start | bytes 393220
  141.8 18.7 %all-to-all-start.4 = ((f32[32,8,640]{2,1,0:T(8,128)}), f32[32,8,640]{2,1,0:T(8,128)S(1)}, u32[]{:S(2)}, u32[]{:S(2)}) async-start(f32[32,8,640]{2,1,0:T(8,128)} %broadcast_in_dim.44), calls=%async_computation.4 | async-start | bytes 1310720 | tf_op jit(solution)/shard_map/all_to_all | solution.py:36
  147.7 3.7 %copy-start.3 = (bf16[256,128]{1,0:T(8,128)(2,1)S(1)}, bf16[256,128]{1,0:T(8,128)(2,1)}, u32[]{:S(2)}) copy-start(bf16[256,128]{1,0:T(8,128)(2,1)} %param.14) | copy-start | bytes 196612

commit v5 on v4

--- a/solution.py
+++ b/solution.py
@@ -51,7 +51,7 @@
     return gather_rows(block, ("tile", "query"))
 
 def row_major(block):
-    return with_layout_constraint(block, Layout(major_to_minor=(0, 1)))
+    return with_layout_constraint(block, Layout(major_to_minor=tuple(range(block.ndim))))
 
 
 def shift_down(block, offset):
@@ -113,35 +113,48 @@
     weight = jnp.where(alive_slot, picked_attn, jnp.zeros((), jnp.float32))
     head_mask = jnp.arange(width, dtype=jnp.int32)[None, :] // head_width == head_index[:, None]
     grad_rows = jnp.dot(query_onehot, every_grad, preferred_element_type=jnp.float32)
-    slot_grad = row_major(jnp.where(head_mask, grad_rows, jnp.zeros((), jnp.float32)))
+    head_grad = jnp.zeros((capacity, head_width), jnp.float32)
+    for head in range(HEADS):
+        head_grad = jnp.where(
+            (head_index == head)[:, None],
+            grad_rows[:, head * head_width : (head + 1) * head_width],
+            head_grad,
+        )
+    lanes = 4 * head_width
+    grad_lanes = row_major(jnp.tile(head_grad, (1, 4)))
     offsets = (0, 1, TILE_W, TILE_W + 1)
     padded = jnp.concatenate([projected, jnp.zeros((TILE_W + 1, width), jnp.bfloat16)], axis=0)
-    corner_table = jnp.concatenate(
-        [padded[offset : offset + token_count] for offset in offsets], axis=1
-    )
+    corner_table = row_major(
+        jnp.stack([padded[offset : offset + token_count] for offset in offsets], axis=1)
+        .reshape(token_count, 4, HEADS, head_width)
+        .transpose(0, 2, 1, 3)
+        .reshape(token_count, HEADS, lanes)
+    ).reshape(token_count * HEADS, lanes)
     base_row = slot_rows[0, 0]
-    picked_all = row_major(corner_table[base_row]).astype(jnp.float32)
-    mixed_rows = jnp.zeros((capacity, width), jnp.float32)
-    contributions = []
+    picked = row_major(corner_table[base_row * HEADS + head_index]).astype(jnp.float32)
+    bilinear_lanes = row_major(jnp.repeat(slot_bilinear[0].T, head_width, axis=1))
+    weighted = picked * bilinear_lanes
+    mixed_head = weighted[:, 0:head_width]
+    for corner in range(1, 4):
+        mixed_head = mixed_head + weighted[:, corner * head_width : (corner + 1) * head_width]
+    corner_dots = jnp.sum(mixed_head * head_grad, axis=1)
+    contributions = row_major((weight[:, None] * bilinear_lanes) * grad_lanes)
+    margin = TILE_W + 1
+    corner_sums = row_major(
+        jnp.zeros(((token_count + margin) * HEADS, lanes), jnp.float32)
+        .at[(base_row + margin) * HEADS + head_index]
+        .add(contributions)
+        .reshape(token_count + margin, HEADS, lanes)
+    )
+    value_grad = None
     for corner in range(4):
-        bilinear = slot_bilinear[0, corner]
-        picked = picked_all[:, corner * width : (corner + 1) * width]
-        mixed_rows = mixed_rows + bilinear[:, None] * picked
-        contributions.append((weight * bilinear)[:, None] * slot_grad)
-    corner_dots = jnp.sum(mixed_rows * slot_grad, axis=1)
-    margin = TILE_W + 1
-    corner_sums = (
-        jnp.zeros((token_count + margin, 4 * width), jnp.float32)
-        .at[base_row + margin]
-        .add(row_major(jnp.concatenate(contributions, axis=1)))
-    )
-    value_grad = corner_sums[margin : margin + token_count, 0:width]
-    for corner in range(1, 4):
         start = margin - offsets[corner]
-        value_grad = (
-            value_grad
-            + corner_sums[start : start + token_count, corner * width : (corner + 1) * width]
-        )
+        block = corner_sums[
+            start : start + token_count, :, corner * head_width : (corner + 1) * head_width
+        ].reshape(token_count, width)
+        value_grad = block if value_grad is None else value_grad + block
+    value_grad = row_major(value_grad)
+    mixed_rows = jnp.tile(mixed_head, (1, HEADS))
     query_float = query_match.astype(jnp.float32)
     sampled_part = over_rows_exact(
         query_float, jnp.where(head_mask, weight[:, None] * mixed_rows, jnp.zeros((), jnp.float32))

time: 163 us -> 241 us (1.48)
  local copies, waits for them, and re-layouts: 20.6 us -> 77.7 us
  other arithmetic: 47.5 us -> 75 us
  matrix products: 25.5 us -> 17.8 us
    add x0 -> x1, other arithmetic: none -> 27.2 us  [local(): value_grad = block if value_grad is None else value_grad + block]
    add x0 -> x3, local copies, waits for them, and re-layouts: none -> 14.4 us  [the longest x2 13.4 us: local(): value_grad = block if value_grad is None else value_grad + block]
    slice x1 -> x4, local copies, waits for them, and re-layouts: 1.3 us -> 15.3 us  [local(): padded[offset:offset + token_count]]
    convert_element_type x2 -> x0, other arithmetic: 13.5 us -> none  [the longest x1 7.05 us: local(): value_rounded = value_grad.astype(jnp.bfloat16)]
    reshape x0 -> x2, local copies, waits for them, and re-layouts: none -> 13.4 us  [the longest x1 12.1 us: local(): corner_table = row_major(jnp.stack([padded[offset:offset + token_count] f...]
    dot_general x1, matrix products: 10.2 us -> 0.49 us  [local(): jnp.dot(query_onehot, every_grad, preferred_element_type=jnp.float32)]
    transpose x0 -> x1, local copies, waits for them, and re-layouts: none -> 7.7 us  [local(): corner_table = row_major(jnp.stack([padded[offset:offset + token_count] f...]
    reduce_sum x0 -> x1, other arithmetic: none -> 7.53 us  [local(): corner_dots = jnp.sum(mixed_head * head_grad, axis=1)]
  transfers between devices with their start and end apart: 3 -> 3, of which waited for: 1 -> 1; matrix products, arithmetic and copies ran while one was open for 42% -> 62% of each run, Pallas kernels for 0% -> 0%
where the time goes in v5:
time: 241 us; the launch traced here: 239 us
  local copies, waits for them, and re-layouts  77.7 us (32%)
  other arithmetic  75 us (31%)
  blocking collectives  36.7 us (15%)
  starting transfers between devices  21.9 us (9%)
  matrix products  17.8 us (7%)
  waiting for transfers between devices  8.39 us (3%)
    add x1, other arithmetic, local(): value_grad = block if value_grad is None else value_grad + block  27.2 us
    all_to_all x1, blocking collectives, scatter_sum_rows(): return jnp.sum(lax.all_to_all(pieces, axes, 0, 0, tiled=True), axis=0)  20.1 us
    scatter-add x1, other arithmetic, local(): corner_sums = row_major(jnp.zeros(((token_count + margin) * HEADS, lanes)...  19.7 us
    all_to_all x1, blocking collectives, sum_everywhere(): block = jnp.sum(lax.all_to_all(copies, 'dp', 0, 0, tiled=True), axis=0)  16.5 us
    slice x4, local copies, waits for them, and re-layouts, local(): padded[offset:offset + token_count]  15.3 us
    all_to_all x2, starting transfers between devices, gather_rows(): gathered = lax.all_to_all(copies, axes, 0, 0, tiled=True)  14.5 us
    add x2, local copies, waits for them, and re-layouts, local(): value_grad = block if value_grad is None else value_grad + block  13.4 us
    gather x1, local copies, waits for them, and re-layouts, local(): corner_table[base_row * HEADS + head_index]  12.1 us
  transfers between devices with their start and end apart: 3, of which 1 were waited for; matrix products, arithmetic and copies ran while one was open for 62% of the time, Pallas kernels for 0%

profile of v5, /device:TPU:1, one launch (start us, length us, event | category | flops | bytes accessed | tf_op | source)
XLA Modules:
  0.0 239.0 jit_solution(18217187545951029639)
XLA Ops:
  0.6 1.1 convolution_exponential_fusion
  1.8 0.1 reshape.387
  1.9 0.1 reduce_sum.63
  1.9 0.1 div.60
  2.0 0.1 div.61
  2.1 0.6 fusion.60
  2.7 1.1 convolution_convert_fusion.3
  3.8 0.7 pad_maximum_fusion.1
  4.5 0.8 broadcast_in_dim.122
  5.3 8.6 %all-to-all-start = ((bf16[32,8,640]{2,1,0:T(8,128)(2,1)}), bf16[32,8,640]{2,1,0:T(8,128)(2,1)S(1)}, u32[]{:S(2)}, u32[]{:S(2)}) async-start(bf16[32,8,640]{2,1,0:T(8,128)(2,1)} %broadcast_in_dim.122), calls=%async_computation | async-start | bytes 655360 | tf_op jit(solution)/shard_map/all_to_all | solution.py:36
  13.9 1.6 convolution_convert_fusion
  15.5 1.3 copy-done.1
  16.8 3.0 %pad_slice_fusion.2 = (bf16[4096,256]{1,0:T(8,128)(2,1)}, bf16[4096,256]{1,0:T(8,128)(2,1)}, bf16[4096,256]{1,0:T(8,128)(2,1)}) fusion(bf16[4096,256]{1,0:T(8,128)(2,1)S(1)} %convolution_convert_fusion), kind=kLoop, calls=%fused_computation.23 | loop fusion | bytes 8388608 | tf_op jit(solution)/shard_map/slice | solution.py:128
  19.8 4.1 %copy.62 = bf16[4096,256]{0,1:T(8,128)(2,1)} copy(bf16[4096,256]{1,0:T(8,128)(2,1)} %copy-done.1) | data formatting | bytes 4194304 | tf_op jit(solution)/shard_map/convert_element_type | solution.py:98
  23.9 4.1 %copy.63 = bf16[4096,256]{0,1:T(8,128)(2,1)} copy(bf16[4096,256]{1,0:T(8,128)(2,1)} %get-tuple-element.14) | data formatting | bytes 4194304 | tf_op jit(solution)/shard_map/slice | solution.py:128
  28.1 4.1 %copy.64 = bf16[4096,256]{0,1:T(8,128)(2,1)} copy(bf16[4096,256]{1,0:T(8,128)(2,1)} %get-tuple-element.15) | data formatting | bytes 4194304 | tf_op jit(solution)/shard_map/slice | solution.py:128
  32.2 4.1 %copy.65 = bf16[4096,256]{0,1:T(8,128)(2,1)} copy(bf16[4096,256]{1,0:T(8,128)(2,1)} %get-tuple-element.16) | data formatting | bytes 4194304 | tf_op jit(solution)/shard_map/slice | solution.py:128
  36.2 7.1 %maximum_bitcast_fusion = bf16[4096,8,4,32]{0,3,1,2:T(8,128)(2,1)} fusion(bf16[4096,1,8,32]{0,3,2,1:T(8,128)(2,1)} %bitcast.84, bf16[4096,1,8,32]{0,3,2,1:T(8,128)(2,1)} %bitcast.83, bf16[4096,1,8,32]{0,3,2,1:T(8,128)(2,1)} %bitcast.82, bf16[4096,1,8,32]{0,3,2,1:T(8,128)(2,1)} %bitcast.81), kind=kLoop, calls=%fused_computation.8 | loop fusion | flops 12582912 | bytes 16777216 | tf_op jit(solution)/shard_map/transpose | solution.py:130
  43.4 7.7 %copy.66 = bf16[4096,8,4,32]{0,3,2,1:T(8,128)(2,1)} copy(bf16[4096,8,4,32]{0,3,1,2:T(8,128)(2,1)} %maximum_bitcast_fusion) | data formatting | bytes 16777216 | tf_op jit(solution)/shard_map/transpose | solution.py:130
  51.1 12.1 %copy.67 = bf16[4096,8,128]{2,1,0:T(8,128)(2,1)} copy(bf16[4096,8,128]{0,2,1:T(8,128)(2,1)} %bitcast.78) | data formatting | bytes 16777216 | tf_op jit(solution)/shard_map/reshape | solution.py:131
  63.2 1.4 compare_select_fusion
  64.6 0.1 broadcast_in_dim.125
  64.7 1.3 copy.49
  66.0 0.6 broadcast_compare_fusion.5
  66.6 0.6 broadcast_compare_fusion.3
  67.9 0.6 iota_compare_fusion.6
  68.5 0.8 compare_select_fusion.1
  69.3 12.1 %gather_fusion = bf16[2048,128]{1,0:T(8,128)(2,1)} fusion(bf16[32768,128]{1,0:T(8,128)(2,1)} %bitcast.79, s32[2048]{0:T(1024)S(1)} %broadcast_clamp_fusion), kind=kCustom, calls=%fused_computation | custom fusion | bytes 1056768 | tf_op jit(solution)/shard_map/gather | solution.py:134
  81.3 1.4 convert_multiply_fusion
  82.8 0.6 and_select_fusion.2
  83.4 0.5 fusion.9
  83.9 0.7 fusion.14
  84.6 7.5 %multiply_reduce_fusion = (f32[2048]{0:T(1024)S(1)}, f32[2048,32]{1,0:T(8,128)}, f32[2048,32]{1,0:T(8,128)}) fusion(f32[2048,128]{1,0:T(8,128)S(1)} %convert_multiply_fusion, f32[2048,256]{1,0:T(8,128)S(1)} %fusion.9, pred[2048]{0:T(1024)(128)(4,1)} %get-tuple-element.22, pred[2048]{0:T(1024)(128)(4,1)} %get-tuple-element.23, ...), kind=kLoop, calls=%fused_computation.46 | loop fusion | flops 849920 | bytes 3694592 | tf_op jit(solution)/shard_map/reduce_sum | solution.py:140
  92.1 2.4 %fusion.18 = f32[32,8,128]{2,1,0:T(8,128)} fusion(s32[2048]{0:T(1024)S(1)} %get-tuple-element.20, f32[2048]{0:T(1024)S(1)} %get-tuple-element.5, s32[2048]{0:T(1024)S(1)} %get-tuple-element.19, pred[2048]{0:T(1024)(128)(4,1)S(1)} %copy-done.14), kind=kOutput, calls=%fused_computation.29 | convolution fusion | flops 807141376 | bytes 157696 | tf_op jit(solution)/shard_map/dot_general | solution.py:18
  94.5 7.4 %all-to-all-start.1 = ((f32[32,8,128]{2,1,0:T(8,128)}), f32[32,8,128]{2,1,0:T(8,128)}, u32[]{:S(2)}, u32[]{:S(2)}) async-start(f32[32,8,128]{2,1,0:T(8,128)} %fusion.18), calls=%async_computation.1 | async-start | bytes 262144 | tf_op jit(solution)/shard_map/all_to_all | solution.py:43
  102.0 1.0 copy.68
  103.0 1.2 fusion.4
  104.2 2.5 %fusion.10 = f32[256,256]{1,0:T(8,128)} fusion(f32[2048,256]{0,1:T(8,128)S(1)} %fusion.4, s32[2048]{0:T(1024)S(1)} %get-tuple-element.20), kind=kOutput, calls=%fused_computation.24 | convolution fusion | flops 1611661312 | bytes 2367488 | tf_op jit(solution)/shard_map/dot_general | solution.py:18
  106.6 2.3 copy.58
  109.0 2.0 tile.8
  111.0 2.6 %copy.59 = f32[2048,128]{1,0:T(8,128)} copy(f32[2048,128]{0,1:T(8,128)} %bitcast.85) | data formatting | bytes 2097152 | tf_op jit(solution)/shard_map/tile | solution.py:124
  113.5 19.7 %scatter_custom_fusion = f32[33288,128]{1,0:T(8,128)} fusion(s32[2048]{0:T(1024)S(1)} %bitcast.98, f32[]{:T(128)} %constant.62.clone.1, f32[2048,128]{1,0:T(8,128)} %copy.59, f32[2048,128]{1,0:T(8,128)S(1)} %copy-done.2, f32[2048]{0:T(1024)S(1)} %broadcast_select_fusion), kind=kCustom, calls=%fused_computation.6 | custom fusion | flops 786432 | bytes 19148804 | tf_op jit(solution)/shard_map/scatter-add | solution.py:146
  133.3 27.2 %slice_add_fusion = bf16[4096,8,32]{2,1,0:T(8,128)(2,1)} fusion(f32[4161,8,128]{2,1,0:T(8,128)} %bitcast.77), kind=kLoop, calls=%fused_computation.3 | loop fusion | flops 4194304 | bytes 18874368 | tf_op jit(solution)/shard_map/add | solution.py:155
  160.5 9.3 %copy.60 = bf16[4096,8,32]{0,2,1:T(8,128)(2,1)} copy(bf16[4096,8,32]{2,1,0:T(8,128)(2,1)} %slice_add_fusion) | data formatting | bytes 4194304 | tf_op jit(solution)/shard_map/add | solution.py:155
  169.8 4.1 %copy.61 = bf16[4096,256]{1,0:T(8,128)(2,1)} copy(bf16[4096,256]{0,1:T(8,128)(2,1)} %bitcast.80) | data formatting | bytes 4194304 | tf_op jit(solution)/shard_map/add | solution.py:155
  173.9 3.1 %fusion.15 = f32[256,256]{0,1:T(8,128)} fusion(bf16[1,4096,256]{2,1,0:T(8,128)(2,1)S(1)} %copy-done, bf16[4096,256]{1,0:T(8,128)(2,1)} %copy.61), kind=kOutput, calls=%fused_computation.27 | convolution fusion | flops 536870912 | bytes 4456448 | tf_op jit(solution)/shard_map/dot_general | solution.py:12
  176.9 0.3 fusion.45
  177.3 0.9 reduce_sum.66
  178.2 0.1 reshape.394
  178.3 1.2 fusion
  179.5 0.1 sub.33
  179.6 0.2 convolution_bitcast_fusion
  179.9 1.0 pad_maximum_fusion
  180.9 0.2 copy.69
  181.1 20.1 %all_to_all.25 = f32[32,8,640]{2,1,0:T(8,128)S(1)} all-to-all(f32[32,8,640]{2,1,0:T(8,128)S(1)} %bitcast.89), channel_id=1, replica_groups=mesh['tile'=16,'query'=2,'dp'=8] {'tile','query'}, dimensions={0} | all-to-all | bytes 1310720 | tf_op jit(solution)/shard_map/all_to_all | solution.py:43
  201.3 0.1 reduce_sum.68
  201.3 16.5 %all_to_all.26 = f32[8,8,640]{2,1,0:T(8,128)S(1)} all-to-all(f32[8,8,640]{2,1,0:T(8,128)S(1)} %broadcast_in_dim.139), channel_id=1, replica_groups=mesh['tile'=16,'query'=2,'dp'=8] {'dp'}, dimensions={0} | all-to-all | bytes 327680 | tf_op jit(solution)/shard_map/all_to_all | solution.py:50
  217.9 0.9 broadcast_in_dim.140
  218.8 5.9 %all-to-all-start.4 = ((f32[32,8,640]{2,1,0:T(8,128)}), f32[32,8,640]{2,1,0:T(8,128)S(1)}, u32[]{:S(2)}, u32[]{:S(2)}) async-start(f32[32,8,640]{2,1,0:T(8,128)} %broadcast_in_dim.140), calls=%async_computation.4 | async-start | bytes 1310720 | tf_op jit(solution)/shard_map/all_to_all | solution.py:36
  224.7 3.7 %fusion.3 = bf16[1,4096,256]{2,1,0:T(8,128)(2,1)} fusion(bf16[256,256]{1,0:T(8,128)(2,1)S(1)} %copy-done.5, bf16[4096,256]{1,0:T(8,128)(2,1)} %copy.61), kind=kOutput, calls=%fused_computation.11 | convolution fusion | flops 537919488 | bytes 4325376 | tf_op jit(solution)/shard_map/dot_general | solution.py:28
  228.4 0.7 fusion.21
  229.1 8.4 %all-to-all-done.4 = f32[32,8,640]{2,1,0:T(8,128)S(1)} async-done(((f32[32,8,640]{2,1,0:T(8,128)}), f32[32,8,640]{2,1,0:T(8,128)S(1)}, u32[]{:S(2)}, u32[]{:S(2)}) %all-to-all-start.4) | async-done | bytes 655392 | tf_op jit(solution)/shard_map/all_to_all | solution.py:36
  237.5 0.8 slice_multiply_fusion
  238.3 0.7 slice_multiply_fusion.2
  (37 shorter events, 0.2 us)
Async XLA Ops:
  0.6 13.2 %copy-start = (bf16[1,4096,256]{2,1,0:T(8,128)(2,1)S(1)}, bf16[1,4096,256]{2,1,0:T(8,128)(2,1)}, u32[]{:S(2)}) copy-start(bf16[1,4096,256]{2,1,0:T(8,128)(2,1)} %param.10) | copy-start | bytes 6291460
  1.9 13.5 %copy-start.11 = (f32[8,8]{1,0:T(8,128)}, f32[8,8]{1,0:T(8,128)S(1)}, u32[]{:S(2)}) copy-start(f32[8,8]{1,0:T(8,128)S(1)} %reduce_sum.63) | copy-start | bytes 772
  5.3 78.1 %all-to-all-start = ((bf16[32,8,640]{2,1,0:T(8,128)(2,1)}), bf16[32,8,640]{2,1,0:T(8,128)(2,1)S(1)}, u32[]{:S(2)}, u32[]{:S(2)}) async-start(bf16[32,8,640]{2,1,0:T(8,128)(2,1)} %broadcast_in_dim.122), calls=%async_computation | async-start | bytes 655360 | tf_op jit(solution)/shard_map/all_to_all | solution.py:36
  15.5 1.3 copy-start.1
  51.1 12.1 %copy-start.7 = (s32[1,2048]{1,0:T(1,128)S(1)}, s32[1,2048]{1,0:T(1,128)}, u32[]{:S(2)}) copy-start(s32[1,2048]{1,0:T(1,128)} %param.16) | copy-start | bytes 24580
  51.1 13.5 %copy-start.8 = (f32[1,4,2048]{2,1,0:T(4,128)S(1)}, f32[1,4,2048]{2,1,0:T(4,128)}, u32[]{:S(2)}) copy-start(f32[1,4,2048]{2,1,0:T(4,128)} %param.18) | copy-start | bytes 98308
  64.7 3.8 %copy-start.9 = (s32[2048,1]{0,1:T(1,128)S(1)}, s32[2048,1]{0,1:T(1,128)}, u32[]{:S(2)}) copy-start(s32[2048,1]{0,1:T(1,128)} %get-tuple-element.9) | copy-start | bytes 24580
  84.6 7.5 %copy-start.14 = (pred[2048]{0:T(1024)(128)(4,1)S(1)}, pred[2048]{0:T(1024)(128)(4,1)}, u32[]{:S(2)}) copy-start(pred[2048]{0:T(1024)(128)(4,1)} %iota_compare_fusion.6) | copy-start | bytes 6148
  92.1 9.9 %copy-start.3 = (f32[2048,32]{1,0:T(8,128)S(1)}, f32[2048,32]{1,0:T(8,128)}, u32[]{:S(2)}) copy-start(f32[2048,32]{1,0:T(8,128)} %get-tuple-element.6) | copy-start | bytes 786436
  94.5 82.8 %all-to-all-start.1 = ((f32[32,8,128]{2,1,0:T(8,128)}), f32[32,8,128]{2,1,0:T(8,128)}, u32[]{:S(2)}, u32[]{:S(2)}) async-start(f32[32,8,128]{2,1,0:T(8,128)} %fusion.18), calls=%async_computation.1 | async-start | bytes 262144 | tf_op jit(solution)/shard_map/all_to_all | solution.py:43
  106.6 6.9 %copy-start.2 = (f32[2048,128]{1,0:T(8,128)S(1)}, f32[2048,128]{1,0:T(8,128)}, u32[]{:S(2)}) copy-start(f32[2048,128]{1,0:T(8,128)} %copy.49) | copy-start | bytes 3145732
  173.9 3.1 %copy-start.4 = (f32[256,256]{1,0:T(8,128)S(1)}, f32[256,256]{1,0:T(8,128)}, u32[]{:S(2)}) copy-start(f32[256,256]{1,0:T(8,128)} %fusion.10) | copy-start | bytes 786436
  173.9 4.4 %copy-start.12 = (f32[8,8]{1,0:T(8,128)S(1)}, f32[8,8]{1,0:T(8,128)}, u32[]{:S(2)}) copy-start(f32[8,8]{1,0:T(8,128)} %copy-done.11) | copy-start | bytes 772
  173.9 5.7 %copy-start.13 = (f32[8,128]{1,0:T(8,128)S(1)}, f32[8,128]{1,0:T(8,128)}, u32[]{:S(2)}) copy-start(f32[8,128]{1,0:T(8,128)} %get-tuple-element.13) | copy-start | bytes 12292
  173.9 5.8 %copy-start.10 = (bf16[1,8,256]{2,1,0:T(8,128)(2,1)S(1)}, bf16[1,8,256]{2,1,0:T(8,128)(2,1)}, u32[]{:S(2)}) copy-start(bf16[1,8,256]{2,1,0:T(8,128)(2,1)} %param.11) | copy-start | bytes 12292
  181.1 43.6 %copy-start.5 = (bf16[256,256]{1,0:T(8,128)(2,1)S(1)}, bf16[256,256]{1,0:T(8,128)(2,1)}, u32[]{:S(2)}) copy-start(bf16[256,256]{1,0:T(8,128)(2,1)} %param.13) | copy-start | bytes 393220
  218.8 18.7 %all-to-all-start.4 = ((f32[32,8,640]{2,1,0:T(8,128)}), f32[32,8,640]{2,1,0:T(8,128)S(1)}, u32[]{:S(2)}, u32[]{:S(2)}) async-start(f32[32,8,640]{2,1,0:T(8,128)} %broadcast_in_dim.140), calls=%async_computation.4 | async-start | bytes 1310720 | tf_op jit(solution)/shard_map/all_to_all | solution.py:36
  224.7 3.7 %copy-start.6 = (bf16[256,128]{1,0:T(8,128)(2,1)S(1)}, bf16[256,128]{1,0:T(8,128)(2,1)}, u32[]{:S(2)}) copy-start(bf16[256,128]{1,0:T(8,128)(2,1)} %param.14) | copy-start | bytes 196612

commit v6 on v4

--- a/solution.py
+++ b/solution.py
@@ -44,7 +44,6 @@
 
 
 def sum_everywhere(block):
-    block = scatter_sum_rows(block, ("tile", "query"))
     count = lax.axis_size("dp")
     copies = jnp.broadcast_to(block[None], (count,) + block.shape)
     block = jnp.sum(lax.all_to_all(copies, "dp", 0, 0, tiled=True), axis=0)
@@ -90,11 +89,13 @@
     attn_rounded = attention.astype(jnp.bfloat16)
     sample_grad = times_transpose(out_grad[0], out_weight).astype(jnp.bfloat16)
     every_both = gather_rows(
-        jnp.concatenate([sample_grad, attn_rounded, out_grad[0]], axis=1), ("tile", "query")
+        jnp.concatenate([sample_grad, attn_rounded, out_grad[0], queries[0]], axis=1),
+        ("tile", "query"),
     )
     every_grad = every_both[:, :width]
     every_attn = every_both[:, width : width + att_width]
-    every_out = every_both[:, width + att_width :]
+    every_out = every_both[:, width + att_width : 2 * width + att_width]
+    every_queries = every_both[:, 2 * width + att_width :]
     projected = jnp.dot(features[0], value_weight, preferred_element_type=jnp.float32).astype(
         jnp.bfloat16
     )
@@ -142,6 +143,8 @@
             value_grad
             + corner_sums[start : start + token_count, corner * width : (corner + 1) * width]
         )
+    value_rounded = value_grad.astype(jnp.bfloat16)
+    value_term = over_rows(features[0], value_rounded)
     query_float = query_match.astype(jnp.float32)
     sampled_part = over_rows_exact(
         query_float, jnp.where(head_mask, weight[:, None] * mixed_rows, jnp.zeros((), jnp.float32))
@@ -152,8 +155,20 @@
         jnp.zeros((), jnp.float32),
     )
     attn_part = over_rows_exact(query_float, dots_table)
-    attn_grad = scatter_sum_rows(attn_part, ("tile", "query"))
     out_term = over_rows_exact(sampled_part, every_out.astype(jnp.float32))
+    page_exponent = jnp.exp(
+        jnp.dot(every_queries, attn_weight, preferred_element_type=jnp.float32)
+    ).reshape(all_queries, HEADS, per_head)
+    page_attention = page_exponent / jnp.sum(page_exponent, axis=2, keepdims=True)
+    part_three = attn_part.reshape(all_queries, HEADS, per_head)
+    part_logits = (
+        page_attention
+        * (part_three - jnp.sum(page_attention * part_three, axis=2, keepdims=True))
+    ).reshape(all_queries, att_width)
+    attn_term = over_rows_exact(every_queries.astype(jnp.float32), part_logits)
+    terms = jnp.concatenate([value_term, attn_term, out_term], axis=1)
+    shares = scatter_sum_rows(jnp.concatenate([terms, attn_part], axis=1), ("tile", "query"))
+    attn_grad = shares[:, terms.shape[1] :]
     attn_three = attention.reshape(local_queries, HEADS, per_head)
     grad_three = attn_grad.reshape(local_queries, HEADS, per_head)
     logit_grad = (
@@ -162,11 +177,8 @@
         .astype(jnp.bfloat16)
     )
     query_grad = times_transpose(logit_grad, attn_weight).astype(jnp.bfloat16)
-    value_rounded = value_grad.astype(jnp.bfloat16)
     feature_grad = times_transpose(value_rounded, value_weight).astype(jnp.bfloat16)
-    value_term = over_rows(features[0], value_rounded)
-    attn_term = over_rows(queries[0], logit_grad)
-    summed = sum_everywhere(jnp.concatenate([value_term, attn_term, out_term], axis=1))
+    summed = sum_everywhere(shares[:, : terms.shape[1]])
     return (
         feature_grad[None],
         query_grad[None],

time: 163 us -> 156 us (0.957)
  starting transfers between devices: 21.8 us -> 14.5 us
    all_to_all x1 -> x0, starting transfers between devices: 7.38 us -> none  [scatter_sum_rows(): return jnp.sum(lax.all_to_all(pieces, axes, 0, 0, tiled=True), axis=0)]
    dot_general x3 -> x4, matrix products: 5.41 us -> 4.42 us  [over_rows_exact(): lax.dot_general(left, right, (((0,), (0,)), ((), ())), precision=lax.Prec...]
  transfers between devices with their start and end apart: 3 -> 2, of which waited for: 1 -> 1; matrix products, arithmetic and copies ran while one was open for 42% -> 23% of each run, Pallas kernels for 0% -> 0%
where the time goes in v6:
time: 156 us; the launch traced here: 155 us
  other arithmetic  48.4 us (31%)
  blocking collectives  38.1 us (24%)
  matrix products  24.5 us (16%)
  local copies, waits for them, and re-layouts  20.7 us (13%)
  starting transfers between devices  14.5 us (9%)
  waiting for transfers between devices  7.03 us (5%)
    scatter-add x1, other arithmetic, local(): corner_sums = jnp.zeros((token_count + margin, 4 * width), jnp.float32).a...  25.7 us
    all_to_all x1, blocking collectives, scatter_sum_rows(): return jnp.sum(lax.all_to_all(pieces, axes, 0, 0, tiled=True), axis=0)  21.6 us
    all_to_all x1, blocking collectives, sum_everywhere(): block = jnp.sum(lax.all_to_all(copies, 'dp', 0, 0, tiled=True), axis=0)  16.5 us
    gather x1, local copies, waits for them, and re-layouts, local(): picked_all = row_major(corner_table[base_row]).astype(jnp.float32)  15.5 us
    all_to_all x2, starting transfers between devices, gather_rows(): gathered = lax.all_to_all(copies, axes, 0, 0, tiled=True)  14.5 us
    dot_general x1, matrix products, local(): jnp.dot(query_onehot, every_grad, preferred_element_type=jnp.float32)  10.2 us
    convert_element_type x1, other arithmetic, local(): value_rounded = value_grad.astype(jnp.bfloat16)  7.05 us
    all_to_all x2, waiting for transfers between devices, gather_rows(): gathered = lax.all_to_all(copies, axes, 0, 0, tiled=True)  7.03 us
  transfers between devices with their start and end apart: 2, of which 1 were waited for; matrix products, arithmetic and copies ran while one was open for 23% of the time, Pallas kernels for 0%

profile of v6, /device:TPU:1, one launch (start us, length us, event | category | flops | bytes accessed | tf_op | source)
XLA Modules:
  0.0 154.7 jit_solution(12009822272404530780)
XLA Ops:
  0.6 0.0 copy-start
  0.6 1.1 convolution_exponential_fusion.1
  1.8 0.1 reshape.257
  1.9 0.1 reduce_sum.72
  1.9 0.1 div.61
  2.0 0.1 div.62
  2.1 1.1 convolution_convert_fusion.3
  3.2 0.7 pad_maximum_fusion.2
  3.9 0.8 broadcast_in_dim.36
  4.7 8.6 %all-to-all-start = ((bf16[32,8,896]{2,1,0:T(8,128)(2,1)}), bf16[32,8,896]{2,1,0:T(8,128)(2,1)S(1)}, u32[]{:S(2)}, u32[]{:S(2)}) async-start(bf16[32,8,896]{2,1,0:T(8,128)(2,1)} %broadcast_in_dim.36), calls=%async_computation | async-start | bytes 917504 | tf_op jit(solution)/shard_map/all_to_all | solution.py:36
  14.0 0.8 compare_select_fusion.2
  14.8 0.7 add_select_fusion.2
  15.5 0.0 copy-done
  15.5 1.6 %convolution_convert_fusion = bf16[4096,256]{1,0:T(8,128)(2,1)S(1)} fusion(bf16[256,256]{1,0:T(8,128)(2,1)} %param.13, bf16[1,4096,256]{2,1,0:T(8,128)(2,1)S(1)} %copy-done), kind=kOutput, calls=%fused_computation.13 | convolution fusion | flops 537919488 | bytes 4325376 | tf_op jit(solution)/shard_map/dot_general | solution.py:99
  17.1 1.3 pad_slice_fusion.2
  18.4 3.9 %pad_maximum_fusion = bf16[4096,1024]{1,0:T(8,128)(2,1)} fusion(bf16[4096,256]{1,0:T(8,128)(2,1)S(1)} %get-tuple-element.17, bf16[4096,256]{1,0:T(8,128)(2,1)S(1)} %get-tuple-element.16, bf16[4096,256]{1,0:T(8,128)(2,1)S(1)} %get-tuple-element.15, bf16[4096,256]{1,0:T(8,128)(2,1)S(1)} %convolution_convert_fusion), kind=kLoop, calls=%fused_computation.12 | loop fusion | flops 33554432 | bytes 16777216 | tf_op jit(solution)/shard_map/concatenate | solution.py:120
  22.4 15.5 %gather_fusion = bf16[2048,1024]{1,0:T(8,128)(2,1)} fusion(bf16[4096,1024]{1,0:T(8,128)(2,1)} %pad_maximum_fusion, s32[2048]{0:T(1024)S(1)} %broadcast_clamp_fusion), kind=kCustom, calls=%fused_computation | custom fusion | bytes 8396800 | tf_op jit(solution)/shard_map/gather | solution.py:124
  37.8 0.0 copy-start.4
  37.8 0.0 copy-start.2
  37.8 6.5 %convert_element_type.33 = f32[2048,1024]{1,0:T(8,128)} convert(bf16[2048,1024]{1,0:T(8,128)(2,1)} %gather_fusion) | non-fusion elementwise | flops 2097152 | bytes 12582912 | tf_op jit(solution)/shard_map/convert_element_type | solution.py:124
  44.3 0.0 copy-done.4
  44.4 0.0 all-to-all-done
  44.4 0.0 copy-done.2
  44.4 0.2 bitcast_reduce_fusion
  44.6 0.7 fusion.21
  45.3 10.2 %multiply_reduce_fusion = (f32[2048]{0:T(1024)S(1)}, f32[2048,256]{1,0:T(8,128)S(1)}, f32[2048,256]{1,0:T(8,128)}, f32[2048,256]{1,0:T(8,128)}, f32[2048,256]{1,0:T(8,128)}, /*index=5*/f32[2048,256]{1,0:T(8,128)}) fusion(f32[2048,1024]{1,0:T(8,128)} %convert_element_type.33, f32[2048]{0:T(1024)S(1)} %bitcast.78, f32[2048]{0:T(1024)S(1)} %bitcast.80, ...), kind=kOutput, calls=%fused_computation.35 | convolution fusion | flops 276822016 | bytes 19096576 | tf_op jit(solution)/shard_map/dot_general | solution.py:116
  55.6 2.7 %fusion.12 = f32[256,256]{1,0:T(8,128)S(1)} fusion(f32[2048,256]{1,0:T(8,128)S(1)} %get-tuple-element.6, f32[2048]{0:T(1024)S(1)} %get-tuple-element.8, s32[256]{0:T(256)S(1)} %and_select_fusion, s32[2048]{0:T(1024)S(1)} %get-tuple-element.31, s32[2048]{0:T(1024)S(1)} %get-tuple-element.30), kind=kOutput, calls=%fused_computation.23 | convolution fusion | flops 1612709888 | bytes 2384896 | tf_op jit(solution)/shard_map/dot_general | solution.py:18
  58.3 1.2 fusion.46
  59.5 0.2 fusion.47
  59.7 0.3 fusion.41
  60.1 25.7 %scatter_custom_fusion = f32[4161,1024]{1,0:T(8,128)} fusion(s32[2048]{0:T(1024)S(1)} %bitcast.86, f32[]{:T(128)} %constant.54.clone.1, f32[2048,256]{1,0:T(8,128)} %get-tuple-element.11, f32[]{:T(128)} %constant.79, f32[2048,256]{1,0:T(8,128)} %get-tuple-element.12, f32[2048,256]{1,0:T(8,128)} %get-tuple-element.13, f32[2048,256]{1,0:T(8,128)} %get-tuple-element.14), kind=kCustom, calls=%fused_computation.3 | custom fusion | flops 8388608 | bytes 25432072 | tf_op jit(solution)/shard_map/scatter-add | solution.py:137
  85.7 7.0 %fusion.11 = bf16[4096,256]{1,0:T(8,128)(2,1)S(1)} fusion(f32[4161,1024]{1,0:T(8,128)} %scatter_custom_fusion), kind=kLoop, calls=%fused_computation.17 | loop fusion | flops 4194304 | bytes 18874368 | tf_op jit(solution)/shard_map/convert_element_type | solution.py:146
  92.8 0.0 copy-start.1
  92.8 0.7 fusion.22
  93.5 0.6 copy-done.1
  94.1 0.1 pad_maximum_fusion.1
  94.2 1.1 copy.16
  95.3 21.6 %all_to_all.20 = f32[32,8,768]{2,1,0:T(8,128)S(1)} all-to-all(f32[32,8,768]{2,1,0:T(8,128)} %bitcast.67), channel_id=1, replica_groups=mesh['tile'=16,'query'=2,'dp'=8] {'tile','query'}, dimensions={0} | all-to-all | bytes 1572864 | tf_op jit(solution)/shard_map/all_to_all | solution.py:43
  117.0 0.0 copy-start.3
  117.0 0.1 reduce_sum.77
  117.1 16.5 %all_to_all.21 = f32[8,8,640]{2,1,0:T(8,128)S(1)} all-to-all(f32[8,8,640]{2,1,0:T(8,128)S(1)} %broadcast_in_dim.43), channel_id=1, replica_groups=mesh['tile'=16,'query'=2,'dp'=8] {'dp'}, dimensions={0} | all-to-all | bytes 327680 | tf_op jit(solution)/shard_map/all_to_all | solution.py:49
  133.5 0.9 broadcast_in_dim.44
  134.4 5.9 %all-to-all-start.3 = ((f32[32,8,640]{2,1,0:T(8,128)}), f32[32,8,640]{2,1,0:T(8,128)S(1)}, u32[]{:S(2)}, u32[]{:S(2)}) async-start(f32[32,8,640]{2,1,0:T(8,128)} %broadcast_in_dim.44), calls=%async_computation.3 | async-start | bytes 1310720 | tf_op jit(solution)/shard_map/all_to_all | solution.py:36
  140.4 0.0 copy-done.3
  140.4 3.7 %fusion.10 = bf16[1,4096,256]{2,1,0:T(8,128)(2,1)} fusion(bf16[4096,256]{1,0:T(8,128)(2,1)} %copy-done.1, bf16[256,256]{1,0:T(8,128)(2,1)S(1)} %copy-done.3), kind=kOutput, calls=%fused_computation.15 | convolution fusion | flops 537919488 | bytes 4325376 | tf_op jit(solution)/shard_map/dot_general | solution.py:28
  144.0 0.1 reshape.262
  144.1 1.2 fusion
  145.3 0.1 sub.45
  145.4 0.8 fusion.25
  146.2 7.0 %all-to-all-done.3 = f32[32,8,640]{2,1,0:T(8,128)S(1)} async-done(((f32[32,8,640]{2,1,0:T(8,128)}), f32[32,8,640]{2,1,0:T(8,128)S(1)}, u32[]{:S(2)}, u32[]{:S(2)}) %all-to-all-start.3) | async-done | bytes 655392 | tf_op jit(solution)/shard_map/all_to_all | solution.py:36
  153.2 0.7 slice_multiply_fusion.6
  153.9 0.8 slice_multiply_fusion.4
  (12 shorter events, 0.1 us)
Async XLA Ops:
  0.6 14.9 %copy-start = (bf16[1,4096,256]{2,1,0:T(8,128)(2,1)S(1)}, bf16[1,4096,256]{2,1,0:T(8,128)(2,1)}, u32[]{:S(2)}) copy-start(bf16[1,4096,256]{2,1,0:T(8,128)(2,1)} %param.10) | copy-start | bytes 6291460
  4.7 39.6 %all-to-all-start = ((bf16[32,8,896]{2,1,0:T(8,128)(2,1)}), bf16[32,8,896]{2,1,0:T(8,128)(2,1)S(1)}, u32[]{:S(2)}, u32[]{:S(2)}) async-start(bf16[32,8,896]{2,1,0:T(8,128)(2,1)} %broadcast_in_dim.36), calls=%async_computation | async-start | bytes 917504 | tf_op jit(solution)/shard_map/all_to_all | solution.py:36
  37.8 6.5 %copy-start.4 = (f32[1,4,2048]{2,1,0:T(4,128)S(1)}, f32[1,4,2048]{2,1,0:T(4,128)}, u32[]{:S(2)}) copy-start(f32[1,4,2048]{2,1,0:T(4,128)} %param.18) | copy-start | bytes 98308
  37.8 6.5 %copy-start.2 = (bf16[256,128]{1,0:T(8,128)(2,1)S(1)}, bf16[256,128]{1,0:T(8,128)(2,1)}, u32[]{:S(2)}) copy-start(bf16[256,128]{1,0:T(8,128)(2,1)} %param.14) | copy-start | bytes 196612
  92.8 1.4 copy-start.1
  117.0 23.4 %copy-start.3 = (bf16[256,256]{1,0:T(8,128)(2,1)S(1)}, bf16[256,256]{1,0:T(8,128)(2,1)}, u32[]{:S(2)}) copy-start(bf16[256,256]{1,0:T(8,128)(2,1)} %param.13) | copy-start | bytes 393220
  134.4 18.8 %all-to-all-start.3 = ((f32[32,8,640]{2,1,0:T(8,128)}), f32[32,8,640]{2,1,0:T(8,128)S(1)}, u32[]{:S(2)}, u32[]{:S(2)}) async-start(f32[32,8,640]{2,1,0:T(8,128)} %broadcast_in_dim.44), calls=%async_computation.3 | async-start | bytes 1310720 | tf_op jit(solution)/shard_map/all_to_all | solution.py:36

commit v7 on v6

--- a/solution.py
+++ b/solution.py
@@ -116,19 +116,29 @@
     grad_rows = jnp.dot(query_onehot, every_grad, preferred_element_type=jnp.float32)
     slot_grad = row_major(jnp.where(head_mask, grad_rows, jnp.zeros((), jnp.float32)))
     offsets = (0, 1, TILE_W, TILE_W + 1)
-    padded = jnp.concatenate([projected, jnp.zeros((TILE_W + 1, width), jnp.bfloat16)], axis=0)
+    padded = jnp.concatenate(
+        [
+            jnp.concatenate([projected, features[0]], axis=1),
+            jnp.zeros((TILE_W + 1, 2 * width), jnp.bfloat16),
+        ],
+        axis=0,
+    )
     corner_table = jnp.concatenate(
         [padded[offset : offset + token_count] for offset in offsets], axis=1
     )
     base_row = slot_rows[0, 0]
     picked_all = row_major(corner_table[base_row]).astype(jnp.float32)
     mixed_rows = jnp.zeros((capacity, width), jnp.float32)
+    mixed_features = jnp.zeros((capacity, width), jnp.float32)
     contributions = []
     for corner in range(4):
         bilinear = slot_bilinear[0, corner]
-        picked = picked_all[:, corner * width : (corner + 1) * width]
+        picked = picked_all[:, 2 * corner * width : (2 * corner + 1) * width]
+        picked_features = picked_all[:, (2 * corner + 1) * width : (2 * corner + 2) * width]
         mixed_rows = mixed_rows + bilinear[:, None] * picked
+        mixed_features = mixed_features + bilinear[:, None] * picked_features
         contributions.append((weight * bilinear)[:, None] * slot_grad)
+    value_term = over_rows_exact(mixed_features, weight[:, None] * slot_grad)
     corner_dots = jnp.sum(mixed_rows * slot_grad, axis=1)
     margin = TILE_W + 1
     corner_sums = (
@@ -144,7 +154,6 @@
             + corner_sums[start : start + token_count, corner * width : (corner + 1) * width]
         )
     value_rounded = value_grad.astype(jnp.bfloat16)
-    value_term = over_rows(features[0], value_rounded)
     query_float = query_match.astype(jnp.float32)
     sampled_part = over_rows_exact(
         query_float, jnp.where(head_mask, weight[:, None] * mixed_rows, jnp.zeros((), jnp.float32))

time: 156 us -> 201 us (1.29)
  local copies, waits for them, and re-layouts: 20.7 us -> 70.1 us
  blocking collectives: 38.1 us -> 21.6 us
  matrix products: 24.5 us -> 38 us
  starting transfers between devices: 14.5 us -> 21.1 us
  waiting for transfers between devices: 7.03 us -> 2.35 us
  other arithmetic: 48.4 us -> 45.2 us
    concatenate x0 -> x2, local copies, waits for them, and re-layouts: none -> 27.6 us  [local(): jnp.concatenate([padded[offset:offset + token_count] for offset in offset...]
    all_to_all x1 -> x0, blocking collectives: 16.5 us -> none  [sum_everywhere(): block = jnp.sum(lax.all_to_all(copies, 'dp', 0, 0, tiled=True), axis=0)]
    unnamed x10, local copies, waits for them, and re-layouts: 0.62 us -> 14.4 us
    gather x1, local copies, waits for them, and re-layouts: 15.5 us -> 24.3 us  [local(): picked_all = row_major(corner_table[base_row]).astype(jnp.float32)]
    all_to_all x0 -> x1, starting transfers between devices: none -> 8.18 us  [sum_everywhere(): block = jnp.sum(lax.all_to_all(copies, 'dp', 0, 0, tiled=True), axis=0)]
    dot_general x4 -> x5, matrix products: 4.42 us -> 12.5 us  [over_rows_exact(): lax.dot_general(left, right, (((0,), (0,)), ((), ())), precision=lax.Prec...]
    convert_element_type x1 -> x0, other arithmetic: 7.05 us -> none  [local(): value_rounded = value_grad.astype(jnp.bfloat16)]
    dot_general x3, matrix products: 5.51 us -> 10.3 us  [times_transpose(): lax.dot_general(left, right, (((1,), (1,)), ((), ())), preferred_element_...]
  transfers between devices with their start and end apart: 2 -> 3, of which waited for: 1 -> 1; matrix products, arithmetic and copies ran while one was open for 23% -> 61% of each run, Pallas kernels for 0% -> 0%
where the time goes in v7:
time: 201 us; the launch traced here: 200 us
  local copies, waits for them, and re-layouts  70.1 us (35%)
  other arithmetic  45.2 us (22%)
  matrix products  38 us (19%)
  blocking collectives  21.6 us (11%)
  starting transfers between devices  21.1 us (10%)
  waiting for transfers between devices  2.35 us (1%)
    concatenate x2, local copies, waits for them, and re-layouts, local(): jnp.concatenate([padded[offset:offset + token_count] for offset in offset...  27.6 us
    scatter-add x1, other arithmetic, local(): corner_sums = jnp.zeros((token_count + margin, 4 * width), jnp.float32).a...  25.3 us
    gather x1, local copies, waits for them, and re-layouts, local(): picked_all = row_major(corner_table[base_row]).astype(jnp.float32)  24.3 us
    all_to_all x1, blocking collectives, scatter_sum_rows(): return jnp.sum(lax.all_to_all(pieces, axes, 0, 0, tiled=True), axis=0)  21.6 us
    unnamed x10, local copies, waits for them, and re-layouts  14.4 us
    all_to_all x2, starting transfers between devices, gather_rows(): gathered = lax.all_to_all(copies, axes, 0, 0, tiled=True)  12.9 us
    dot_general x5, matrix products, over_rows_exact(): lax.dot_general(left, right, (((0,), (0,)), ((), ())), precision=lax.Prec...  12.5 us
    convert_element_type x1, other arithmetic, local(): picked_all = row_major(corner_table[base_row]).astype(jnp.float32)  11.3 us
  transfers between devices with their start and end apart: 3, of which 1 were waited for; matrix products, arithmetic and copies ran while one was open for 61% of the time, Pallas kernels for 0%

profile of v7, /device:TPU:1, one launch (start us, length us, event | category | flops | bytes accessed | tf_op | source)
XLA Modules:
  0.0 199.9 jit_solution(5483011428012002788)
XLA Ops:
  0.6 0.0 copy-start
  0.6 1.0 convolution_exponential_fusion.1
  1.7 0.1 reshape.257
  1.7 0.1 reduce_sum.72
  1.8 0.1 div.61
  1.9 0.1 div.62
  2.0 1.1 convolution_convert_fusion.3
  3.1 0.7 pad_maximum_fusion.1
  3.8 0.8 broadcast_in_dim.32
  4.6 8.6 %all-to-all-start = ((bf16[32,8,896]{2,1,0:T(8,128)(2,1)}), bf16[32,8,896]{2,1,0:T(8,128)(2,1)S(1)}, u32[]{:S(2)}, u32[]{:S(2)}) async-start(bf16[32,8,896]{2,1,0:T(8,128)(2,1)} %broadcast_in_dim.32), calls=%async_computation | async-start | bytes 917504 | tf_op jit(solution)/shard_map/all_to_all | solution.py:36
  13.9 0.8 compare_select_fusion.2
  14.7 0.7 add_select_fusion.2
  15.4 2.9 %copy.20 = bf16[1,4096,256]{1,2,0:T(8,128)(2,1)S(1)} copy(bf16[1,4096,256]{2,1,0:T(8,128)(2,1)} %param.10) | data formatting | bytes 4194304 | tf_op args[0]
  18.3 0.0 copy-done
  18.3 3.7 %constant_dynamic-update-slice_fusion.1 = (bf16[4096,2048]{0,1:T(8,128)(2,1)}, bf16[4096,256]{0,1:T(8,128)(2,1)S(1)}) fusion(bf16[256,256]{1,0:T(8,128)(2,1)S(1)} %copy-done, bf16[1,4096,256]{2,1,0:T(8,128)(2,1)} %param.10), kind=kOutput, calls=%fused_computation.115 | convolution fusion | flops 537919488 | bytes 6422528 | tf_op jit(solution)/shard_map/dot_general | solution.py:99
  22.0 1.4 constant_dynamic-update-slice_fusion
  23.5 3.4 %fusion.13 = bf16[4161,512]{0,1:T(8,128)(2,1)S(1)} fusion(bf16[4096,256]{0,1:T(8,128)(2,1)S(1)} %bitcast.63, bf16[4096,256]{0,1:T(8,128)(2,1)S(1)} %get-tuple-element.30), kind=kLoop, calls=%fused_computation.18 | loop fusion | flops 14913024 | bytes 8455168 | tf_op jit(solution)/shard_map/concatenate | solution.py:121
  26.9 5.0 %slice_dynamic-update-slice_fusion.2 = bf16[4096,2048]{0,1:T(8,128)(2,1)} fusion(bf16[4096,2048]{0,1:T(8,128)(2,1)} %constant_dynamic-update-slice_fusion, bf16[4161,512]{0,1:T(8,128)(2,1)S(1)} %fusion.13), kind=kLoop, calls=%fused_computation.21 | loop fusion | bytes 8388608
  31.9 5.0 %slice_dynamic-update-slice_fusion.1 = bf16[4096,2048]{0,1:T(8,128)(2,1)} fusion(bf16[4096,2048]{0,1:T(8,128)(2,1)} %slice_dynamic-update-slice_fusion.2, bf16[4161,512]{0,1:T(8,128)(2,1)S(1)} %fusion.13), kind=kLoop, calls=%fused_computation.20 | loop fusion | bytes 8388608
  36.9 5.0 %slice_dynamic-update-slice_fusion = bf16[4096,2048]{0,1:T(8,128)(2,1)} fusion(bf16[4096,2048]{0,1:T(8,128)(2,1)} %slice_dynamic-update-slice_fusion.1, bf16[4161,512]{0,1:T(8,128)(2,1)S(1)} %fusion.13), kind=kLoop, calls=%fused_computation.19 | loop fusion | bytes 8388608 | tf_op jit(solution)/shard_map/concatenate | solution.py:126
  41.9 22.6 %copy.21 = bf16[4096,2048]{1,0:T(8,128)(2,1)} copy(bf16[4096,2048]{0,1:T(8,128)(2,1)} %slice_dynamic-update-slice_fusion) | data formatting | bytes 33554432 | tf_op jit(solution)/shard_map/concatenate | solution.py:126
  64.5 24.3 %gather_fusion = bf16[2048,2048]{1,0:T(8,128)(2,1)} fusion(bf16[4096,2048]{1,0:T(8,128)(2,1)} %copy.21, s32[2048]{0:T(1024)S(1)} %broadcast_clamp_fusion), kind=kCustom, calls=%fused_computation | custom fusion | bytes 16785408 | tf_op jit(solution)/shard_map/gather | solution.py:130
  88.7 0.0 copy-start.2
  88.8 0.0 copy-start.1
  88.8 11.3 %convert_element_type.33 = f32[2048,2048]{1,0:T(8,128)} convert(bf16[2048,2048]{1,0:T(8,128)(2,1)} %gather_fusion) | non-fusion elementwise | flops 4194304 | bytes 25165824 | tf_op jit(solution)/shard_map/convert_element_type | solution.py:130
  100.0 0.0 copy-done.2
  100.0 0.0 all-to-all-done
  100.0 0.0 copy-done.1
  100.1 0.2 bitcast_reduce_fusion
  100.3 0.7 fusion.31
  101.0 9.5 %multiply_reduce_fusion = (f32[2048]{0:T(1024)S(1)}, f32[2048,256]{1,0:T(8,128)S(1)}, f32[2048,256]{1,0:T(8,128)S(1)}, f32[2048,256]{1,0:T(8,128)}, f32[2048,256...) fusion(f32[2048,2048]{1,0:T(8,128)} %convert_element_type.33, f32[2048]{0:T(1024)S(1)} %bitcast.76, ...), kind=kOutput, calls=%fused_computation.47 | convolution fusion | flops 276822016 | bytes 21193728 | tf_op jit(solution)/shard_map/dot_general | solution.py:116
  110.5 8.1 %fusion.21 = f32[256,256]{0,1:T(8,128)S(1)} fusion(f32[2048,2048]{1,0:T(8,128)} %convert_element_type.33, f32[2048,256]{1,0:T(8,128)S(1)} %get-tuple-element.31, f32[2048]{0:T(1024)S(1)} %get-tuple-element.8, f32[2048]{0:T(1024)S(1)} %bitcast.77, f32[2048]{0:T(1024)S(1)} %bitcast.80, f32[2048]{0:T(1024)S(1)} %bitcast.74, f32[2048]{0:T(1024)S(1)} %bitcast.83), kind=kOutput, calls=%fused_computation.39 | convolution fusion | flops 1614807040 | bytes 10788864 | tf_op jit(solution)/shard_map/dot_general | solution.py:18
  118.6 2.7 %fusion.15 = f32[256,256]{1,0:T(8,128)S(1)} fusion(f32[2048,256]{1,0:T(8,128)S(1)} %get-tuple-element.6, f32[2048]{0:T(1024)S(1)} %get-tuple-element.8, s32[256]{0:T(256)S(1)} %and_select_fusion, s32[2048]{0:T(1024)S(1)} %get-tuple-element.28, s32[2048]{0:T(1024)S(1)} %get-tuple-element.27), kind=kOutput, calls=%fused_computation.29 | convolution fusion | flops 1612709888 | bytes 2384896 | tf_op jit(solution)/shard_map/dot_general | solution.py:18
  121.3 1.2 fusion.58
  122.6 0.2 fusion.59
  122.8 0.3 fusion.53
  123.1 0.1 pad_maximum_fusion
  123.2 1.1 copy.22
  124.3 21.6 %all_to_all.20 = f32[32,8,768]{2,1,0:T(8,128)S(1)} all-to-all(f32[32,8,768]{2,1,0:T(8,128)} %bitcast.64), channel_id=1, replica_groups=mesh['tile'=16,'query'=2,'dp'=8] {'tile','query'}, dimensions={0} | all-to-all | bytes 1572864 | tf_op jit(solution)/shard_map/all_to_all | solution.py:43
  145.9 0.1 reduce_sum.77
  146.0 0.7 broadcast_in_dim.43
  146.7 8.2 %all-to-all-start.2 = ((f32[8,8,640]{2,1,0:T(8,128)}), f32[8,8,640]{2,1,0:T(8,128)S(1)}, u32[]{:S(2)}, u32[]{:S(2)}) async-start(f32[8,8,640]{2,1,0:T(8,128)} %broadcast_in_dim.43), calls=%async_computation.2 | async-start | bytes 327680 | tf_op jit(solution)/shard_map/all_to_all | solution.py:49
  154.9 25.3 %scatter_custom_fusion = f32[4161,1024]{1,0:T(8,128)} fusion(s32[2048]{0:T(1024)S(1)} %bitcast.87, f32[]{:T(128)} %constant.54.clone.1, f32[2048,256]{1,0:T(8,128)S(1)} %get-tuple-element.11, f32[]{:T(128)} %constant.79, f32[2048,256]{1,0:T(8,128)} %get-tuple-element.12, f32[2048,256]{1,0:T(8,128)} %get-tuple-element.13, f32[2048,256]{1,0:T(8,128)} %get-tuple-element.14), kind=kCustom, calls=%fused_computation.6 | custom fusion | flops 8388608 | bytes 25432072 | tf_op jit(solution)/shard_map/scatter-add | solution.py:147
  180.2 0.0 all-to-all-done.2
  180.2 0.9 broadcast_in_dim.44
  181.1 4.3 %all-to-all-start.3 = ((f32[32,8,640]{2,1,0:T(8,128)}), f32[32,8,640]{2,1,0:T(8,128)S(1)}, u32[]{:S(2)}, u32[]{:S(2)}) async-start(f32[32,8,640]{2,1,0:T(8,128)} %broadcast_in_dim.44), calls=%async_computation.3 | async-start | bytes 1310720 | tf_op jit(solution)/shard_map/all_to_all | solution.py:36
  185.5 8.5 %fusion.12 = bf16[1,4096,256]{2,1,0:T(8,128)(2,1)} fusion(bf16[256,256]{1,0:T(8,128)(2,1)S(1)} %copy-done, f32[4161,1024]{1,0:T(8,128)} %scatter_custom_fusion), kind=kOutput, calls=%fused_computation.17 | convolution fusion | flops 542113792 | bytes 19005440 | tf_op jit(solution)/shard_map/dot_general | solution.py:28
  193.9 0.1 reshape.262
  194.0 1.2 fusion
  195.2 0.1 sub.45
  195.3 0.8 fusion.32
  196.1 2.3 %all-to-all-done.3 = f32[32,8,640]{2,1,0:T(8,128)S(1)} async-done(((f32[32,8,640]{2,1,0:T(8,128)}), f32[32,8,640]{2,1,0:T(8,128)S(1)}, u32[]{:S(2)}, u32[]{:S(2)}) %all-to-all-start.3) | async-done | bytes 655392 | tf_op jit(solution)/shard_map/all_to_all | solution.py:36
  198.4 0.7 slice_multiply_fusion.11
  199.1 0.8 slice_multiply_fusion.9
  (11 shorter events, 0.1 us)
Async XLA Ops:
  0.6 17.7 %copy-start = (bf16[256,256]{1,0:T(8,128)(2,1)S(1)}, bf16[256,256]{1,0:T(8,128)(2,1)}, u32[]{:S(2)}) copy-start(bf16[256,256]{1,0:T(8,128)(2,1)} %param.13) | copy-start | bytes 393220
  4.6 95.4 %all-to-all-start = ((bf16[32,8,896]{2,1,0:T(8,128)(2,1)}), bf16[32,8,896]{2,1,0:T(8,128)(2,1)S(1)}, u32[]{:S(2)}, u32[]{:S(2)}) async-start(bf16[32,8,896]{2,1,0:T(8,128)(2,1)} %broadcast_in_dim.32), calls=%async_computation | async-start | bytes 917504 | tf_op jit(solution)/shard_map/all_to_all | solution.py:36
  88.7 11.3 %copy-start.2 = (f32[1,4,2048]{2,1,0:T(4,128)S(1)}, f32[1,4,2048]{2,1,0:T(4,128)}, u32[]{:S(2)}) copy-start(f32[1,4,2048]{2,1,0:T(4,128)} %param.18) | copy-start | bytes 98308
  88.8 11.3 %copy-start.1 = (bf16[256,128]{1,0:T(8,128)(2,1)S(1)}, bf16[256,128]{1,0:T(8,128)(2,1)}, u32[]{:S(2)}) copy-start(bf16[256,128]{1,0:T(8,128)(2,1)} %param.14) | copy-start | bytes 196612
  146.7 33.5 %all-to-all-start.2 = ((f32[8,8,640]{2,1,0:T(8,128)}), f32[8,8,640]{2,1,0:T(8,128)S(1)}, u32[]{:S(2)}, u32[]{:S(2)}) async-start(f32[8,8,640]{2,1,0:T(8,128)} %broadcast_in_dim.43), calls=%async_computation.2 | async-start | bytes 327680 | tf_op jit(solution)/shard_map/all_to_all | solution.py:49
  181.1 17.3 %all-to-all-start.3 = ((f32[32,8,640]{2,1,0:T(8,128)}), f32[32,8,640]{2,1,0:T(8,128)S(1)}, u32[]{:S(2)}, u32[]{:S(2)}) async-start(f32[32,8,640]{2,1,0:T(8,128)} %broadcast_in_dim.44), calls=%async_computation.3 | async-start | bytes 1310720 | tf_op jit(solution)/shard_map/all_to_all | solution.py:36

commit v8 on v6

--- a/solution.py
+++ b/solution.py
@@ -166,7 +166,7 @@
         * (part_three - jnp.sum(page_attention * part_three, axis=2, keepdims=True))
     ).reshape(all_queries, att_width)
     attn_term = over_rows_exact(every_queries.astype(jnp.float32), part_logits)
-    terms = jnp.concatenate([value_term, attn_term, out_term], axis=1)
+    terms = jnp.concatenate([value_term, attn_term, out_term], axis=1) * grad_scale
     shares = scatter_sum_rows(jnp.concatenate([terms, attn_part], axis=1), ("tile", "query"))
     attn_grad = shares[:, terms.shape[1] :]
     attn_three = attention.reshape(local_queries, HEADS, per_head)
@@ -182,9 +182,9 @@
     return (
         feature_grad[None],
         query_grad[None],
-        summed[:, :width] * grad_scale,
-        summed[:, width : width + att_width] * grad_scale,
-        summed[:, width + att_width :] * grad_scale,
+        summed[:, :width],
+        summed[:, width : width + att_width],
+        summed[:, width + att_width :],
     )
 
 

time: 156 us -> 156 us (level)
  no operation moved by 1% of the time
where the time goes in v8:
time: 156 us; the launch traced here: 155 us
  other arithmetic  46.9 us (30%)
  blocking collectives  38.1 us (24%)
  matrix products  24.5 us (16%)
  local copies, waits for them, and re-layouts  22.1 us (14%)
  starting transfers between devices  14.5 us (9%)
  waiting for transfers between devices  7.03 us (5%)
    scatter-add x1, other arithmetic, local(): corner_sums = jnp.zeros((token_count + margin, 4 * width), jnp.float32).a...  25.7 us
    all_to_all x1, blocking collectives, scatter_sum_rows(): return jnp.sum(lax.all_to_all(pieces, axes, 0, 0, tiled=True), axis=0)  21.6 us
    all_to_all x1, blocking collectives, sum_everywhere(): block = jnp.sum(lax.all_to_all(copies, 'dp', 0, 0, tiled=True), axis=0)  16.5 us
    gather x1, local copies, waits for them, and re-layouts, local(): picked_all = row_major(corner_table[base_row]).astype(jnp.float32)  15.5 us
    all_to_all x2, starting transfers between devices, gather_rows(): gathered = lax.all_to_all(copies, axes, 0, 0, tiled=True)  14.5 us
    dot_general x1, matrix products, local(): jnp.dot(query_onehot, every_grad, preferred_element_type=jnp.float32)  10.2 us
    convert_element_type x1, other arithmetic, local(): value_rounded = value_grad.astype(jnp.bfloat16)  7.05 us
    all_to_all x2, waiting for transfers between devices, gather_rows(): gathered = lax.all_to_all(copies, axes, 0, 0, tiled=True)  7.03 us
  transfers between devices with their start and end apart: 2, of which 1 were waited for; matrix products, arithmetic and copies ran while one was open for 23% of the time, Pallas kernels for 0%

profile of v8, /device:TPU:1, one launch (start us, length us, event | category | flops | bytes accessed | tf_op | source)
XLA Modules:
  0.0 154.8 jit_solution(1327557763506216488)
XLA Ops:
  0.6 0.0 copy-start
  0.6 1.1 convolution_exponential_fusion.1
  1.8 0.1 reshape.257
  1.9 0.1 reduce_sum.72
  1.9 0.1 div.61
  2.0 0.1 div.62
  2.1 1.1 convolution_convert_fusion.3
  3.2 0.7 pad_maximum_fusion.2
  3.9 0.8 broadcast_in_dim.36
  4.7 8.6 %all-to-all-start = ((bf16[32,8,896]{2,1,0:T(8,128)(2,1)}), bf16[32,8,896]{2,1,0:T(8,128)(2,1)S(1)}, u32[]{:S(2)}, u32[]{:S(2)}) async-start(bf16[32,8,896]{2,1,0:T(8,128)(2,1)} %broadcast_in_dim.36), calls=%async_computation | async-start | bytes 917504 | tf_op jit(solution)/shard_map/all_to_all | solution.py:36
  14.0 0.8 compare_select_fusion.2
  14.8 0.7 add_select_fusion.2
  15.5 0.0 copy-done
  15.5 1.6 %convolution_convert_fusion = bf16[4096,256]{1,0:T(8,128)(2,1)S(1)} fusion(bf16[256,256]{1,0:T(8,128)(2,1)} %param.13, bf16[1,4096,256]{2,1,0:T(8,128)(2,1)S(1)} %copy-done), kind=kOutput, calls=%fused_computation.13 | convolution fusion | flops 537919488 | bytes 4325376 | tf_op jit(solution)/shard_map/dot_general | solution.py:99
  17.1 1.3 pad_slice_fusion.2
  18.4 3.9 %pad_maximum_fusion = bf16[4096,1024]{1,0:T(8,128)(2,1)} fusion(bf16[4096,256]{1,0:T(8,128)(2,1)S(1)} %get-tuple-element.17, bf16[4096,256]{1,0:T(8,128)(2,1)S(1)} %get-tuple-element.16, bf16[4096,256]{1,0:T(8,128)(2,1)S(1)} %get-tuple-element.15, bf16[4096,256]{1,0:T(8,128)(2,1)S(1)} %convolution_convert_fusion), kind=kLoop, calls=%fused_computation.12 | loop fusion | flops 33554432 | bytes 16777216 | tf_op jit(solution)/shard_map/concatenate | solution.py:120
  22.4 15.5 %gather_fusion = bf16[2048,1024]{1,0:T(8,128)(2,1)} fusion(bf16[4096,1024]{1,0:T(8,128)(2,1)} %pad_maximum_fusion, s32[2048]{0:T(1024)S(1)} %broadcast_clamp_fusion), kind=kCustom, calls=%fused_computation | custom fusion | bytes 8396800 | tf_op jit(solution)/shard_map/gather | solution.py:124
  37.8 0.0 copy-start.4
  37.8 0.0 copy-start.2
  37.8 6.5 %convert_element_type.33 = f32[2048,1024]{1,0:T(8,128)} convert(bf16[2048,1024]{1,0:T(8,128)(2,1)} %gather_fusion) | non-fusion elementwise | flops 2097152 | bytes 12582912 | tf_op jit(solution)/shard_map/convert_element_type | solution.py:124
  44.3 0.0 copy-done.4
  44.4 0.0 all-to-all-done
  44.4 0.0 copy-done.2
  44.4 0.2 bitcast_reduce_fusion
  44.6 0.7 fusion.21
  45.3 10.2 %multiply_reduce_fusion = (f32[2048]{0:T(1024)S(1)}, f32[2048,256]{1,0:T(8,128)S(1)}, f32[2048,256]{1,0:T(8,128)}, f32[2048,256]{1,0:T(8,128)}, f32[2048,256]{1,0:T(8,128)}, /*index=5*/f32[2048,256]{1,0:T(8,128)}) fusion(f32[2048,1024]{1,0:T(8,128)} %convert_element_type.33, f32[2048]{0:T(1024)S(1)} %bitcast.78, f32[2048]{0:T(1024)S(1)} %bitcast.80, ...), kind=kOutput, calls=%fused_computation.35 | convolution fusion | flops 276822016 | bytes 19096576 | tf_op jit(solution)/shard_map/dot_general | solution.py:116
  55.6 2.7 %fusion.12 = f32[256,256]{1,0:T(8,128)S(1)} fusion(f32[2048,256]{1,0:T(8,128)S(1)} %get-tuple-element.6, f32[2048]{0:T(1024)S(1)} %get-tuple-element.8, s32[256]{0:T(256)S(1)} %and_select_fusion, s32[2048]{0:T(1024)S(1)} %get-tuple-element.31, s32[2048]{0:T(1024)S(1)} %get-tuple-element.30), kind=kOutput, calls=%fused_computation.23 | convolution fusion | flops 1612709888 | bytes 2384896 | tf_op jit(solution)/shard_map/dot_general | solution.py:18
  58.3 1.2 fusion.46
  59.5 0.2 fusion.47
  59.7 0.3 fusion.41
  60.1 25.7 %scatter_custom_fusion = f32[4161,1024]{1,0:T(8,128)} fusion(s32[2048]{0:T(1024)S(1)} %bitcast.86, f32[]{:T(128)} %constant.53.clone.1, f32[2048,256]{1,0:T(8,128)} %get-tuple-element.11, f32[]{:T(128)} %constant.78, f32[2048,256]{1,0:T(8,128)} %get-tuple-element.12, f32[2048,256]{1,0:T(8,128)} %get-tuple-element.13, f32[2048,256]{1,0:T(8,128)} %get-tuple-element.14), kind=kCustom, calls=%fused_computation.3 | custom fusion | flops 8388608 | bytes 25432072 | tf_op jit(solution)/shard_map/scatter-add | solution.py:137
  85.7 7.0 %fusion.11 = bf16[4096,256]{1,0:T(8,128)(2,1)S(1)} fusion(f32[4161,1024]{1,0:T(8,128)} %scatter_custom_fusion), kind=kLoop, calls=%fused_computation.17 | loop fusion | flops 4194304 | bytes 18874368 | tf_op jit(solution)/shard_map/convert_element_type | solution.py:146
  92.8 0.0 copy-start.1
  92.8 0.7 fusion.22
  93.5 0.6 copy-done.1
  94.1 0.1 maximum_multiply_fusion
  94.2 0.1 pad_maximum_fusion.1
  94.2 1.1 copy.16
  95.4 21.6 %all_to_all.20 = f32[32,8,768]{2,1,0:T(8,128)S(1)} all-to-all(f32[32,8,768]{2,1,0:T(8,128)} %bitcast.67), channel_id=1, replica_groups=mesh['tile'=16,'query'=2,'dp'=8] {'tile','query'}, dimensions={0} | all-to-all | bytes 1572864 | tf_op jit(solution)/shard_map/all_to_all | solution.py:43
  117.0 0.0 copy-start.3
  117.0 0.1 reduce_sum.77
  117.1 16.5 %all_to_all.21 = f32[8,8,640]{2,1,0:T(8,128)S(1)} all-to-all(f32[8,8,640]{2,1,0:T(8,128)S(1)} %broadcast_in_dim.43), channel_id=1, replica_groups=mesh['tile'=16,'query'=2,'dp'=8] {'dp'}, dimensions={0} | all-to-all | bytes 327680 | tf_op jit(solution)/shard_map/all_to_all | solution.py:49
  133.6 0.9 broadcast_in_dim.44
  134.5 5.9 %all-to-all-start.3 = ((f32[32,8,640]{2,1,0:T(8,128)}), f32[32,8,640]{2,1,0:T(8,128)S(1)}, u32[]{:S(2)}, u32[]{:S(2)}) async-start(f32[32,8,640]{2,1,0:T(8,128)} %broadcast_in_dim.44), calls=%async_computation.3 | async-start | bytes 1310720 | tf_op jit(solution)/shard_map/all_to_all | solution.py:36
  140.4 0.0 copy-done.3
  140.4 3.7 %fusion.10 = bf16[1,4096,256]{2,1,0:T(8,128)(2,1)} fusion(bf16[4096,256]{1,0:T(8,128)(2,1)} %copy-done.1, bf16[256,256]{1,0:T(8,128)(2,1)S(1)} %copy-done.3), kind=kOutput, calls=%fused_computation.15 | convolution fusion | flops 537919488 | bytes 4325376 | tf_op jit(solution)/shard_map/dot_general | solution.py:28
  144.1 0.1 reshape.262
  144.2 1.2 fusion
  145.4 0.1 sub.45
  145.5 0.8 fusion.25
  146.2 7.0 %all-to-all-done.3 = f32[32,8,640]{2,1,0:T(8,128)S(1)} async-done(((f32[32,8,640]{2,1,0:T(8,128)}), f32[32,8,640]{2,1,0:T(8,128)S(1)}, u32[]{:S(2)}, u32[]{:S(2)}) %all-to-all-start.3) | async-done | bytes 655392 | tf_op jit(solution)/shard_map/all_to_all | solution.py:36
  153.3 0.7 slice.117
  153.9 0.8 fusion.64
  (12 shorter events, 0.1 us)
Async XLA Ops:
  0.6 14.9 %copy-start = (bf16[1,4096,256]{2,1,0:T(8,128)(2,1)S(1)}, bf16[1,4096,256]{2,1,0:T(8,128)(2,1)}, u32[]{:S(2)}) copy-start(bf16[1,4096,256]{2,1,0:T(8,128)(2,1)} %param.10) | copy-start | bytes 6291460
  4.7 39.6 %all-to-all-start = ((bf16[32,8,896]{2,1,0:T(8,128)(2,1)}), bf16[32,8,896]{2,1,0:T(8,128)(2,1)S(1)}, u32[]{:S(2)}, u32[]{:S(2)}) async-start(bf16[32,8,896]{2,1,0:T(8,128)(2,1)} %broadcast_in_dim.36), calls=%async_computation | async-start | bytes 917504 | tf_op jit(solution)/shard_map/all_to_all | solution.py:36
  37.8 6.5 %copy-start.4 = (f32[1,4,2048]{2,1,0:T(4,128)S(1)}, f32[1,4,2048]{2,1,0:T(4,128)}, u32[]{:S(2)}) copy-start(f32[1,4,2048]{2,1,0:T(4,128)} %param.18) | copy-start | bytes 98308
  37.8 6.5 %copy-start.2 = (bf16[256,128]{1,0:T(8,128)(2,1)S(1)}, bf16[256,128]{1,0:T(8,128)(2,1)}, u32[]{:S(2)}) copy-start(bf16[256,128]{1,0:T(8,128)(2,1)} %param.14) | copy-start | bytes 196612
  92.8 1.4 copy-start.1
  117.0 23.4 %copy-start.3 = (bf16[256,256]{1,0:T(8,128)(2,1)S(1)}, bf16[256,256]{1,0:T(8,128)(2,1)}, u32[]{:S(2)}) copy-start(bf16[256,256]{1,0:T(8,128)(2,1)} %param.13) | copy-start | bytes 393220
  134.5 18.8 %all-to-all-start.3 = ((f32[32,8,640]{2,1,0:T(8,128)}), f32[32,8,640]{2,1,0:T(8,128)S(1)}, u32[]{:S(2)}, u32[]{:S(2)}) async-start(f32[32,8,640]{2,1,0:T(8,128)} %broadcast_in_dim.44), calls=%async_computation.3 | async-start | bytes 1310720 | tf_op jit(solution)/shard_map/all_to_all | solution.py:36

commit v9 on v8

--- a/solution.py
+++ b/solution.py
@@ -121,12 +121,12 @@
         [padded[offset : offset + token_count] for offset in offsets], axis=1
     )
     base_row = slot_rows[0, 0]
-    picked_all = row_major(corner_table[base_row]).astype(jnp.float32)
+    picked_all = row_major(corner_table[base_row])
     mixed_rows = jnp.zeros((capacity, width), jnp.float32)
     contributions = []
     for corner in range(4):
         bilinear = slot_bilinear[0, corner]
-        picked = picked_all[:, corner * width : (corner + 1) * width]
+        picked = picked_all[:, corner * width : (corner + 1) * width].astype(jnp.float32)
         mixed_rows = mixed_rows + bilinear[:, None] * picked
         contributions.append((weight * bilinear)[:, None] * slot_grad)
     corner_dots = jnp.sum(mixed_rows * slot_grad, axis=1)

time: 156 us -> 148 us (0.949)
  other arithmetic: 46.9 us -> 40.4 us
    convert_element_type x1 -> x0, other arithmetic: 6.49 us -> none  [local(): picked_all = row_major(corner_table[base_row]).astype(jnp.float32)]
  transfers between devices with their start and end apart: 2 -> 2, of which waited for: 1 -> 1; matrix products, arithmetic and copies ran while one was open for 23% -> 20% of each run, Pallas kernels for 0% -> 0%
where the time goes in v9:
time: 148 us; the launch traced here: 147 us
  other arithmetic  40.4 us (27%)
  blocking collectives  38.1 us (26%)
  matrix products  23.7 us (16%)
  local copies, waits for them, and re-layouts  22.2 us (15%)
  starting transfers between devices  14.5 us (10%)
  waiting for transfers between devices  7.03 us (5%)
  between operations  1.52 us (1%)
    scatter-add x1, other arithmetic, local(): corner_sums = jnp.zeros((token_count + margin, 4 * width), jnp.float32).a...  25.7 us
    all_to_all x1, blocking collectives, scatter_sum_rows(): return jnp.sum(lax.all_to_all(pieces, axes, 0, 0, tiled=True), axis=0)  21.6 us
    all_to_all x1, blocking collectives, sum_everywhere(): block = jnp.sum(lax.all_to_all(copies, 'dp', 0, 0, tiled=True), axis=0)  16.5 us
    gather x1, local copies, waits for them, and re-layouts, local(): picked_all = row_major(corner_table[base_row])  15.5 us
    all_to_all x2, starting transfers between devices, gather_rows(): gathered = lax.all_to_all(copies, axes, 0, 0, tiled=True)  14.5 us
    dot_general x1, matrix products, local(): jnp.dot(query_onehot, every_grad, preferred_element_type=jnp.float32)  9.37 us
    convert_element_type x1, other arithmetic, local(): value_rounded = value_grad.astype(jnp.bfloat16)  7.05 us
    all_to_all x2, waiting for transfers between devices, gather_rows(): gathered = lax.all_to_all(copies, axes, 0, 0, tiled=True)  7.03 us
  transfers between devices with their start and end apart: 2, of which 1 were waited for; matrix products, arithmetic and copies ran while one was open for 20% of the time, Pallas kernels for 0%

profile of v9, /device:TPU:1, one launch (start us, length us, event | category | flops | bytes accessed | tf_op | source)
XLA Modules:
  0.0 147.4 jit_solution(7337888356125373574)
XLA Ops:
  0.6 0.0 copy-start
  0.6 1.1 convolution_exponential_fusion.1
  1.8 0.1 reshape.257
  1.9 0.1 reduce_sum.72
  1.9 0.1 div.61
  2.0 0.1 div.62
  2.1 1.1 convolution_convert_fusion.3
  3.2 0.7 pad_maximum_fusion.2
  3.9 0.8 broadcast_in_dim.36
  4.7 8.6 %all-to-all-start = ((bf16[32,8,896]{2,1,0:T(8,128)(2,1)}), bf16[32,8,896]{2,1,0:T(8,128)(2,1)S(1)}, u32[]{:S(2)}, u32[]{:S(2)}) async-start(bf16[32,8,896]{2,1,0:T(8,128)(2,1)} %broadcast_in_dim.36), calls=%async_computation | async-start | bytes 917504 | tf_op jit(solution)/shard_map/all_to_all | solution.py:36
  14.0 0.8 compare_select_fusion.2
  14.8 0.7 add_select_fusion.2
  15.5 0.0 copy-done
  15.5 1.6 %convolution_convert_fusion = bf16[4096,256]{1,0:T(8,128)(2,1)S(1)} fusion(bf16[256,256]{1,0:T(8,128)(2,1)} %param.13, bf16[1,4096,256]{2,1,0:T(8,128)(2,1)S(1)} %copy-done), kind=kOutput, calls=%fused_computation.13 | convolution fusion | flops 537919488 | bytes 4325376 | tf_op jit(solution)/shard_map/dot_general | solution.py:99
  17.1 1.3 pad_slice_fusion.2
  18.4 3.9 %pad_maximum_fusion = bf16[4096,1024]{1,0:T(8,128)(2,1)} fusion(bf16[4096,256]{1,0:T(8,128)(2,1)S(1)} %get-tuple-element.17, bf16[4096,256]{1,0:T(8,128)(2,1)S(1)} %get-tuple-element.16, bf16[4096,256]{1,0:T(8,128)(2,1)S(1)} %get-tuple-element.15, bf16[4096,256]{1,0:T(8,128)(2,1)S(1)} %convolution_convert_fusion), kind=kLoop, calls=%fused_computation.12 | loop fusion | flops 33554432 | bytes 16777216 | tf_op jit(solution)/shard_map/concatenate | solution.py:120
  22.4 0.0 copy-start.4
  22.4 0.0 copy-start.2
  22.4 15.5 %gather_fusion = bf16[2048,1024]{1,0:T(8,128)(2,1)} fusion(bf16[4096,1024]{1,0:T(8,128)(2,1)} %pad_maximum_fusion, s32[2048]{0:T(1024)S(1)} %broadcast_clamp_fusion), kind=kCustom, calls=%fused_computation | custom fusion | bytes 8396800 | tf_op jit(solution)/shard_map/gather | solution.py:124
  37.9 0.0 copy-done.4
  37.9 0.0 all-to-all-done
  37.9 0.0 copy-done.2
  37.9 0.2 bitcast_reduce_fusion
  38.2 0.7 fusion.18
  38.9 9.4 %multiply_reduce_fusion = (f32[2048]{0:T(1024)S(1)}, f32[2048,256]{1,0:T(8,128)S(1)}, f32[2048,256]{1,0:T(8,128)}, f32[2048,256]{1,0:T(8,128)}, f32[2048,256]{1,0:T(8,128)}, /*index=5*/f32[2048,256]{1,0:T(8,128)}) fusion(bf16[2048,1024]{1,0:T(8,128)(2,1)} %gather_fusion, f32[2048]{0:T(1024)S(1)} %bitcast.79, f32[2048]{0:T(1024)S(1)} %bitcast.81, ...), kind=kOutput, calls=%fused_computation.28 | convolution fusion | flops 278919168 | bytes 14902272 | tf_op jit(solution)/shard_map/dot_general | solution.py:116
  48.2 2.7 %fusion.12 = f32[256,256]{1,0:T(8,128)S(1)} fusion(f32[2048,256]{1,0:T(8,128)S(1)} %get-tuple-element.6, f32[2048]{0:T(1024)S(1)} %get-tuple-element.8, s32[256]{0:T(256)S(1)} %and_select_fusion, s32[2048]{0:T(1024)S(1)} %get-tuple-element.31, s32[2048]{0:T(1024)S(1)} %get-tuple-element.30), kind=kOutput, calls=%fused_computation.23 | convolution fusion | flops 1612709888 | bytes 2384896 | tf_op jit(solution)/shard_map/dot_general | solution.py:18
  51.0 1.2 fusion.43
  52.2 0.2 fusion.44
  52.4 0.3 fusion.38
  52.7 25.7 %scatter_custom_fusion = f32[4161,1024]{1,0:T(8,128)} fusion(s32[2048]{0:T(1024)S(1)} %bitcast.86, f32[]{:T(128)} %constant.53.clone.1, f32[2048,256]{1,0:T(8,128)} %get-tuple-element.11, f32[]{:T(128)} %constant.78, f32[2048,256]{1,0:T(8,128)} %get-tuple-element.12, f32[2048,256]{1,0:T(8,128)} %get-tuple-element.13, f32[2048,256]{1,0:T(8,128)} %get-tuple-element.14), kind=kCustom, calls=%fused_computation.3 | custom fusion | flops 8388608 | bytes 25432072 | tf_op jit(solution)/shard_map/scatter-add | solution.py:137
  78.4 7.0 %fusion.11 = bf16[4096,256]{1,0:T(8,128)(2,1)S(1)} fusion(f32[4161,1024]{1,0:T(8,128)} %scatter_custom_fusion), kind=kLoop, calls=%fused_computation.17 | loop fusion | flops 4194304 | bytes 18874368 | tf_op jit(solution)/shard_map/convert_element_type | solution.py:146
  85.5 0.0 copy-start.1
  85.5 0.7 fusion.19
  86.2 0.6 copy-done.1
  86.8 0.1 maximum_multiply_fusion
  86.9 0.1 pad_maximum_fusion.1
  86.9 1.1 copy.16
  88.1 21.6 %all_to_all.20 = f32[32,8,768]{2,1,0:T(8,128)S(1)} all-to-all(f32[32,8,768]{2,1,0:T(8,128)} %bitcast.67), channel_id=1, replica_groups=mesh['tile'=16,'query'=2,'dp'=8] {'tile','query'}, dimensions={0} | all-to-all | bytes 1572864 | tf_op jit(solution)/shard_map/all_to_all | solution.py:43
  109.7 0.0 copy-start.3
  109.7 0.1 reduce_sum.77
  109.8 16.5 %all_to_all.21 = f32[8,8,640]{2,1,0:T(8,128)S(1)} all-to-all(f32[8,8,640]{2,1,0:T(8,128)S(1)} %broadcast_in_dim.43), channel_id=1, replica_groups=mesh['tile'=16,'query'=2,'dp'=8] {'dp'}, dimensions={0} | all-to-all | bytes 327680 | tf_op jit(solution)/shard_map/all_to_all | solution.py:49
  126.3 0.9 broadcast_in_dim.44
  127.2 5.9 %all-to-all-start.3 = ((f32[32,8,640]{2,1,0:T(8,128)}), f32[32,8,640]{2,1,0:T(8,128)S(1)}, u32[]{:S(2)}, u32[]{:S(2)}) async-start(f32[32,8,640]{2,1,0:T(8,128)} %broadcast_in_dim.44), calls=%async_computation.3 | async-start | bytes 1310720 | tf_op jit(solution)/shard_map/all_to_all | solution.py:36
  133.1 0.0 copy-done.3
  133.1 3.7 %fusion.10 = bf16[1,4096,256]{2,1,0:T(8,128)(2,1)} fusion(bf16[4096,256]{1,0:T(8,128)(2,1)} %copy-done.1, bf16[256,256]{1,0:T(8,128)(2,1)S(1)} %copy-done.3), kind=kOutput, calls=%fused_computation.15 | convolution fusion | flops 537919488 | bytes 4325376 | tf_op jit(solution)/shard_map/dot_general | solution.py:28
  136.8 0.1 reshape.262
  136.8 1.2 fusion
  138.0 0.1 sub.45
  138.1 0.8 fusion.22
  138.9 7.0 %all-to-all-done.3 = f32[32,8,640]{2,1,0:T(8,128)S(1)} async-done(((f32[32,8,640]{2,1,0:T(8,128)}), f32[32,8,640]{2,1,0:T(8,128)S(1)}, u32[]{:S(2)}, u32[]{:S(2)}) %all-to-all-start.3) | async-done | bytes 655392 | tf_op jit(solution)/shard_map/all_to_all | solution.py:36
  145.9 0.7 slice.117
  146.6 0.8 fusion.60
  (12 shorter events, 0.1 us)
Async XLA Ops:
  0.6 14.9 %copy-start = (bf16[1,4096,256]{2,1,0:T(8,128)(2,1)S(1)}, bf16[1,4096,256]{2,1,0:T(8,128)(2,1)}, u32[]{:S(2)}) copy-start(bf16[1,4096,256]{2,1,0:T(8,128)(2,1)} %param.10) | copy-start | bytes 6291460
  4.7 33.2 %all-to-all-start = ((bf16[32,8,896]{2,1,0:T(8,128)(2,1)}), bf16[32,8,896]{2,1,0:T(8,128)(2,1)S(1)}, u32[]{:S(2)}, u32[]{:S(2)}) async-start(bf16[32,8,896]{2,1,0:T(8,128)(2,1)} %broadcast_in_dim.36), calls=%async_computation | async-start | bytes 917504 | tf_op jit(solution)/shard_map/all_to_all | solution.py:36
  22.4 15.5 %copy-start.4 = (f32[1,4,2048]{2,1,0:T(4,128)S(1)}, f32[1,4,2048]{2,1,0:T(4,128)}, u32[]{:S(2)}) copy-start(f32[1,4,2048]{2,1,0:T(4,128)} %param.18) | copy-start | bytes 98308
  22.4 15.5 %copy-start.2 = (bf16[256,128]{1,0:T(8,128)(2,1)S(1)}, bf16[256,128]{1,0:T(8,128)(2,1)}, u32[]{:S(2)}) copy-start(bf16[256,128]{1,0:T(8,128)(2,1)} %param.14) | copy-start | bytes 196612
  85.5 1.4 copy-start.1
  109.7 23.4 %copy-start.3 = (bf16[256,256]{1,0:T(8,128)(2,1)S(1)}, bf16[256,256]{1,0:T(8,128)(2,1)}, u32[]{:S(2)}) copy-start(bf16[256,256]{1,0:T(8,128)(2,1)} %param.13) | copy-start | bytes 393220
  127.2 18.8 %all-to-all-start.3 = ((f32[32,8,640]{2,1,0:T(8,128)}), f32[32,8,640]{2,1,0:T(8,128)S(1)}, u32[]{:S(2)}, u32[]{:S(2)}) async-start(f32[32,8,640]{2,1,0:T(8,128)} %broadcast_in_dim.44), calls=%async_computation.3 | async-start | bytes 1310720 | tf_op jit(solution)/shard_map/all_to_all | solution.py:36

commit v10 on v9

--- a/solution.py
+++ b/solution.py
@@ -86,16 +86,18 @@
     attention = (exponent / jnp.sum(exponent, axis=2, keepdims=True)).reshape(
         local_queries, att_width
     )
-    attn_rounded = attention.astype(jnp.bfloat16)
     sample_grad = times_transpose(out_grad[0], out_weight).astype(jnp.bfloat16)
     every_both = gather_rows(
-        jnp.concatenate([sample_grad, attn_rounded, out_grad[0], queries[0]], axis=1),
-        ("tile", "query"),
+        jnp.concatenate([sample_grad, out_grad[0], queries[0]], axis=1), ("tile", "query")
     )
     every_grad = every_both[:, :width]
-    every_attn = every_both[:, width : width + att_width]
-    every_out = every_both[:, width + att_width : 2 * width + att_width]
-    every_queries = every_both[:, 2 * width + att_width :]
+    every_out = every_both[:, width : 2 * width]
+    every_queries = every_both[:, 2 * width :]
+    page_exponent = jnp.exp(
+        jnp.dot(every_queries, attn_weight, preferred_element_type=jnp.float32)
+    ).reshape(all_queries, HEADS, per_head)
+    page_attention = page_exponent / jnp.sum(page_exponent, axis=2, keepdims=True)
+    every_attn = page_attention.reshape(all_queries, att_width).astype(jnp.bfloat16)
     projected = jnp.dot(features[0], value_weight, preferred_element_type=jnp.float32).astype(
         jnp.bfloat16
     )
@@ -156,10 +158,6 @@
     )
     attn_part = over_rows_exact(query_float, dots_table)
     out_term = over_rows_exact(sampled_part, every_out.astype(jnp.float32))
-    page_exponent = jnp.exp(
-        jnp.dot(every_queries, attn_weight, preferred_element_type=jnp.float32)
-    ).reshape(all_queries, HEADS, per_head)
-    page_attention = page_exponent / jnp.sum(page_exponent, axis=2, keepdims=True)
     part_three = attn_part.reshape(all_queries, HEADS, per_head)
     part_logits = (
         page_attention

time: 148 us -> 148 us (level)
  other arithmetic: 40.4 us -> 44.4 us
  matrix products: 23.7 us -> 20.2 us
    mul x2 -> x3, other arithmetic: 0.01 us -> 3.96 us  [local(): contributions.append((weight * bilinear)[:, None] * slot_grad)]
    dot_general x1, matrix products: 9.37 us -> 6.69 us  [local(): jnp.dot(query_onehot, every_grad, preferred_element_type=jnp.float32)]
where the time goes in v10:
time: 148 us; the launch traced here: 147 us
  other arithmetic  44.4 us (30%)
  blocking collectives  38.1 us (26%)
  local copies, waits for them, and re-layouts  22.1 us (15%)
  matrix products  20.2 us (14%)
  starting transfers between devices  14.5 us (10%)
  waiting for transfers between devices  6.56 us (4%)
  between operations  1.52 us (1%)
    scatter-add x1, other arithmetic, local(): corner_sums = jnp.zeros((token_count + margin, 4 * width), jnp.float32).a...  25.7 us
    all_to_all x1, blocking collectives, scatter_sum_rows(): return jnp.sum(lax.all_to_all(pieces, axes, 0, 0, tiled=True), axis=0)  21.6 us
    all_to_all x1, blocking collectives, sum_everywhere(): block = jnp.sum(lax.all_to_all(copies, 'dp', 0, 0, tiled=True), axis=0)  16.5 us
    gather x1, local copies, waits for them, and re-layouts, local(): picked_all = row_major(corner_table[base_row])  15.5 us
    all_to_all x2, starting transfers between devices, gather_rows(): gathered = lax.all_to_all(copies, axes, 0, 0, tiled=True)  14.5 us
    convert_element_type x1, other arithmetic, local(): value_rounded = value_grad.astype(jnp.bfloat16)  7.05 us
    dot_general x1, matrix products, local(): jnp.dot(query_onehot, every_grad, preferred_element_type=jnp.float32)  6.69 us
    all_to_all x2, waiting for transfers between devices, gather_rows(): gathered = lax.all_to_all(copies, axes, 0, 0, tiled=True)  6.56 us
  transfers between devices with their start and end apart: 2, of which 1 were waited for; matrix products, arithmetic and copies ran while one was open for 20% of the time, Pallas kernels for 0%

profile of v10, /device:TPU:1, one launch (start us, length us, event | category | flops | bytes accessed | tf_op | source)
XLA Modules:
  0.0 147.4 jit_solution(12554447810795468851)
XLA Ops:
  0.6 0.0 copy-start
  0.6 1.2 convolution_convert_fusion.3
  1.9 0.7 pad_maximum_fusion.2
  2.6 0.8 broadcast_in_dim.32
  3.4 8.6 %all-to-all-start = ((bf16[32,8,768]{2,1,0:T(8,128)(2,1)}), bf16[32,8,768]{2,1,0:T(8,128)(2,1)S(1)}, u32[]{:S(2)}, u32[]{:S(2)}) async-start(bf16[32,8,768]{2,1,0:T(8,128)(2,1)} %broadcast_in_dim.32), calls=%async_computation | async-start | bytes 786432 | tf_op jit(solution)/shard_map/all_to_all | solution.py:36
  12.6 0.8 compare_select_fusion.2
  13.4 0.7 add_select_fusion.2
  14.1 0.0 copy-done
  14.2 1.6 %convolution_convert_fusion = bf16[4096,256]{1,0:T(8,128)(2,1)S(1)} fusion(bf16[256,256]{1,0:T(8,128)(2,1)} %param.13, bf16[1,4096,256]{2,1,0:T(8,128)(2,1)S(1)} %copy-done), kind=kOutput, calls=%fused_computation.13 | convolution fusion | flops 537919488 | bytes 4325376 | tf_op jit(solution)/shard_map/dot_general | solution.py:101
  15.8 1.3 pad_slice_fusion.2
  17.1 3.9 %pad_maximum_fusion = bf16[4096,1024]{1,0:T(8,128)(2,1)} fusion(bf16[4096,256]{1,0:T(8,128)(2,1)S(1)} %get-tuple-element.17, bf16[4096,256]{1,0:T(8,128)(2,1)S(1)} %get-tuple-element.16, bf16[4096,256]{1,0:T(8,128)(2,1)S(1)} %get-tuple-element.15, bf16[4096,256]{1,0:T(8,128)(2,1)S(1)} %convolution_convert_fusion), kind=kLoop, calls=%fused_computation.12 | loop fusion | flops 33554432 | bytes 16777216 | tf_op jit(solution)/shard_map/concatenate | solution.py:122
  21.0 0.0 copy-start.4
  21.0 0.0 copy-start.2
  21.0 15.5 %gather_fusion = bf16[2048,1024]{1,0:T(8,128)(2,1)} fusion(bf16[4096,1024]{1,0:T(8,128)(2,1)} %pad_maximum_fusion, s32[2048]{0:T(1024)S(1)} %broadcast_clamp_fusion), kind=kCustom, calls=%fused_computation | custom fusion | bytes 8396800 | tf_op jit(solution)/shard_map/gather | solution.py:126
  36.5 0.0 copy-done.4
  36.6 0.0 all-to-all-done
  36.6 0.0 copy-done.2
  36.6 0.2 bitcast_reduce_fusion
  36.8 6.7 %multiply_reduce_fusion = (f32[2048]{0:T(1024)S(1)}, f32[2048,256]{1,0:T(8,128)S(1)}, f32[2048,256]{1,0:T(8,128)S(1)}) fusion(bf16[2048,1024]{1,0:T(8,128)(2,1)} %gather_fusion, f32[2048]{0:T(1024)S(1)} %bitcast.77, f32[2048]{0:T(1024)S(1)} %bitcast.79, f32[2048]{0:T(1024)S(1)} %bitcast.75, f32[2048]{0:T(1024)S(1)} %bitcast.81, ...), kind=kOutput, calls=%fused_computation.28 | convolution fusion | flops 276822016 | bytes 8578048 | tf_op jit(solution)/shard_map/dot_general | solution.py:118
  43.5 1.2 fusion.43
  44.7 0.2 fusion.44
  45.0 0.7 fusion.18
  45.7 2.7 %fusion.12 = f32[256,256]{1,0:T(8,128)S(1)} fusion(f32[2048,256]{1,0:T(8,128)S(1)} %get-tuple-element.8, f32[2048]{0:T(1024)S(1)} %get-tuple-element.10, s32[256]{0:T(256)S(1)} %and_select_fusion, s32[2048]{0:T(1024)S(1)} %get-tuple-element.31, s32[2048]{0:T(1024)S(1)} %get-tuple-element.30), kind=kOutput, calls=%fused_computation.23 | convolution fusion | flops 1612709888 | bytes 2384896 | tf_op jit(solution)/shard_map/dot_general | solution.py:18
  48.4 0.3 fusion.38
  48.7 3.9 %broadcast_multiply_fusion.3 = (f32[2048,256]{1,0:T(8,128)}, f32[2048,256]{1,0:T(8,128)}, f32[2048,256]{1,0:T(8,128)}, f32[2048,256]{1,0:T(8,128)}) fusion(f32[2048,256]{1,0:T(8,128)S(1)} %get-tuple-element.32, f32[2048]{0:T(1024)S(1)} %get-tuple-element.9, f32[2048]{0:T(1024)S(1)} %get-tuple-element.27, f32[2048]{0:T(1024)S(1)} %get-tuple-element.28, ...), kind=kLoop, calls=%fused_computation.49 | loop fusion | flops 2097152 | bytes 10518528 | tf_op jit(solution)/shard_map/mul | solution.py:133
  52.7 25.7 %scatter_custom_fusion = f32[4161,1024]{1,0:T(8,128)} fusion(s32[2048]{0:T(1024)S(1)} %bitcast.85, f32[]{:T(128)} %constant.53.clone.1, f32[2048,256]{1,0:T(8,128)} %get-tuple-element.12, f32[]{:T(128)} %constant.78, f32[2048,256]{1,0:T(8,128)} %get-tuple-element.13, f32[2048,256]{1,0:T(8,128)} %get-tuple-element.14, f32[2048,256]{1,0:T(8,128)} %get-tuple-element.11), kind=kCustom, calls=%fused_computation.3 | custom fusion | flops 8388608 | bytes 25432072 | tf_op jit(solution)/shard_map/scatter-add | solution.py:139
  78.3 7.0 %fusion.11 = bf16[4096,256]{1,0:T(8,128)(2,1)S(1)} fusion(f32[4161,1024]{1,0:T(8,128)} %scatter_custom_fusion), kind=kLoop, calls=%fused_computation.17 | loop fusion | flops 4194304 | bytes 18874368 | tf_op jit(solution)/shard_map/convert_element_type | solution.py:148
  85.4 0.0 copy-start.1
  85.4 0.7 fusion.19
  86.1 0.6 copy-done.1
  86.7 0.1 maximum_multiply_fusion
  86.8 0.1 pad_maximum_fusion.1
  86.8 1.1 copy.16
  88.0 21.6 %all_to_all.20 = f32[32,8,768]{2,1,0:T(8,128)S(1)} all-to-all(f32[32,8,768]{2,1,0:T(8,128)} %bitcast.67), channel_id=1, replica_groups=mesh['tile'=16,'query'=2,'dp'=8] {'tile','query'}, dimensions={0} | all-to-all | bytes 1572864 | tf_op jit(solution)/shard_map/all_to_all | solution.py:43
  109.6 0.0 copy-start.5
  109.6 0.0 copy-start.3
  109.6 0.1 reduce_sum.77
  109.7 16.5 %all_to_all.21 = f32[8,8,640]{2,1,0:T(8,128)S(1)} all-to-all(f32[8,8,640]{2,1,0:T(8,128)S(1)} %broadcast_in_dim.43), channel_id=1, replica_groups=mesh['tile'=16,'query'=2,'dp'=8] {'dp'}, dimensions={0} | all-to-all | bytes 327680 | tf_op jit(solution)/shard_map/all_to_all | solution.py:49
  126.2 0.9 broadcast_in_dim.44
  127.1 5.9 %all-to-all-start.3 = ((f32[32,8,640]{2,1,0:T(8,128)}), f32[32,8,640]{2,1,0:T(8,128)S(1)}, u32[]{:S(2)}, u32[]{:S(2)}) async-start(f32[32,8,640]{2,1,0:T(8,128)} %broadcast_in_dim.44), calls=%async_computation.3 | async-start | bytes 1310720 | tf_op jit(solution)/shard_map/all_to_all | solution.py:36
  133.0 0.0 copy-done.5
  133.0 0.1 convolution_exponential_fusion.1
  133.2 0.1 reshape.259
  133.2 0.1 reduce_sum.74
  133.3 0.1 div.70
  133.4 0.1 div.71
  133.5 0.0 copy-done.3
  133.5 3.7 %fusion.10 = bf16[1,4096,256]{2,1,0:T(8,128)(2,1)} fusion(bf16[4096,256]{1,0:T(8,128)(2,1)} %copy-done.1, bf16[256,256]{1,0:T(8,128)(2,1)S(1)} %copy-done.3), kind=kOutput, calls=%fused_computation.15 | convolution fusion | flops 537919488 | bytes 4325376 | tf_op jit(solution)/shard_map/dot_general | solution.py:28
  137.2 0.1 reshape.262
  137.2 1.2 fusion
  138.4 0.1 sub.45
  138.5 0.8 fusion.22
  139.3 6.6 %all-to-all-done.3 = f32[32,8,640]{2,1,0:T(8,128)S(1)} async-done(((f32[32,8,640]{2,1,0:T(8,128)}), f32[32,8,640]{2,1,0:T(8,128)S(1)}, u32[]{:S(2)}, u32[]{:S(2)}) %all-to-all-start.3) | async-done | bytes 655392 | tf_op jit(solution)/shard_map/all_to_all | solution.py:36
  145.9 0.7 slice.112
  146.5 0.8 fusion.59
  (11 shorter events, 0.1 us)
Async XLA Ops:
  0.6 13.5 %copy-start = (bf16[1,4096,256]{2,1,0:T(8,128)(2,1)S(1)}, bf16[1,4096,256]{2,1,0:T(8,128)(2,1)}, u32[]{:S(2)}) copy-start(bf16[1,4096,256]{2,1,0:T(8,128)(2,1)} %param.10) | copy-start | bytes 6291460
  3.4 33.2 %all-to-all-start = ((bf16[32,8,768]{2,1,0:T(8,128)(2,1)}), bf16[32,8,768]{2,1,0:T(8,128)(2,1)S(1)}, u32[]{:S(2)}, u32[]{:S(2)}) async-start(bf16[32,8,768]{2,1,0:T(8,128)(2,1)} %broadcast_in_dim.32), calls=%async_computation | async-start | bytes 786432 | tf_op jit(solution)/shard_map/all_to_all | solution.py:36
  21.0 15.5 %copy-start.4 = (f32[1,4,2048]{2,1,0:T(4,128)S(1)}, f32[1,4,2048]{2,1,0:T(4,128)}, u32[]{:S(2)}) copy-start(f32[1,4,2048]{2,1,0:T(4,128)} %param.18) | copy-start | bytes 98308
  21.0 15.5 %copy-start.2 = (bf16[256,128]{1,0:T(8,128)(2,1)S(1)}, bf16[256,128]{1,0:T(8,128)(2,1)}, u32[]{:S(2)}) copy-start(bf16[256,128]{1,0:T(8,128)(2,1)} %param.14) | copy-start | bytes 196612
  85.4 1.4 copy-start.1
  109.6 23.4 %copy-start.5 = (bf16[1,8,256]{2,1,0:T(8,128)(2,1)S(1)}, bf16[1,8,256]{2,1,0:T(8,128)(2,1)}, u32[]{:S(2)}) copy-start(bf16[1,8,256]{2,1,0:T(8,128)(2,1)} %param.11) | copy-start | bytes 12292
  109.6 23.9 %copy-start.3 = (bf16[256,256]{1,0:T(8,128)(2,1)S(1)}, bf16[256,256]{1,0:T(8,128)(2,1)}, u32[]{:S(2)}) copy-start(bf16[256,256]{1,0:T(8,128)(2,1)} %param.13) | copy-start | bytes 393220
  127.1 18.8 %all-to-all-start.3 = ((f32[32,8,640]{2,1,0:T(8,128)}), f32[32,8,640]{2,1,0:T(8,128)S(1)}, u32[]{:S(2)}, u32[]{:S(2)}) async-start(f32[32,8,640]{2,1,0:T(8,128)} %broadcast_in_dim.44), calls=%async_computation.3 | async-start | bytes 1310720 | tf_op jit(solution)/shard_map/all_to_all | solution.py:36

commit v11 on v10

--- a/solution.py
+++ b/solution.py
@@ -111,11 +111,16 @@
     query_match = query_index[:, None] == jnp.arange(all_queries, dtype=jnp.int32)[None, :]
     query_onehot = query_match.astype(jnp.bfloat16)
     column_match = attn_column[:, None] == jnp.arange(att_width, dtype=jnp.int32)[None, :]
-    attn_rows = jnp.dot(query_onehot, every_attn, preferred_element_type=jnp.float32)
+    picked_rows = jnp.dot(
+        query_onehot,
+        jnp.concatenate([every_grad, every_attn], axis=1),
+        preferred_element_type=jnp.float32,
+    )
+    grad_rows = picked_rows[:, :width]
+    attn_rows = picked_rows[:, width:]
     picked_attn = jnp.sum(jnp.where(column_match, attn_rows, jnp.zeros((), jnp.float32)), axis=1)
     weight = jnp.where(alive_slot, picked_attn, jnp.zeros((), jnp.float32))
     head_mask = jnp.arange(width, dtype=jnp.int32)[None, :] // head_width == head_index[:, None]
-    grad_rows = jnp.dot(query_onehot, every_grad, preferred_element_type=jnp.float32)
     slot_grad = row_major(jnp.where(head_mask, grad_rows, jnp.zeros((), jnp.float32)))
     offsets = (0, 1, TILE_W, TILE_W + 1)
     padded = jnp.concatenate([projected, jnp.zeros((TILE_W + 1, width), jnp.bfloat16)], axis=0)

time: 148 us -> 152 us (1.027)
  matrix products: 20.2 us -> 13.6 us
  other arithmetic: 44.4 us -> 50.6 us
  local copies, waits for them, and re-layouts: 22.1 us -> 26.7 us
    reduce_sum x0 -> x2, other arithmetic: none -> 10.2 us  [the longest x1 10 us: local(): corner_dots = jnp.sum(mixed_rows * slot_grad, axis=1)]
    dot_general x2 -> x1, matrix products: 7.35 us -> 0.78 us  [local(): jnp.dot(query_onehot, jnp.concatenate([every_grad, every_attn], axis=1),...]
    mul x3 -> x2, other arithmetic: 3.96 us -> 0.01 us  [local(): contributions.append((weight * bilinear)[:, None] * slot_grad)]
    unnamed x12 -> x13, local copies, waits for them, and re-layouts: 0.62 us -> 3.56 us
where the time goes in v11:
time: 152 us
  other arithmetic  50.6 us (33%)
  blocking collectives  38.1 us (25%)
  local copies, waits for them, and re-layouts  26.7 us (18%)
  starting transfers between devices  14.5 us (10%)
  matrix products  13.6 us (9%)
  waiting for transfers between devices  6.57 us (4%)
  between operations  1.52 us (1%)
    scatter-add x1, other arithmetic, local(): corner_sums = jnp.zeros((token_count + margin, 4 * width), jnp.float32).a...  25.7 us
    all_to_all x1, blocking collectives, scatter_sum_rows(): return jnp.sum(lax.all_to_all(pieces, axes, 0, 0, tiled=True), axis=0)  21.6 us
    all_to_all x1, blocking collectives, sum_everywhere(): block = jnp.sum(lax.all_to_all(copies, 'dp', 0, 0, tiled=True), axis=0)  16.5 us
    gather x1, local copies, waits for them, and re-layouts, local(): picked_all = row_major(corner_table[base_row])  15.5 us
    all_to_all x2, starting transfers between devices, gather_rows(): gathered = lax.all_to_all(copies, axes, 0, 0, tiled=True)  14.5 us
    reduce_sum x1, other arithmetic, local(): corner_dots = jnp.sum(mixed_rows * slot_grad, axis=1)  10 us
    convert_element_type x1, other arithmetic, local(): value_rounded = value_grad.astype(jnp.bfloat16)  7.05 us
    all_to_all x2, waiting for transfers between devices, gather_rows(): gathered = lax.all_to_all(copies, axes, 0, 0, tiled=True)  6.57 us
  transfers between devices with their start and end apart: 2, of which 1 were waited for; matrix products, arithmetic and copies ran while one was open for 20% of the time, Pallas kernels for 0%

profile of v11, /device:TPU:1, one launch (start us, length us, event | category | flops | bytes accessed | tf_op | source)
XLA Modules:
  0.0 151.5 jit_solution(12578773145889840590)
XLA Ops:
  0.6 0.0 copy-start
  0.6 1.2 convolution_convert_fusion.3
  1.9 0.7 pad_maximum_fusion.2
  2.6 0.8 broadcast_in_dim.32
  3.4 8.6 %all-to-all-start = ((bf16[32,8,768]{2,1,0:T(8,128)(2,1)}), bf16[32,8,768]{2,1,0:T(8,128)(2,1)S(1)}, u32[]{:S(2)}, u32[]{:S(2)}) async-start(bf16[32,8,768]{2,1,0:T(8,128)(2,1)} %broadcast_in_dim.32), calls=%async_computation | async-start | bytes 786432 | tf_op jit(solution)/shard_map/all_to_all | solution.py:36
  12.6 0.8 compare_select_fusion.3
  13.4 0.7 add_select_fusion
  14.1 0.0 copy-done
  14.2 1.6 %convolution_convert_fusion = bf16[4096,256]{1,0:T(8,128)(2,1)S(1)} fusion(bf16[256,256]{1,0:T(8,128)(2,1)} %param.13, bf16[1,4096,256]{2,1,0:T(8,128)(2,1)S(1)} %copy-done), kind=kOutput, calls=%fused_computation.13 | convolution fusion | flops 537919488 | bytes 4325376 | tf_op jit(solution)/shard_map/dot_general | solution.py:101
  15.8 1.3 pad_slice_fusion.2
  17.1 3.9 %pad_maximum_fusion = bf16[4096,1024]{1,0:T(8,128)(2,1)} fusion(bf16[4096,256]{1,0:T(8,128)(2,1)S(1)} %get-tuple-element.15, bf16[4096,256]{1,0:T(8,128)(2,1)S(1)} %get-tuple-element.14, bf16[4096,256]{1,0:T(8,128)(2,1)S(1)} %get-tuple-element.13, bf16[4096,256]{1,0:T(8,128)(2,1)S(1)} %convolution_convert_fusion), kind=kLoop, calls=%fused_computation.12 | loop fusion | flops 33554432 | bytes 16777216 | tf_op jit(solution)/shard_map/concatenate | solution.py:127
  21.0 0.0 copy-start.4
  21.0 0.0 copy-start.2
  21.0 15.5 %gather_fusion = bf16[2048,1024]{1,0:T(8,128)(2,1)} fusion(bf16[4096,1024]{1,0:T(8,128)(2,1)} %pad_maximum_fusion, s32[2048]{0:T(1024)S(1)} %broadcast_clamp_fusion), kind=kCustom, calls=%fused_computation | custom fusion | bytes 8396800 | tf_op jit(solution)/shard_map/gather | solution.py:131
  36.5 0.0 copy-done.4
  36.6 0.0 all-to-all-done
  36.6 0.0 copy-done.2
  36.6 0.2 bitcast_reduce_fusion
  36.9 0.1 copy.20
  37.0 0.8 fusion.18
  37.8 1.5 slice.109
  39.2 0.1 fusion.27
  39.4 2.9 %copy.23 = f32[2048,256]{1,0:T(8,128)} copy(f32[2048,256]{0,1:T(8,128)} %slice.109) | data formatting | bytes 4194304
  42.3 10.0 %multiply_reduce_fusion = (f32[2048]{0:T(1024)S(1)}, f32[2048,256]{1,0:T(8,128)S(1)}, f32[2048,256]{1,0:T(8,128)}, f32[2048,256]{1,0:T(8,128)}, f32[2048,256]{1,0:T(8,128)}, /*index=5*/f32[2048,256]{1,0:T(8,128)}) fusion(f32[2048,256]{1,0:T(8,128)} %copy.23, s32[256]{0:T(256)S(1)} %and_select_fusion, s32[2048]{0:T(1024)S(1)} %get-tuple-element.27, ...), kind=kLoop, calls=%fused_computation.27 | loop fusion | flops 9959424 | bytes 16860160 | tf_op jit(solution)/shard_map/reduce_sum | solution.py:139
  52.3 2.7 %fusion.12 = f32[256,256]{1,0:T(8,128)S(1)} fusion(f32[2048,256]{1,0:T(8,128)S(1)} %get-tuple-element.6, f32[2048]{0:T(1024)S(1)} %get-tuple-element.8, s32[256]{0:T(256)S(1)} %and_select_fusion, s32[2048]{0:T(1024)S(1)} %get-tuple-element.28, s32[2048]{0:T(1024)S(1)} %get-tuple-element.27), kind=kOutput, calls=%fused_computation.22 | convolution fusion | flops 1612709888 | bytes 2384896 | tf_op jit(solution)/shard_map/dot_general | solution.py:18
  55.1 1.2 fusion.49
  56.3 0.2 fusion.50
  56.5 0.3 fusion.45
  56.8 25.7 %scatter_custom_fusion = f32[4161,1024]{1,0:T(8,128)} fusion(s32[2048]{0:T(1024)S(1)} %bitcast.87, f32[]{:T(128)} %constant.53.clone.1, f32[2048,256]{1,0:T(8,128)} %get-tuple-element.12, f32[]{:T(128)} %constant.78, f32[2048,256]{1,0:T(8,128)} %get-tuple-element.11, f32[2048,256]{1,0:T(8,128)} %get-tuple-element.10, f32[2048,256]{1,0:T(8,128)} %get-tuple-element.9), kind=kCustom, calls=%fused_computation.3 | custom fusion | flops 8388608 | bytes 25432072 | tf_op jit(solution)/shard_map/scatter-add | solution.py:144
  82.5 7.0 %fusion.11 = bf16[4096,256]{1,0:T(8,128)(2,1)S(1)} fusion(f32[4161,1024]{1,0:T(8,128)} %scatter_custom_fusion), kind=kLoop, calls=%fused_computation.17 | loop fusion | flops 4194304 | bytes 18874368 | tf_op jit(solution)/shard_map/convert_element_type | solution.py:153
  89.6 0.0 copy-start.1
  89.6 0.7 fusion.19
  90.3 0.6 copy-done.1
  90.9 0.1 maximum_multiply_fusion
  91.0 0.1 pad_maximum_fusion.1
  91.0 1.1 copy.22
  92.2 21.6 %all_to_all.20 = f32[32,8,768]{2,1,0:T(8,128)S(1)} all-to-all(f32[32,8,768]{2,1,0:T(8,128)} %bitcast.69), channel_id=1, replica_groups=mesh['tile'=16,'query'=2,'dp'=8] {'tile','query'}, dimensions={0} | all-to-all | bytes 1572864 | tf_op jit(solution)/shard_map/all_to_all | solution.py:43
  113.8 0.0 copy-start.5
  113.8 0.0 copy-start.3
  113.8 0.1 reduce_sum.77
  113.9 16.5 %all_to_all.21 = f32[8,8,640]{2,1,0:T(8,128)S(1)} all-to-all(f32[8,8,640]{2,1,0:T(8,128)S(1)} %broadcast_in_dim.43), channel_id=1, replica_groups=mesh['tile'=16,'query'=2,'dp'=8] {'dp'}, dimensions={0} | all-to-all | bytes 327680 | tf_op jit(solution)/shard_map/all_to_all | solution.py:49
  130.4 0.9 broadcast_in_dim.44
  131.3 5.9 %all-to-all-start.3 = ((f32[32,8,640]{2,1,0:T(8,128)}), f32[32,8,640]{2,1,0:T(8,128)S(1)}, u32[]{:S(2)}, u32[]{:S(2)}) async-start(f32[32,8,640]{2,1,0:T(8,128)} %broadcast_in_dim.44), calls=%async_computation.3 | async-start | bytes 1310720 | tf_op jit(solution)/shard_map/all_to_all | solution.py:36
  137.2 0.0 copy-done.5
  137.2 0.1 convolution_exponential_fusion.1
  137.3 0.1 reshape.259
  137.4 0.1 reduce_sum.74
  137.5 0.1 div.70
  137.6 0.1 div.71
  137.7 0.0 copy-done.3
  137.7 3.7 %fusion.10 = bf16[1,4096,256]{2,1,0:T(8,128)(2,1)} fusion(bf16[4096,256]{1,0:T(8,128)(2,1)} %copy-done.1, bf16[256,256]{1,0:T(8,128)(2,1)S(1)} %copy-done.3), kind=kOutput, calls=%fused_computation.15 | convolution fusion | flops 537919488 | bytes 4325376 | tf_op jit(solution)/shard_map/dot_general | solution.py:28
  141.3 0.1 reshape.262
  141.4 1.2 fusion
  142.6 0.1 sub.45
  142.7 0.8 fusion.22
  143.5 6.6 %all-to-all-done.3 = f32[32,8,640]{2,1,0:T(8,128)S(1)} async-done(((f32[32,8,640]{2,1,0:T(8,128)}), f32[32,8,640]{2,1,0:T(8,128)S(1)}, u32[]{:S(2)}, u32[]{:S(2)}) %all-to-all-start.3) | async-done | bytes 655392 | tf_op jit(solution)/shard_map/all_to_all | solution.py:36
  150.0 0.7 slice.122
  150.7 0.8 fusion.66
  (13 shorter events, 0.1 us)
Async XLA Ops:
  0.6 13.5 %copy-start = (bf16[1,4096,256]{2,1,0:T(8,128)(2,1)S(1)}, bf16[1,4096,256]{2,1,0:T(8,128)(2,1)}, u32[]{:S(2)}) copy-start(bf16[1,4096,256]{2,1,0:T(8,128)(2,1)} %param.10) | copy-start | bytes 6291460
  3.4 33.2 %all-to-all-start = ((bf16[32,8,768]{2,1,0:T(8,128)(2,1)}), bf16[32,8,768]{2,1,0:T(8,128)(2,1)S(1)}, u32[]{:S(2)}, u32[]{:S(2)}) async-start(bf16[32,8,768]{2,1,0:T(8,128)(2,1)} %broadcast_in_dim.32), calls=%async_computation | async-start | bytes 786432 | tf_op jit(solution)/shard_map/all_to_all | solution.py:36
  21.0 15.5 %copy-start.4 = (f32[1,4,2048]{2,1,0:T(4,128)S(1)}, f32[1,4,2048]{2,1,0:T(4,128)}, u32[]{:S(2)}) copy-start(f32[1,4,2048]{2,1,0:T(4,128)} %param.18) | copy-start | bytes 98308
  21.0 15.6 %copy-start.2 = (bf16[256,128]{1,0:T(8,128)(2,1)S(1)}, bf16[256,128]{1,0:T(8,128)(2,1)}, u32[]{:S(2)}) copy-start(bf16[256,128]{1,0:T(8,128)(2,1)} %param.14) | copy-start | bytes 196612
  89.6 1.4 copy-start.1
  113.8 23.4 %copy-start.5 = (bf16[1,8,256]{2,1,0:T(8,128)(2,1)S(1)}, bf16[1,8,256]{2,1,0:T(8,128)(2,1)}, u32[]{:S(2)}) copy-start(bf16[1,8,256]{2,1,0:T(8,128)(2,1)} %param.11) | copy-start | bytes 12292
  113.8 23.9 %copy-start.3 = (bf16[256,256]{1,0:T(8,128)(2,1)S(1)}, bf16[256,256]{1,0:T(8,128)(2,1)}, u32[]{:S(2)}) copy-start(bf16[256,256]{1,0:T(8,128)(2,1)} %param.13) | copy-start | bytes 393220
  131.3 18.8 %all-to-all-start.3 = ((f32[32,8,640]{2,1,0:T(8,128)}), f32[32,8,640]{2,1,0:T(8,128)S(1)}, u32[]{:S(2)}, u32[]{:S(2)}) async-start(f32[32,8,640]{2,1,0:T(8,128)} %broadcast_in_dim.44), calls=%async_computation.3 | async-start | bytes 1310720 | tf_op jit(solution)/shard_map/all_to_all | solution.py:36
